TPU v7x, 512 devices: a whole 4x8x8 slice. The times are simulated.
512 devices in a mesh: seq: 64 (over y, x, z_hi), head: 8 (over z_lo, core).
Axes of the slice: x: 4, y: 8, z: 8 (z_hi: 2, z_lo: 4; z = z_hi * 4 + z_lo), core: 2. Of those that a mesh axis runs over, the one named last changes fastest.
Arguments:
- queries: bfloat16 [32768, 16, 128], P('seq', 'head'), may hold values from -6 to 6
- keys: bfloat16 [32768, 16, 128], P('seq', 'head'), may hold values from -6 to 6
- values: bfloat16 [32768, 16, 128], P('seq', 'head'), may hold values from -6 to 6
- clusters: int32 [16, 32768, 1], P('head', 'seq'), may hold values from 0 to 255; in each aligned block of 512 rows (0 to 511, 512 to 1023, ..., all dimensions but the last counted through in order) at most 8 rows name the same one
- cent_keys: bfloat16 [16, 256, 128], P('head', 'seq'), may hold values from -6 to 6
- cent_values: bfloat16 [16, 256, 128], P('head', 'seq'), may hold values from -6 to 6
- out_weight: bfloat16 [2048, 4096], P('head'), may hold values from -0.1875 to 0.1875
Outputs:
- mixed: bfloat16 [4096, 32768], P('head', 'seq')
Inputs may be any that keep to these rules, and one draw needn't show every extreme that they name: `clusters`: among the 512 tokens of one device in one head (an aligned block of rows), no cluster is named more than 8 times; in some such block a cluster is named exactly 8 times.
All inputs are finite; a program needn't handle non-finite values.
Results may differ from a plain program's by a relative error of at most 0.017.
Values may be sent and summed in bfloat16 or wider, within the bound.
No kernel may reach another device: no remote copies, remote signals or barrier semaphores. Data moves between devices by JAX's collectives and lax.ppermute only.
A program may use at most 128 MiB of HBM per device.

v0:
```python
import jax
import jax.numpy as jnp
from jax import lax
from jax.sharding import PartitionSpec as P

CLUSTERS = 256
MOST = 8


def masked_scores(query_in, key_in, where_in, scale):
    sources, count, depth, width = query_in.shape
    nheads = where_in.shape[3]
    hsize = width // nheads
    query_five = query_in.reshape(sources, count, depth, nheads, hsize)
    key_five = key_in.reshape(sources, count, depth, nheads, hsize)
    raw = jnp.einsum(
        "aimhe,bikhe->ihambk", query_five, key_five, preferred_element_type=jnp.float32
    )
    scores = raw.reshape(count, nheads, sources * depth, sources * depth) * scale
    where_now = jnp.transpose(where_in, (1, 3, 0, 2)).reshape(count, nheads, sources * depth)
    allowed = (where_now[:, :, None, :] >= 0) & (
        where_now[:, :, None, :] <= where_now[:, :, :, None]
    )
    return (jnp.where(allowed, scores, -1e30), query_five)


def weigh_values(rounded, value_in):
    sources, count, depth, width = value_in.shape
    nheads = rounded.shape[1]
    value_five = value_in.reshape(sources, count, depth, nheads, width // nheads)
    shaped = rounded.reshape(count, nheads, sources * depth, sources, depth)
    return jnp.einsum("ihqbk,bikhe->ihqe", shaped, value_five, preferred_element_type=jnp.float32)


def to_slots(array_in, sources, depth):
    count, nheads = (array_in.shape[0], array_in.shape[1])
    tail = array_in.shape[3:]
    shaped = array_in.reshape((count, nheads, sources, depth) + tail)
    if len(tail) == 1:
        moved = jnp.transpose(shaped, (2, 0, 3, 1, 4))
        return moved.reshape(sources, count, depth, nheads * tail[0])
    return jnp.transpose(shaped, (2, 0, 3, 1))


def on_device(queries, keys, values, clusters, cent_keys, cent_values, out_weight):
    tok_dev, heads_dev, head_dim = queries.shape
    owners = lax.axis_size("seq")
    per_owner = CLUSTERS // owners
    slot_total = CLUSTERS * MOST
    scale = head_dim ** (-0.5)
    assign = clusters[:, :, 0]
    order = jnp.arange(tok_dev, dtype=jnp.int32)
    earlier = (assign[:, :, None] == assign[:, None, :]) & (
        order[None, None, :] < order[None, :, None]
    )
    rank = jnp.sum(earlier.astype(jnp.int32), axis=2)
    slot_of = (assign * MOST + rank).T
    head_cols = jnp.arange(heads_dev, dtype=jnp.int32)[None, :]
    position = lax.axis_index("seq") * tok_dev + order

    def place(rows_in):
        empty = jnp.zeros((slot_total, heads_dev, head_dim), rows_in.dtype)
        filled = empty.at[slot_of, head_cols].set(rows_in)
        return filled.reshape(owners, per_owner, MOST, heads_dev * head_dim)

    where_buf = jnp.full((slot_total, heads_dev), -1, jnp.int32)
    where_buf = where_buf.at[slot_of, head_cols].set(
        jnp.broadcast_to(position[:, None], (tok_dev, heads_dev))
    )
    where_buf = where_buf.reshape(owners, per_owner, MOST, heads_dev)
    cent_all_k, cent_all_v = (
        lax.all_gather(cent_keys, "seq", axis=1, tiled=True),
        lax.all_gather(cent_values, "seq", axis=1, tiled=True),
    )
    query_in = lax.all_to_all(place(queries), "seq", split_axis=0, concat_axis=0, tiled=True)
    key_in = lax.all_to_all(place(keys), "seq", split_axis=0, concat_axis=0, tiled=True)
    value_in = lax.all_to_all(place(values), "seq", split_axis=0, concat_axis=0, tiled=True)
    where_in = lax.all_to_all(where_buf, "seq", split_axis=0, concat_axis=0, tiled=True)
    sources, count, depth, width = query_in.shape
    local, query_five = masked_scores(query_in, key_in, where_in, scale)
    top = jnp.max(local, axis=-1, keepdims=True)
    w_local = jnp.exp(local - top)
    numer = weigh_values(w_local.astype(jnp.bfloat16), value_in)
    denom = jnp.sum(w_local, axis=-1)
    returned = (
        lax.all_to_all(
            to_slots(numer, sources, depth).astype(jnp.bfloat16),
            "seq",
            split_axis=0,
            concat_axis=0,
            tiled=True,
        ).astype(jnp.float32),
        lax.all_to_all(
            to_slots(top[..., 0], sources, depth).astype(jnp.bfloat16),
            "seq",
            split_axis=0,
            concat_axis=0,
            tiled=True,
        ).astype(jnp.float32),
        lax.all_to_all(
            to_slots(denom, sources, depth).astype(jnp.bfloat16),
            "seq",
            split_axis=0,
            concat_axis=0,
            tiled=True,
        ).astype(jnp.float32),
    )
    numer_s, top_s, denom_s = returned
    numer_t = numer_s.reshape(slot_total, heads_dev, head_dim)[slot_of, head_cols]
    top_t = top_s.reshape(slot_total, heads_dev)[slot_of, head_cols]
    denom_t = denom_s.reshape(slot_total, heads_dev)[slot_of, head_cols]
    memory = (
        jnp.einsum("the,hce->thc", queries, cent_all_k, preferred_element_type=jnp.float32) * scale
    )
    top = jnp.maximum(top_t, jnp.max(memory, axis=-1))
    w_memory = jnp.exp(memory - top[:, :, None])
    factor = jnp.exp(top_t - top)
    numer = numer_t * factor[:, :, None] + jnp.einsum(
        "thc,hce->the",
        w_memory.astype(jnp.bfloat16),
        cent_all_v,
        preferred_element_type=jnp.float32,
    )
    denom = denom_t * factor + jnp.sum(w_memory, axis=-1)
    attended = (numer / denom[:, :, None]).astype(jnp.bfloat16)
    flat_out = attended.reshape(tok_dev, heads_dev * head_dim)
    return lax.psum_scatter(
        jnp.einsum("kc,tk->ct", out_weight, flat_out, preferred_element_type=jnp.float32).astype(
            jnp.bfloat16
        ),
        "head",
        scatter_dimension=0,
        tiled=True,
    )


def solution(mesh):
    return jax.shard_map(
        on_device,
        mesh=mesh,
        in_specs=(
            P("seq", "head", None),
            P("seq", "head", None),
            P("seq", "head", None),
            P("head", "seq", None),
            P("head", "seq", None),
            P("head", "seq", None),
            P("head", None),
        ),
        out_specs=P("head", "seq"),
        check_vma=False,
    )
```

profile of v0, /device:TPU:6, one launch (start us, length us, event | category | flops | bytes accessed | tf_op | source)
XLA Modules:
  0.0 806.8 jit_solution(5865518857260931860)
XLA Ops:
  6.6 0.8 copy.192
  7.4 0.7 convert_reduce_fusion
  8.2 0.7 shift-left_or_fusion
  8.9 0.7 and_reduce_fusion
  9.6 0.8 multiply_reduce_fusion.1
  11.0 4.3 scatter_custom_fusion
  15.4 0.4 reshape.128
  15.7 0.7 copy.124
  16.5 19.0 %all-to-all-start = ((s32[64,4,8,2]{2,1,3,0:T(4,128)}), s32[64,4,8,2]{2,1,3,0:T(4,128)S(1)}, u32[]{:S(2)}, u32[]{:S(2)}) async-start(s32[64,4,8,2]{2,1,3,0:T(4,128)} %copy.124), calls=%async_computation | async-start | bytes 524288 | tf_op jit(solution)/shard_map/all_to_all | solution.py:78
  35.9 3.9 scatter_custom_fusion.1
  39.8 1.2 reshape.129
  41.0 9.9 %all-to-all-done = s32[64,4,8,2]{2,1,3,0:T(4,128)S(1)} async-done(((s32[64,4,8,2]{2,1,3,0:T(4,128)}), s32[64,4,8,2]{2,1,3,0:T(4,128)S(1)}, u32[]{:S(2)}, u32[]{:S(2)}) %all-to-all-start) | async-done | bytes 16416 | tf_op jit(solution)/shard_map/all_to_all | solution.py:78
  50.9 6.9 all-to-all-start.1
  57.9 3.9 scatter_custom_fusion.2
  61.8 1.2 reshape.131
  62.9 25.2 %all-to-all-done.1 = bf16[64,4,8,256]{3,2,1,0:T(8,128)(2,1)} async-done(((bf16[64,4,8,256]{3,2,1,0:T(8,128)(2,1)}), bf16[64,4,8,256]{3,2,1,0:T(8,128)(2,1)}, u32[]{:S(2)}, u32[]{:S(2)}) %all-to-all-start.1) | async-done | bytes 1048608 | tf_op jit(solution)/shard_map/all_to_all | solution.py:75
  88.2 7.7 all-to-all-start.2
  95.8 4.1 scatter_custom_fusion.3
  99.9 1.2 reshape.133
  101.5 24.3 %all-to-all-done.2 = bf16[64,4,8,256]{3,2,1,0:T(8,128)(2,1)} async-done(((bf16[64,4,8,256]{3,2,1,0:T(8,128)(2,1)}), bf16[64,4,8,256]{3,2,1,0:T(8,128)(2,1)}, u32[]{:S(2)}, u32[]{:S(2)}) %all-to-all-start.2) | async-done | bytes 1048608 | tf_op jit(solution)/shard_map/all_to_all | solution.py:76
  125.8 7.7 all-to-all-start.3
  133.5 6.9 fusion
  140.4 5.7 copy-done.1
  146.1 6.4 exponential_reduce_fusion
  152.7 9.4 %copy.130 = f32[4,2,64,8,64,8]{4,5,3,2,1,0:T(8,128)S(1)} copy(f32[4,2,64,8,64,8]{4,3,5,2,1,0:T(8,128)} %copy-done.1) | data formatting | bytes 16777216 | tf_op jit(solution)/shard_map/mul | solution.py:19
  162.1 0.8 copy.148
  162.9 12.5 %exponential_convert_fusion = bf16[4,2,512,64,8]{3,4,2,1,0:T(8,128)(2,1)} fusion(f32[4,2,512,64,8]{3,4,2,1,0:T(8,128)S(1)} %bitcast.84, f32[4,2,512]{2,1,0:T(2,128)S(1)} %sub.34, s32[4,2,512]{2,1,0:T(2,128)S(1)} %le.25, s32[4,2,64,8]{2,3,1,0:T(8,128)S(1)} %bitcast.91, pred[4,2,64,8]{2,3,1,0:T(8,128)(4,1)S(1)} %broadcast_compare_fusion), kind=kLoop, calls=%fused_computation.8 | loop fusion | flops 10485760 | bytes 12636160 | tf_op jit(solution)/shard_map/convert_element_type | solution.py:83
  175.4 15.1 %all-to-all-start.6 = ((bf16[64,4,8,2]{2,1,3,0:T(4,128)(2,1)}), bf16[64,4,8,2]{2,1,3,0:T(4,128)(2,1)S(1)}, u32[]{:S(2)}, u32[]{:S(2)}) async-start(bf16[64,4,8,2]{2,1,3,0:T(4,128)(2,1)} %copy.148), calls=%async_computation.6 | async-start | bytes 262144 | tf_op jit(solution)/shard_map/all_to_all | solution.py:100
  190.5 0.8 copy.136
  191.3 12.0 %copy.132 = bf16[4,2,512,64,8]{2,4,3,1,0:T(8,128)(2,1)} copy(bf16[4,2,512,64,8]{3,4,2,1,0:T(8,128)(2,1)} %exponential_convert_fusion) | data formatting | bytes 8388608 | tf_op jit(solution)/shard_map/convert_element_type | solution.py:83
  203.5 14.9 %all-to-all-start.5 = ((bf16[64,4,8,2]{2,1,3,0:T(4,128)(2,1)}), bf16[64,4,8,2]{2,1,3,0:T(4,128)(2,1)S(1)}, u32[]{:S(2)}, u32[]{:S(2)}) async-start(bf16[64,4,8,2]{2,1,3,0:T(4,128)(2,1)} %copy.136), calls=%async_computation.5 | async-start | bytes 262144 | tf_op jit(solution)/shard_map/all_to_all | solution.py:93
  218.5 4.0 fusion.2
  222.4 1.3 copy.190
  223.7 7.6 all-to-all-done.5
  231.3 7.7 all-to-all-start.4
  239.4 216.7 %all_gather.6 = bf16[2,256,128]{2,0,1:T(2,128)(2,1)S(1)} all-gather(bf16[2,4,128]{2,0,1:T(2,128)(2,1)S(1)} %copy.139), channel_id=1, replica_groups=mesh['seq'=64,'head'=8] {'seq'}, dimensions={1}, use_global_device_ids=true | all-gather | bytes 133120 | tf_op jit(solution)/shard_map/all_gather | solution.py:72
  456.2 227.6 %all_gather.7 = bf16[2,256,128]{2,0,1:T(2,128)(2,1)} all-gather(bf16[2,4,128]{2,0,1:T(2,128)(2,1)S(1)} %copy.145), channel_id=1, replica_groups=mesh['seq'=64,'head'=8] {'seq'}, dimensions={1}, use_global_device_ids=true | all-gather | bytes 133120 | tf_op jit(solution)/shard_map/all_gather | solution.py:73
  683.8 1.9 fusion.27
  686.0 0.3 reshape.166
  686.3 9.1 %gather_fusion.2 = f32[1024]{0:T(1024)S(1)} fusion(f32[2048,2]{0,1:T(2,128)S(1)} %reshape.166, s32[1024]{0:T(1024)S(1)} %reshape.167), kind=kCustom, calls=%fused_computation.2 | custom fusion | bytes 16384 | tf_op jit(solution)/shard_map/gather | solution.py:111
  696.2 9.1 %gather_fusion.1 = f32[1024]{0:T(1024)S(1)} fusion(f32[2048,2]{0,1:T(2,128)S(1)} %reshape.164, s32[1024]{0:T(1024)S(1)} %reshape.167), kind=kCustom, calls=%fused_computation.1 | custom fusion | bytes 16384 | tf_op jit(solution)/shard_map/gather | solution.py:110
  705.9 3.1 reshape.162
  709.0 16.2 %gather_fusion = f32[1024,128]{1,0:T(8,128)} fusion(f32[2048,2,128]{2,1,0:T(2,128)} %reshape.162, s32[1024]{0:T(1024)S(1)} %reshape.167), kind=kCustom, calls=%fused_computation | custom fusion | bytes 1056768 | tf_op jit(solution)/shard_map/gather | solution.py:109
  725.2 2.0 copy.144
  727.2 1.4 fusion.6
  728.6 3.2 fusion.1
  731.9 66.0 %reduce-scatter.2.cloned.1.call-done = bf16[512,512]{0,1:T(8,128)(2,1)} async-done(((bf16[4096,512]{0,1:T(8,128)(2,1)}), bf16[512,512]{0,1:T(8,128)(2,1)}) %reduce-scatter.2.cloned.1.call-update) | async-done | bytes 524304 | tf_op jit(solution)/shard_map/reduce_scatter | solution.py:127
  797.9 2.0 copy.152
  (51 shorter events, 3.8 us)
Async XLA Ops:
  6.5 722.1 %copy-start = (bf16[256,4096]{1,0:T(8,128)(2,1)S(1)}, bf16[256,4096]{1,0:T(8,128)(2,1)}, u32[]{:S(2)}) copy-start(bf16[256,4096]{1,0:T(8,128)(2,1)} %param.13) | copy-start | bytes 6291460
  16.5 34.4 %all-to-all-start = ((s32[64,4,8,2]{2,1,3,0:T(4,128)}), s32[64,4,8,2]{2,1,3,0:T(4,128)S(1)}, u32[]{:S(2)}, u32[]{:S(2)}) async-start(s32[64,4,8,2]{2,1,3,0:T(4,128)} %copy.124), calls=%async_computation | async-start | bytes 524288 | tf_op jit(solution)/shard_map/all_to_all | solution.py:78
  50.9 37.2 %all-to-all-start.1 = ((bf16[64,4,8,256]{3,2,1,0:T(8,128)(2,1)}), bf16[64,4,8,256]{3,2,1,0:T(8,128)(2,1)}, u32[]{:S(2)}, u32[]{:S(2)}) async-start(bf16[64,4,8,256]{3,2,1,0:T(8,128)(2,1)} %reshape.129), calls=%async_computation.1 | async-start | bytes 2097152 | tf_op jit(solution)/shard_map/all_to_all | solution.py:75
  88.2 37.6 %all-to-all-start.2 = ((bf16[64,4,8,256]{3,2,1,0:T(8,128)(2,1)}), bf16[64,4,8,256]{3,2,1,0:T(8,128)(2,1)}, u32[]{:S(2)}, u32[]{:S(2)}) async-start(bf16[64,4,8,256]{3,2,1,0:T(8,128)(2,1)} %reshape.131), calls=%async_computation.2 | async-start | bytes 2097152 | tf_op jit(solution)/shard_map/all_to_all | solution.py:76
  125.8 49.6 %all-to-all-start.3 = ((bf16[64,4,8,256]{3,2,1,0:T(8,128)(2,1)}), bf16[64,4,8,256]{3,2,1,0:T(8,128)(2,1)}, u32[]{:S(2)}, u32[]{:S(2)}) async-start(bf16[64,4,8,256]{3,2,1,0:T(8,128)(2,1)} %reshape.133), calls=%async_computation.3 | async-start | bytes 2097152 | tf_op jit(solution)/shard_map/all_to_all | solution.py:77
  140.4 5.7 copy-start.1
  175.4 28.2 %all-to-all-start.6 = ((bf16[64,4,8,2]{2,1,3,0:T(4,128)(2,1)}), bf16[64,4,8,2]{2,1,3,0:T(4,128)(2,1)S(1)}, u32[]{:S(2)}, u32[]{:S(2)}) async-start(bf16[64,4,8,2]{2,1,3,0:T(4,128)(2,1)} %copy.148), calls=%async_computation.6 | async-start | bytes 262144 | tf_op jit(solution)/shard_map/all_to_all | solution.py:100
  203.5 27.8 %all-to-all-start.5 = ((bf16[64,4,8,2]{2,1,3,0:T(4,128)(2,1)}), bf16[64,4,8,2]{2,1,3,0:T(4,128)(2,1)S(1)}, u32[]{:S(2)}, u32[]{:S(2)}) async-start(bf16[64,4,8,2]{2,1,3,0:T(4,128)(2,1)} %copy.136), calls=%async_computation.5 | async-start | bytes 262144 | tf_op jit(solution)/shard_map/all_to_all | solution.py:93
  218.4 21.0 %copy-start.5 = (bf16[2,4,128]{2,1,0:T(4,128)(2,1)S(1)}, bf16[2,4,128]{2,1,0:T(4,128)(2,1)}, u32[]{:S(2)}) copy-start(bf16[2,4,128]{2,1,0:T(4,128)(2,1)} %param.11) | copy-start | bytes 6148
  218.4 21.0 %copy-start.6 = (bf16[2,4,128]{2,1,0:T(4,128)(2,1)S(1)}, bf16[2,4,128]{2,1,0:T(4,128)(2,1)}, u32[]{:S(2)}) copy-start(bf16[2,4,128]{2,1,0:T(4,128)(2,1)} %param.12) | copy-start | bytes 6148
  218.4 465.4 %copy-start.3 = (bf16[512,2,128]{2,1,0:T(2,128)(2,1)S(1)}, bf16[512,2,128]{2,1,0:T(2,128)(2,1)}, u32[]{:S(2)}) copy-start(bf16[512,2,128]{2,1,0:T(2,128)(2,1)} %param.7) | copy-start | bytes 786436
  231.3 474.5 %all-to-all-start.4 = ((bf16[64,4,8,256]{3,2,1,0:T(8,128)(2,1)}), bf16[64,4,8,256]{3,2,1,0:T(8,128)(2,1)}, u32[]{:S(2)}, u32[]{:S(2)}) async-start(bf16[64,4,8,256]{3,2,1,0:T(8,128)(2,1)} %bitcast.81), calls=%async_computation.4 | async-start | bytes 2097152 | tf_op jit(solution)/shard_map/all_to_all | solution.py:86
  239.0 558.9 %reduce-scatter.2.cloned.1.call-start = ((), (), s32[]{:S(2)}) async-start(), calls=%async_computation.8 | async-start | bytes 4718592 | tf_op jit(solution)/shard_map/reduce_scatter | solution.py:127
  696.2 9.4 %copy-start.4 = (f32[512,2]{0,1:T(2,128)S(1)}, f32[512,2]{0,1:T(2,128)}, u32[]{:S(2)}) copy-start(f32[512,2]{0,1:T(2,128)} %get-tuple-element.15) | copy-start | bytes 12292
  696.2 9.4 %copy-start.2 = (f32[512,2,256]{0,2,1:T(8,128)S(1)}, f32[512,2,256]{0,2,1:T(8,128)}, u32[]{:S(2)}) copy-start(f32[512,2,256]{0,2,1:T(8,128)} %get-tuple-element.16) | copy-start | bytes 3145732
Sparse Core Ops, SparseCore 0:
  732.0 65.8 reduce-scatter.1
where the time goes:
time: 808 us; the launch traced here: 807 us
  blocking collectives  444 us (55%)
  waiting for transfers between devices  133 us (16%)
  local copies, waits for them, and re-layouts  96.6 us (12%)
  starting transfers between devices  79.1 us (10%)
  other arithmetic  22.2 us (3%)
  matrix products  17.4 us (2%)
  between operations  13.8 us (2%)
    all_gather x1, blocking collectives, on_device(): lax.all_gather(cent_values, 'seq', axis=1, tiled=True)  228 us
    all_gather x1, blocking collectives, on_device(): lax.all_gather(cent_keys, 'seq', axis=1, tiled=True)  217 us
    reduce_scatter x1, waiting for transfers between devices, on_device(): lax.psum_scatter(jnp.einsum('kc,tk->ct', out_weight, flat_out, preferred_...  66 us
    all_to_all x1, waiting for transfers between devices, on_device(): lax.all_to_all(place(queries), 'seq', split_axis=0, concat_axis=0, tiled=...  25.2 us
    all_to_all x1, waiting for transfers between devices, on_device(): lax.all_to_all(place(keys), 'seq', split_axis=0, concat_axis=0, tiled=True)  24.3 us
    unnamed x26, local copies, waits for them, and re-layouts  23.4 us
    all_to_all x1, starting transfers between devices, on_device(): lax.all_to_all(where_buf, 'seq', split_axis=0, concat_axis=0, tiled=True)  19 us
    gather x2, local copies, waits for them, and re-layouts, on_device(): numer_s.reshape(slot_total, heads_dev, head_dim)[slot_of, head_cols]  18.2 us
  transfers between devices with their start and end apart: 8, of which 6 were waited for; matrix products, arithmetic and copies ran while one was open for 11% of the time, Pallas kernels for 0%

commit v1 on v0

v1 whole, which is shorter than its diff:
```python
import jax
import jax.numpy as jnp
from jax import lax
from jax.sharding import PartitionSpec as P

CLUSTERS = 256
MOST = 8


def on_device(queries, keys, values, clusters, cent_keys, cent_values, out_weight):
    tok_dev, heads_dev, head_dim = queries.shape
    owners = lax.axis_size("seq")
    per_owner = CLUSTERS // owners
    group = per_owner * MOST
    width = heads_dev * head_dim
    cent_rows = 2 * per_owner
    count_rows = 8
    scale = head_dim ** (-0.5)
    dtype = queries.dtype

    assign = clusters[:, :, 0]
    order = jnp.arange(tok_dev, dtype=jnp.int32)
    earlier = (assign[:, :, None] == assign[:, None, :]) & (
        order[None, None, :] < order[None, :, None]
    )
    rank = jnp.sum(earlier.astype(jnp.int32), axis=2)
    slot_of = (assign * MOST + rank).T
    head_cols = jnp.arange(heads_dev, dtype=jnp.int32)[None, :]
    owner_of = slot_of // group
    within = slot_of % group

    counts = jnp.sum(
        (assign[:, :, None] == jnp.arange(CLUSTERS, dtype=jnp.int32)[None, None, :]).astype(jnp.int32),
        axis=1,
    )
    counts = jnp.transpose(counts.reshape(heads_dev, owners, per_owner), (1, 0, 2))
    counts = counts.reshape(owners, heads_dev * per_owner).astype(dtype)
    counts = jnp.pad(counts, ((0, 0), (0, count_rows * width - heads_dev * per_owner)))
    counts = counts.reshape(owners, count_rows, width)

    rows = jnp.stack([queries, keys, values], axis=2)
    body = jnp.zeros((owners, 3, group, heads_dev, head_dim), dtype)
    body = body.at[owner_of, :, within, head_cols].set(rows)
    body = body.reshape(owners, 3 * group, width)
    cent = jnp.stack([cent_keys, cent_values], axis=0).reshape(1, cent_rows, width)
    cent = jnp.broadcast_to(cent, (owners, cent_rows, width))
    send = jnp.concatenate([body, cent, counts], axis=1)
    recv = lax.all_to_all(send, "seq", split_axis=0, concat_axis=0, tiled=True)

    five = (owners, per_owner, MOST, heads_dev, head_dim)
    q_in = recv[:, 0:group].reshape(five)
    k_in = recv[:, group : 2 * group].reshape(five)
    v_in = recv[:, 2 * group : 3 * group].reshape(five)
    cent_in = recv[:, 3 * group : 3 * group + cent_rows].reshape(
        owners, 2, heads_dev, per_owner, head_dim
    )
    cent_in = jnp.transpose(cent_in, (1, 2, 0, 3, 4)).reshape(2, heads_dev, CLUSTERS, head_dim)
    cent_k_all, cent_v_all = cent_in[0], cent_in[1]
    cnt = recv[:, 3 * group + cent_rows, : heads_dev * per_owner].astype(jnp.int32)
    cnt = cnt.reshape(owners, heads_dev, per_owner)

    span = owners * MOST
    local = jnp.einsum("acrhe,bcshe->charbs", q_in, k_in, preferred_element_type=jnp.float32)
    local = local.reshape(per_owner, heads_dev, span, span) * scale
    depth = jnp.arange(MOST, dtype=jnp.int32)
    valid = depth[None, None, None, :] < jnp.transpose(cnt, (2, 1, 0))[..., None]
    valid = valid.reshape(per_owner, heads_dev, span)
    line = jnp.arange(span, dtype=jnp.int32)
    allowed = valid[:, :, None, :] & (line[None, :] <= line[:, None])[None, None]
    local = jnp.where(allowed, local, -1e30)
    memory = jnp.einsum("acrhe,hde->chard", q_in, cent_k_all, preferred_element_type=jnp.float32)
    memory = memory.reshape(per_owner, heads_dev, span, CLUSTERS) * scale
    top = jnp.maximum(jnp.max(local, axis=-1), jnp.max(memory, axis=-1))[..., None]
    w_local = jnp.exp(local - top)
    w_memory = jnp.exp(memory - top)
    denom = jnp.sum(w_local, axis=-1) + jnp.sum(w_memory, axis=-1)
    numer = jnp.einsum(
        "chrbs,bcshe->chre",
        w_local.astype(dtype).reshape(per_owner, heads_dev, span, owners, MOST),
        v_in,
        preferred_element_type=jnp.float32,
    )
    numer = numer + jnp.einsum(
        "chrd,hde->chre", w_memory.astype(dtype), cent_v_all, preferred_element_type=jnp.float32
    )
    result = (numer / denom[..., None]).astype(dtype)
    result = result.reshape(per_owner, heads_dev, owners, MOST, head_dim)
    back = jnp.transpose(result, (2, 0, 3, 1, 4)).reshape(owners, group, width)
    back = lax.all_to_all(back, "seq", split_axis=0, concat_axis=0, tiled=True)
    back = back.reshape(owners * group, heads_dev, head_dim)
    attended = back[slot_of, head_cols]

    flat_out = attended.reshape(tok_dev, heads_dev * head_dim)
    return lax.psum_scatter(
        jnp.einsum("kc,tk->ct", out_weight, flat_out, preferred_element_type=jnp.float32).astype(
            jnp.bfloat16
        ),
        "head",
        scatter_dimension=0,
        tiled=True,
    )


def solution(mesh):
    return jax.shard_map(
        on_device,
        mesh=mesh,
        in_specs=(
            P("seq", "head", None),
            P("seq", "head", None),
            P("seq", "head", None),
            P("head", "seq", None),
            P("head", "seq", None),
            P("head", "seq", None),
            P("head", None),
        ),
        out_specs=P("head", "seq"),
        check_vma=False,
    )
```

time: 808 us -> 431 us (0.53)
  blocking collectives: 444 us -> 0 us
  local copies, waits for them, and re-layouts: 96.6 us -> 154 us
  starting transfers between devices: 79.1 us -> 29.8 us
  waiting for transfers between devices: 133 us -> 170 us
  other arithmetic: 22.2 us -> 35.3 us
  matrix products: 17.4 us -> 26.3 us
    all_gather x2 -> x0, blocking collectives: 444 us -> none  [the longest x1 228 us: on_device(): lax.all_gather(cent_values, 'seq', axis=1, tiled=True)]
    unnamed x26 -> x35, local copies, waits for them, and re-layouts: 23.4 us -> 106 us
    all_to_all x7 -> x2, waiting for transfers between devices: 67.3 us -> 117 us  [the longest x1 86.3 us: on_device(): recv = lax.all_to_all(send, 'seq', split_axis=0, concat_axis=0, tiled=True)]
    all_to_all x7 -> x2, starting transfers between devices: 79 us -> 29.8 us  [the longest x1 19.2 us: on_device(): recv = lax.all_to_all(send, 'seq', split_axis=0, concat_axis=0, tiled=True)]
    gather x8 -> x1, local copies, waits for them, and re-layouts: 37 us -> 4.98 us  [on_device(): attended = back[slot_of, head_cols]]
    reduce_scatter x1, waiting for transfers between devices: 66 us -> 53.4 us  [on_device(): lax.psum_scatter(jnp.einsum('kc,tk->ct', out_weight, flat_out, preferred_...]
    dot_general x4, matrix products: 14.2 us -> 23.2 us  [the longest x1 12.9 us: on_device(): jnp.einsum('acrhe,bcshe->charbs', q_in, k_in, preferred_element_type=jnp....]
  transfers between devices with their start and end apart: 8 -> 3, of which waited for: 6 -> 3; matrix products, arithmetic and copies ran while one was open for 11% -> 0% of each run, Pallas kernels for 0% -> 0%
where the time goes in v1:
time: 431 us; the launch traced here: 429 us
  waiting for transfers between devices  170 us (39%)
  local copies, waits for them, and re-layouts  154 us (36%)
  other arithmetic  35.3 us (8%)
  starting transfers between devices  29.8 us (7%)
  matrix products  26.3 us (6%)
  between operations  13.8 us (3%)
    unnamed x35, local copies, waits for them, and re-layouts  106 us
    all_to_all x1, waiting for transfers between devices, on_device(): recv = lax.all_to_all(send, 'seq', split_axis=0, concat_axis=0, tiled=True)  86.3 us
    reduce_scatter x1, waiting for transfers between devices, on_device(): lax.psum_scatter(jnp.einsum('kc,tk->ct', out_weight, flat_out, preferred_...  53.4 us
    all_to_all x1, waiting for transfers between devices, on_device(): back = lax.all_to_all(back, 'seq', split_axis=0, concat_axis=0, tiled=True)  30.4 us
    all_to_all x1, starting transfers between devices, on_device(): recv = lax.all_to_all(send, 'seq', split_axis=0, concat_axis=0, tiled=True)  19.2 us
    dot_general x1, matrix products, on_device(): jnp.einsum('acrhe,bcshe->charbs', q_in, k_in, preferred_element_type=jnp....  12.9 us
    convert_element_type x1, other arithmetic, on_device(): w_local.astype(dtype).reshape(per_owner, heads_dev, span, owners, MOST)  12.8 us
    reduce_sum x2, other arithmetic, on_device(): denom = jnp.sum(w_local, axis=-1) + jnp.sum(w_memory, axis=-1)  12.8 us
  transfers between devices with their start and end apart: 3, of which 3 were waited for; matrix products, arithmetic and copies ran while one was open for 0% of the time, Pallas kernels for 0%

profile of v1, /device:TPU:6, one launch (start us, length us, event | category | flops | bytes accessed | tf_op | source)
XLA Modules:
  0.0 429.1 jit_solution(8648670177063734893)
XLA Ops:
  6.6 0.8 copy.215
  7.4 0.2 convert_reduce_fusion.1
  7.7 0.7 convert_reduce_fusion
  8.4 0.7 fusion.18
  9.1 0.7 multiply_reduce_fusion
  9.8 0.7 and_reduce_fusion
  10.6 0.1 copy.147
  10.8 0.2 reshape.165
  10.9 2.4 pad_maximum_fusion.1
  13.4 0.7 copy.148
  14.0 2.9 broadcast.82
  16.9 95.0 %scatter_fusion = bf16[4096,3,128]{2,1,0:T(4,128)(2,1)} fusion(bf16[4096,3,128]{2,1,0:T(4,128)(2,1)} %broadcast.82, s32[1024]{0:T(1024)S(1)} %reshape.165, bf16[1024,3,128]{2,1,0:T(4,128)(2,1)S(1)} %copy.148), kind=kCustom, calls=%fused_computation.1 | custom fusion | bytes 2363392
  111.9 7.3 %copy.213 = bf16[64,32,2,3,128]{4,2,1,3,0:T(2,128)(2,1)} copy(bf16[64,32,2,3,128]{4,3,2,1,0:T(4,128)(2,1)} %bitcast.125) | data formatting | bytes 6291456
  119.2 6.0 %reshape.144 = bf16[64,96,256]{2,1,0:T(8,128)(2,1)} reshape(bf16[64,3,32,2,128]{4,3,2,1,0:T(2,128)(2,1)} %bitcast.126) | data formatting | bytes 6291456 | tf_op jit(solution)/shard_map/reshape | solution.py:44
  125.6 0.3 copy.178
  125.9 3.4 pad_maximum_fusion
  129.3 19.2 %all-to-all-start = ((bf16[64,112,256]{2,1,0:T(8,128)(2,1)}), bf16[64,112,256]{2,1,0:T(8,128)(2,1)}, u32[]{:S(2)}, u32[]{:S(2)}) async-start(bf16[64,112,256]{2,1,0:T(8,128)(2,1)} %pad_maximum_fusion), calls=%async_computation | async-start | bytes 7340032 | tf_op jit(solution)/shard_map/all_to_all | solution.py:48
  148.6 0.3 iota_compare_fusion
  148.8 0.4 broadcast_compare_fusion
  149.2 86.3 %all-to-all-done = bf16[64,112,256]{2,1,0:T(8,128)(2,1)} async-done(((bf16[64,112,256]{2,1,0:T(8,128)(2,1)}), bf16[64,112,256]{2,1,0:T(8,128)(2,1)}, u32[]{:S(2)}, u32[]{:S(2)}) %all-to-all-start) | async-done | bytes 3670048 | tf_op jit(solution)/shard_map/all_to_all | solution.py:48
  235.5 0.9 slice.32
  236.6 1.7 slice.35
  238.2 1.0 reshape.148
  239.4 4.3 slice_bitcast_fusion
  243.7 3.0 fusion.21
  246.7 0.8 copy.160
  247.6 12.9 %fusion = (f32[4,2,64,8]{3,2,1,0:T(8,128)S(1)}, f32[4,2,64,8,64,8]{4,3,5,2,1,0:T(8,128)}) fusion(pred[64,8,64,8]{2,1,3,0:T(8,128)(4,1)S(1)} %broadcast_compare_fusion, pred[4,2,64,8]{2,3,1,0:T(8,128)(4,1)S(1)} %iota_compare_fusion.3, bf16[64,4,8,2,128,1]{4,2,3,1,0,5:T(8,128)(2,1)} %get-tuple-element.7, bf16[64,4,8,2,128,1]{4,2,3,1,0,5:T(8,128)(2,1)} %get-tuple-element.6), kind=kOutput, calls=%fused_computation.5 | convolution fusion | flops 545255424 | bytes 10768384 | tf_op jit(solution)/shard_map/acrhe,bcshe->charbs/dot_general | solution.py:63
  260.5 0.7 copy.167
  261.2 0.2 max.12
  261.3 11.2 %exponential_reduce_fusion = f32[4,2,64,8]{3,2,1,0:T(8,128)} fusion(f32[4,2,64,8,64,8]{4,3,5,2,1,0:T(8,128)} %get-tuple-element.14, f32[4,2,64,8]{3,2,1,0:T(8,128)S(1)} %max.11, pred[64,8,64,8]{2,1,3,0:T(8,128)(4,1)S(1)} %broadcast_compare_fusion, pred[4,2,64,8]{2,3,1,0:T(8,128)(4,1)} %copy-done.8), kind=kLoop, calls=%fused_computation.2 | loop fusion | flops 8384512 | bytes 8687616 | tf_op jit(solution)/shard_map/reduce_sum | solution.py:76
  272.6 7.8 %copy.156 = f32[4,2,64,8,64,8]{4,5,3,2,1,0:T(8,128)} copy(f32[4,2,64,8,64,8]{4,3,5,2,1,0:T(8,128)S(1)} %copy-done.1) | data formatting | bytes 16777216 | tf_op jit(solution)/shard_map/mul | solution.py:64
  280.4 1.5 exponential_reduce_fusion.1
  281.9 0.1 copy.168
  282.1 0.2 add.55
  282.3 12.8 %exponential_convert_fusion = bf16[4,2,512,64,8]{3,4,2,1,0:T(8,128)(2,1)} fusion(f32[4,2,512,64,8]{3,4,2,1,0:T(8,128)} %bitcast.124, f32[4,2,512]{2,1,0:T(2,128)S(1)} %max.12, pred[512,64,8]{1,2,0:T(8,128)(4,1)S(1)} %iota_compare_fusion, pred[4,2,64,8]{2,3,1,0:T(8,128)(4,1)} %copy-done.8), kind=kLoop, calls=%fused_computation.3 | loop fusion | flops 8388608 | bytes 12865536 | tf_op jit(solution)/shard_map/convert_element_type | solution.py:79
  295.1 12.0 %copy.161 = bf16[4,2,512,64,8]{2,4,3,1,0:T(8,128)(2,1)} copy(bf16[4,2,512,64,8]{3,4,2,1,0:T(8,128)(2,1)} %exponential_convert_fusion) | data formatting | bytes 8388608 | tf_op jit(solution)/shard_map/convert_element_type | solution.py:79
  307.1 5.3 %fusion.4 = f32[2,128,4,512]{1,3,0,2:T(8,128)S(1)} fusion(bf16[2,256,128,1]{2,1,0,3:T(8,128)(2,1)S(1)} %bitcast.130, f32[4,2,64,8,256]{4,2,3,0,1:T(8,128)} %get-tuple-element.16, f32[4,2,512]{2,1,0:T(2,128)S(1)} %max.12), kind=kOutput, calls=%fused_computation.16 | convolution fusion | flops 270532608 | bytes 6438912 | tf_op jit(solution)/shard_map/chrd,hde->chre/dot_general | solution.py:83
  312.4 2.0 fusion.9
  314.4 1.3 copy.214
  315.8 10.6 %all-to-all-start.1 = ((bf16[64,32,256]{2,1,0:T(8,128)(2,1)}), bf16[64,32,256]{2,1,0:T(8,128)(2,1)}, u32[]{:S(2)}, u32[]{:S(2)}) async-start(bf16[64,32,256]{2,1,0:T(8,128)(2,1)} %bitcast.122), calls=%async_computation.1 | async-start | bytes 2097152 | tf_op jit(solution)/shard_map/all_to_all | solution.py:89
  326.5 0.1 copy.170
  326.6 0.2 reshape.159
  326.8 30.4 %all-to-all-done.1 = bf16[64,32,256]{2,1,0:T(8,128)(2,1)} async-done(((bf16[64,32,256]{2,1,0:T(8,128)(2,1)}), bf16[64,32,256]{2,1,0:T(8,128)(2,1)}, u32[]{:S(2)}, u32[]{:S(2)}) %all-to-all-start.1) | async-done | bytes 1048608 | tf_op jit(solution)/shard_map/all_to_all | solution.py:89
  357.2 1.3 reshape.152
  358.5 5.0 %gather_fusion = bf16[1024,128]{1,0:T(8,128)(2,1)S(1)} fusion(bf16[2048,2,128]{2,1,0:T(2,128)(2,1)S(1)} %reshape.152, s32[1024]{0:T(1024)S(1)} %reshape.159), kind=kCustom, calls=%fused_computation | custom fusion | bytes 532480 | tf_op jit(solution)/shard_map/gather | solution.py:91
  363.6 3.2 fusion.1
  366.8 53.4 %reduce-scatter.2.cloned.1.call-done = bf16[512,512]{0,1:T(8,128)(2,1)} async-done(((bf16[4096,512]{0,1:T(8,128)(2,1)}), bf16[512,512]{0,1:T(8,128)(2,1)}) %reduce-scatter.2.cloned.1.call-update) | async-done | bytes 524304 | tf_op jit(solution)/shard_map/reduce_scatter | solution.py:94
  420.2 2.0 copy.171
  (53 shorter events, 1.1 us)
Async XLA Ops:
  6.5 357.1 %copy-start = (bf16[256,4096]{1,0:T(8,128)(2,1)S(1)}, bf16[256,4096]{1,0:T(8,128)(2,1)}, u32[]{:S(2)}) copy-start(bf16[256,4096]{1,0:T(8,128)(2,1)} %param.13) | copy-start | bytes 6291460
  8.4 2.2 copy-start.9
  119.2 6.6 %copy-start.12 = (bf16[2,4,128]{2,1,0:T(4,128)(2,1)S(1)}, bf16[2,4,128]{2,1,0:T(4,128)(2,1)}, u32[]{:S(2)}) copy-start(bf16[2,4,128]{2,1,0:T(4,128)(2,1)} %param.12) | copy-start | bytes 6148
  119.2 6.6 %copy-start.13 = (bf16[2,4,128]{2,1,0:T(4,128)(2,1)S(1)}, bf16[2,4,128]{2,1,0:T(4,128)(2,1)}, u32[]{:S(2)}) copy-start(bf16[2,4,128]{2,1,0:T(4,128)(2,1)} %param.11) | copy-start | bytes 6148
  129.3 106.2 %all-to-all-start = ((bf16[64,112,256]{2,1,0:T(8,128)(2,1)}), bf16[64,112,256]{2,1,0:T(8,128)(2,1)}, u32[]{:S(2)}, u32[]{:S(2)}) async-start(bf16[64,112,256]{2,1,0:T(8,128)(2,1)} %pad_maximum_fusion), calls=%async_computation | async-start | bytes 7340032 | tf_op jit(solution)/shard_map/all_to_all | solution.py:48
  236.6 11.0 %copy-start.8 = (pred[4,2,64,8]{2,3,1,0:T(8,128)(4,1)}, pred[4,2,64,8]{2,3,1,0:T(8,128)(4,1)S(1)}, u32[]{:S(2)}) copy-start(pred[4,2,64,8]{2,3,1,0:T(8,128)(4,1)S(1)} %iota_compare_fusion.3) | copy-start | bytes 12292
  247.6 12.9 %copy-start.6 = (f32[4,2,64,8]{3,2,1,0:T(8,128)S(1)}, f32[4,2,64,8]{3,2,1,0:T(8,128)}, u32[]{:S(2)}) copy-start(f32[4,2,64,8]{3,2,1,0:T(8,128)} %copy.160) | copy-start | bytes 49156
  261.3 11.3 %copy-start.1 = (f32[4,2,64,8,64,8]{4,3,5,2,1,0:T(8,128)S(1)}, f32[4,2,64,8,64,8]{4,3,5,2,1,0:T(8,128)}, u32[]{:S(2)}) copy-start(f32[4,2,64,8,64,8]{4,3,5,2,1,0:T(8,128)} %get-tuple-element.14) | copy-start | bytes 25165828
  272.6 7.8 %copy-start.2 = (f32[4,2,64,8,256]{4,2,3,0,1:T(8,128)S(1)}, f32[4,2,64,8,256]{4,2,3,0,1:T(8,128)}, u32[]{:S(2)}) copy-start(f32[4,2,64,8,256]{4,2,3,0,1:T(8,128)} %get-tuple-element.16) | copy-start | bytes 12582916
  272.6 7.8 %copy-start.7 = (f32[4,2,64,8]{2,3,0,1:T(8,128)S(1)}, f32[4,2,64,8]{2,3,0,1:T(8,128)}, u32[]{:S(2)}) copy-start(f32[4,2,64,8]{2,3,0,1:T(8,128)} %copy.167) | copy-start | bytes 49156
  280.4 1.7 copy-start.4
  307.1 5.4 %copy-start.3 = (bf16[4,2,512,64,8]{2,4,3,1,0:T(8,128)(2,1)S(1)}, bf16[4,2,512,64,8]{2,4,3,1,0:T(8,128)(2,1)}, u32[]{:S(2)}) copy-start(bf16[4,2,512,64,8]{2,4,3,1,0:T(8,128)(2,1)} %copy.161) | copy-start | bytes 12582916
  307.1 5.4 %copy-start.5 = (bf16[64,4,8,2,128]{4,2,3,1,0:T(8,128)(2,1)S(1)}, bf16[64,4,8,2,128]{4,2,3,1,0:T(8,128)(2,1)}, u32[]{:S(2)}) copy-start(bf16[64,4,8,2,128]{4,2,3,1,0:T(8,128)(2,1)} %get-tuple-element.5) | copy-start | bytes 3145732
  314.4 12.0 %copy-start.10 = (s32[2,512]{1,0:T(2,128)S(1)}, s32[2,512]{1,0:T(2,128)}, u32[]{:S(2)}) copy-start(s32[2,512]{1,0:T(2,128)} %copy-done.9) | copy-start | bytes 12292
  314.4 12.0 %copy-start.11 = (s32[2,512,1]{1,2,0:T(1,128)S(1)}, s32[2,512,1]{1,2,0:T(1,128)}, u32[]{:S(2)}) copy-start(s32[2,512,1]{1,2,0:T(1,128)} %param.10) | copy-start | bytes 12292
  315.8 41.4 %all-to-all-start.1 = ((bf16[64,32,256]{2,1,0:T(8,128)(2,1)}), bf16[64,32,256]{2,1,0:T(8,128)(2,1)}, u32[]{:S(2)}, u32[]{:S(2)}) async-start(bf16[64,32,256]{2,1,0:T(8,128)(2,1)} %bitcast.122), calls=%async_computation.1 | async-start | bytes 2097152 | tf_op jit(solution)/shard_map/all_to_all | solution.py:89
  326.4 93.8 %reduce-scatter.2.cloned.1.call-start = ((), (), s32[]{:S(2)}) async-start(), calls=%async_computation.3 | async-start | bytes 4718592 | tf_op jit(solution)/shard_map/reduce_scatter | solution.py:94
Sparse Core Ops, SparseCore 0:
  366.9 53.1 reduce-scatter.1

commit v2 on v1

--- a/solution.py
+++ b/solution.py
@@ -26,8 +26,6 @@
     rank = jnp.sum(earlier.astype(jnp.int32), axis=2)
     slot_of = (assign * MOST + rank).T
     head_cols = jnp.arange(heads_dev, dtype=jnp.int32)[None, :]
-    owner_of = slot_of // group
-    within = slot_of % group
 
     counts = jnp.sum(
         (assign[:, :, None] == jnp.arange(CLUSTERS, dtype=jnp.int32)[None, None, :]).astype(jnp.int32),
@@ -38,10 +36,12 @@
     counts = jnp.pad(counts, ((0, 0), (0, count_rows * width - heads_dev * per_owner)))
     counts = counts.reshape(owners, count_rows, width)
 
-    rows = jnp.stack([queries, keys, values], axis=2)
-    body = jnp.zeros((owners, 3, group, heads_dev, head_dim), dtype)
-    body = body.at[owner_of, :, within, head_cols].set(rows)
-    body = body.reshape(owners, 3 * group, width)
+    slot_ids = jnp.arange(owners * group, dtype=jnp.int32)
+    onehot = (slot_of.T[:, None, :] == slot_ids[None, :, None]).astype(dtype)
+    onehot = onehot.reshape(heads_dev, owners, group, tok_dev)
+    rows = jnp.stack([queries, keys, values], axis=1)
+    body = jnp.einsum("hogt,tkhe->okghe", onehot, rows, preferred_element_type=jnp.float32)
+    body = body.astype(dtype).reshape(owners, 3 * group, width)
     cent = jnp.stack([cent_keys, cent_values], axis=0).reshape(1, cent_rows, width)
     cent = jnp.broadcast_to(cent, (owners, cent_rows, width))
     send = jnp.concatenate([body, cent, counts], axis=1)

time: 431 us -> 331 us (0.77)
  local copies, waits for them, and re-layouts: 154 us -> 54.5 us
    unnamed x35 -> x27, local copies, waits for them, and re-layouts: 106 us -> 1.93 us
    convert_element_type x0 -> x1, local copies, waits for them, and re-layouts: none -> 4.91 us  [on_device(): body = body.astype(dtype).reshape(owners, 3 * group, width)]
where the time goes in v2:
time: 331 us; the launch traced here: 330 us
  waiting for transfers between devices  170 us (51%)
  local copies, waits for them, and re-layouts  54.5 us (16%)
  other arithmetic  32 us (10%)
  starting transfers between devices  30 us (9%)
  matrix products  29 us (9%)
  between operations  13.7 us (4%)
    all_to_all x1, waiting for transfers between devices, on_device(): recv = lax.all_to_all(send, 'seq', split_axis=0, concat_axis=0, tiled=True)  86.2 us
    reduce_scatter x1, waiting for transfers between devices, on_device(): lax.psum_scatter(jnp.einsum('kc,tk->ct', out_weight, flat_out, preferred_...  53.6 us
    all_to_all x1, waiting for transfers between devices, on_device(): back = lax.all_to_all(back, 'seq', split_axis=0, concat_axis=0, tiled=True)  30.5 us
    all_to_all x1, starting transfers between devices, on_device(): recv = lax.all_to_all(send, 'seq', split_axis=0, concat_axis=0, tiled=True)  19.2 us
    dot_general x1, matrix products, on_device(): jnp.einsum('acrhe,bcshe->charbs', q_in, k_in, preferred_element_type=jnp....  12.9 us
    convert_element_type x1, other arithmetic, on_device(): w_local.astype(dtype).reshape(per_owner, heads_dev, span, owners, MOST)  12.8 us
    reduce_sum x2, other arithmetic, on_device(): denom = jnp.sum(w_local, axis=-1) + jnp.sum(w_memory, axis=-1)  12.8 us
    convert_element_type x1, local copies, waits for them, and re-layouts, on_device(): w_local.astype(dtype).reshape(per_owner, heads_dev, span, owners, MOST)  12 us
  transfers between devices with their start and end apart: 3, of which 3 were waited for; matrix products, arithmetic and copies ran while one was open for 0% of the time, Pallas kernels for 0%

profile of v2, /device:TPU:6, one launch (start us, length us, event | category | flops | bytes accessed | tf_op | source)
XLA Modules:
  0.0 329.5 jit_solution(18201905263913397259)
XLA Ops:
  6.6 0.8 copy.223
  7.5 0.2 convert_reduce_fusion.1
  7.7 0.7 convert_reduce_fusion
  8.4 1.3 fusion.28
  9.7 1.0 copy.222
  10.7 1.1 copy_bitcast_fusion.1
  11.8 2.7 convert_bitcast_fusion
  14.5 4.9 %copy.158 = bf16[64,3,32,2,128]{4,3,2,1,0:T(2,128)(2,1)} copy(bf16[64,3,32,2,128]{4,0,2,1,3:T(8,128)(2,1)S(1)} %convert_bitcast_fusion) | data formatting | bytes 6291456 | tf_op jit(solution)/shard_map/convert_element_type | solution.py:44
  19.4 6.0 %reshape.154 = bf16[64,96,256]{2,1,0:T(8,128)(2,1)} reshape(bf16[64,3,32,2,128]{4,3,2,1,0:T(2,128)(2,1)} %copy.158) | data formatting | bytes 6291456 | tf_op jit(solution)/shard_map/reshape | solution.py:44
  25.4 0.1 convert_element_type.53
  25.5 0.1 copy.159
  25.7 0.3 copy.189
  26.1 3.4 %pad_maximum_fusion = bf16[64,112,256]{2,1,0:T(8,128)(2,1)} fusion(bf16[64,8,256]{2,1,0:T(8,128)(2,1)S(1)} %copy.189, bf16[64,8,256]{2,1,0:T(8,128)(2,1)S(1)} %broadcast_in_dim.14, bf16[64,96,256]{2,1,0:T(8,128)(2,1)} %reshape.154), kind=kLoop, calls=%fused_computation.18 | loop fusion | flops 11010048 | bytes 7340032 | tf_op jit(solution)/shard_map/concatenate | solution.py:47
  29.5 19.2 %all-to-all-start = ((bf16[64,112,256]{2,1,0:T(8,128)(2,1)}), bf16[64,112,256]{2,1,0:T(8,128)(2,1)}, u32[]{:S(2)}, u32[]{:S(2)}) async-start(bf16[64,112,256]{2,1,0:T(8,128)(2,1)} %pad_maximum_fusion), calls=%async_computation | async-start | bytes 7340032 | tf_op jit(solution)/shard_map/all_to_all | solution.py:48
  48.7 0.1 copy.166
  48.8 0.3 iota_compare_fusion
  49.1 0.4 broadcast_compare_fusion
  49.4 86.2 %all-to-all-done = bf16[64,112,256]{2,1,0:T(8,128)(2,1)} async-done(((bf16[64,112,256]{2,1,0:T(8,128)(2,1)}), bf16[64,112,256]{2,1,0:T(8,128)(2,1)}, u32[]{:S(2)}, u32[]{:S(2)}) %all-to-all-start) | async-done | bytes 3670048 | tf_op jit(solution)/shard_map/all_to_all | solution.py:48
  135.6 0.9 slice.32
  136.7 1.7 slice.35
  138.4 1.0 reshape.158
  139.4 0.1 fusion.30
  139.5 4.2 %slice_bitcast_fusion = (bf16[64,4,8,2,128]{4,2,3,1,0:T(8,128)(2,1)}, bf16[64,4,8,2,128,1]{4,2,3,1,0,5:T(8,128)(2,1)}, bf16[64,4,8,2,128,1]{4,2,3,1,0,5:T(8,128)(2,1)}, bf16[64,4,8,2,128]{4,2,3,1,0:T(8,128)(2,1)S(1)}) fusion(bf16[64,112,256]{2,1,0:T(8,128)(2,1)} %all-to-all-done), kind=kLoop, calls=%fused_computation.28 | loop fusion | bytes 7340032 | tf_op jit(solution)/shard_map/reshape | solution.py:53
  143.8 3.0 fusion.31
  146.8 0.8 copy.169
  147.6 12.9 %fusion = (f32[4,2,64,8]{3,2,1,0:T(8,128)S(1)}, f32[4,2,64,8,64,8]{4,3,5,2,1,0:T(8,128)}) fusion(pred[64,8,64,8]{2,1,3,0:T(8,128)(4,1)S(1)} %broadcast_compare_fusion, pred[4,2,64,8]{2,3,1,0:T(8,128)(4,1)S(1)} %iota_compare_fusion.3, bf16[64,4,8,2,128,1]{4,2,3,1,0,5:T(8,128)(2,1)} %get-tuple-element.9, bf16[64,4,8,2,128,1]{4,2,3,1,0,5:T(8,128)(2,1)} %get-tuple-element.8), kind=kOutput, calls=%fused_computation.4 | convolution fusion | flops 545255424 | bytes 10768384 | tf_op jit(solution)/shard_map/acrhe,bcshe->charbs/dot_general | solution.py:63
  160.5 0.7 copy.176
  161.3 0.2 max.12
  161.4 11.2 %exponential_reduce_fusion = f32[4,2,64,8]{3,2,1,0:T(8,128)} fusion(f32[4,2,64,8,64,8]{4,3,5,2,1,0:T(8,128)} %get-tuple-element.14, f32[4,2,64,8]{3,2,1,0:T(8,128)S(1)} %max.11, pred[64,8,64,8]{2,1,3,0:T(8,128)(4,1)S(1)} %broadcast_compare_fusion, pred[4,2,64,8]{2,3,1,0:T(8,128)(4,1)} %copy-done.8), kind=kLoop, calls=%fused_computation.1 | loop fusion | flops 8384512 | bytes 8687616 | tf_op jit(solution)/shard_map/reduce_sum | solution.py:76
  172.7 7.8 %copy.165 = f32[4,2,64,8,64,8]{4,5,3,2,1,0:T(8,128)} copy(f32[4,2,64,8,64,8]{4,3,5,2,1,0:T(8,128)S(1)} %copy-done.1) | data formatting | bytes 16777216 | tf_op jit(solution)/shard_map/mul | solution.py:64
  180.5 1.5 exponential_reduce_fusion.1
  182.0 0.1 copy.177
  182.2 0.2 add.38
  182.3 12.8 %exponential_convert_fusion = bf16[4,2,512,64,8]{3,4,2,1,0:T(8,128)(2,1)} fusion(f32[4,2,512,64,8]{3,4,2,1,0:T(8,128)} %bitcast.105, f32[4,2,512]{2,1,0:T(2,128)S(1)} %max.12, pred[512,64,8]{1,2,0:T(8,128)(4,1)S(1)} %iota_compare_fusion, pred[4,2,64,8]{2,3,1,0:T(8,128)(4,1)} %copy-done.8), kind=kLoop, calls=%fused_computation.2 | loop fusion | flops 8388608 | bytes 12865536 | tf_op jit(solution)/shard_map/convert_element_type | solution.py:79
  195.2 12.0 %copy.170 = bf16[4,2,512,64,8]{2,4,3,1,0:T(8,128)(2,1)} copy(bf16[4,2,512,64,8]{3,4,2,1,0:T(8,128)(2,1)} %exponential_convert_fusion) | data formatting | bytes 8388608 | tf_op jit(solution)/shard_map/convert_element_type | solution.py:79
  207.2 5.3 %fusion.11 = f32[2,128,4,512]{1,3,0,2:T(8,128)S(1)} fusion(bf16[2,256,128,1]{2,1,0,3:T(8,128)(2,1)S(1)} %bitcast.108, f32[4,2,64,8,256]{4,2,3,0,1:T(8,128)} %get-tuple-element.16, f32[4,2,512]{2,1,0:T(2,128)S(1)} %max.12), kind=kOutput, calls=%fused_computation.20 | convolution fusion | flops 270532608 | bytes 6438912 | tf_op jit(solution)/shard_map/chrd,hde->chre/dot_general | solution.py:83
  212.5 2.0 fusion.16
  214.5 1.3 copy.221
  215.8 10.7 %all-to-all-start.1 = ((bf16[64,32,256]{2,1,0:T(8,128)(2,1)}), bf16[64,32,256]{2,1,0:T(8,128)(2,1)}, u32[]{:S(2)}, u32[]{:S(2)}) async-start(bf16[64,32,256]{2,1,0:T(8,128)(2,1)} %bitcast.102), calls=%async_computation.1 | async-start | bytes 2097152 | tf_op jit(solution)/shard_map/all_to_all | solution.py:89
  226.6 0.1 copy.179
  226.7 0.2 reshape.165
  226.9 30.5 %all-to-all-done.1 = bf16[64,32,256]{2,1,0:T(8,128)(2,1)} async-done(((bf16[64,32,256]{2,1,0:T(8,128)(2,1)}), bf16[64,32,256]{2,1,0:T(8,128)(2,1)}, u32[]{:S(2)}, u32[]{:S(2)}) %all-to-all-start.1) | async-done | bytes 1048608 | tf_op jit(solution)/shard_map/all_to_all | solution.py:89
  257.4 1.3 reshape.162
  258.7 5.0 %gather_fusion = bf16[1024,128]{1,0:T(8,128)(2,1)S(1)} fusion(bf16[2048,2,128]{2,1,0:T(2,128)(2,1)S(1)} %reshape.162, s32[1024]{0:T(1024)S(1)} %reshape.165), kind=kCustom, calls=%fused_computation | custom fusion | bytes 532480 | tf_op jit(solution)/shard_map/gather | solution.py:91
  263.7 0.1 reshape.163
  263.8 3.2 fusion.4
  267.1 53.6 %reduce-scatter.2.cloned.1.call-done = bf16[512,512]{0,1:T(8,128)(2,1)} async-done(((bf16[4096,512]{0,1:T(8,128)(2,1)}), bf16[512,512]{0,1:T(8,128)(2,1)}) %reduce-scatter.2.cloned.1.call-update) | async-done | bytes 524304 | tf_op jit(solution)/shard_map/reduce_scatter | solution.py:94
  320.6 2.0 copy.180
  (42 shorter events, 0.6 us)
Async XLA Ops:
  6.5 257.3 %copy-start = (bf16[256,4096]{1,0:T(8,128)(2,1)S(1)}, bf16[256,4096]{1,0:T(8,128)(2,1)}, u32[]{:S(2)}) copy-start(bf16[256,4096]{1,0:T(8,128)(2,1)} %param.13) | copy-start | bytes 6291460
  19.4 6.6 %copy-start.10 = (bf16[2,4,128]{2,1,0:T(4,128)(2,1)S(1)}, bf16[2,4,128]{2,1,0:T(4,128)(2,1)}, u32[]{:S(2)}) copy-start(bf16[2,4,128]{2,1,0:T(4,128)(2,1)} %param.12) | copy-start | bytes 6148
  19.4 6.6 %copy-start.11 = (bf16[2,4,128]{2,1,0:T(4,128)(2,1)S(1)}, bf16[2,4,128]{2,1,0:T(4,128)(2,1)}, u32[]{:S(2)}) copy-start(bf16[2,4,128]{2,1,0:T(4,128)(2,1)} %param.11) | copy-start | bytes 6148
  29.5 106.2 %all-to-all-start = ((bf16[64,112,256]{2,1,0:T(8,128)(2,1)}), bf16[64,112,256]{2,1,0:T(8,128)(2,1)}, u32[]{:S(2)}, u32[]{:S(2)}) async-start(bf16[64,112,256]{2,1,0:T(8,128)(2,1)} %pad_maximum_fusion), calls=%async_computation | async-start | bytes 7340032 | tf_op jit(solution)/shard_map/all_to_all | solution.py:48
  136.7 11.0 %copy-start.8 = (pred[4,2,64,8]{2,3,1,0:T(8,128)(4,1)}, pred[4,2,64,8]{2,3,1,0:T(8,128)(4,1)S(1)}, u32[]{:S(2)}) copy-start(pred[4,2,64,8]{2,3,1,0:T(8,128)(4,1)S(1)} %iota_compare_fusion.3) | copy-start | bytes 12292
  147.6 12.9 %copy-start.6 = (f32[4,2,64,8]{3,2,1,0:T(8,128)S(1)}, f32[4,2,64,8]{3,2,1,0:T(8,128)}, u32[]{:S(2)}) copy-start(f32[4,2,64,8]{3,2,1,0:T(8,128)} %copy.169) | copy-start | bytes 49156
  161.4 11.3 %copy-start.1 = (f32[4,2,64,8,64,8]{4,3,5,2,1,0:T(8,128)S(1)}, f32[4,2,64,8,64,8]{4,3,5,2,1,0:T(8,128)}, u32[]{:S(2)}) copy-start(f32[4,2,64,8,64,8]{4,3,5,2,1,0:T(8,128)} %get-tuple-element.14) | copy-start | bytes 25165828
  172.7 7.8 %copy-start.2 = (f32[4,2,64,8,256]{4,2,3,0,1:T(8,128)S(1)}, f32[4,2,64,8,256]{4,2,3,0,1:T(8,128)}, u32[]{:S(2)}) copy-start(f32[4,2,64,8,256]{4,2,3,0,1:T(8,128)} %get-tuple-element.16) | copy-start | bytes 12582916
  172.7 7.8 %copy-start.7 = (f32[4,2,64,8]{2,3,0,1:T(8,128)S(1)}, f32[4,2,64,8]{2,3,0,1:T(8,128)}, u32[]{:S(2)}) copy-start(f32[4,2,64,8]{2,3,0,1:T(8,128)} %copy.176) | copy-start | bytes 49156
  180.5 1.7 copy-start.4
  207.2 5.4 %copy-start.3 = (bf16[4,2,512,64,8]{2,4,3,1,0:T(8,128)(2,1)S(1)}, bf16[4,2,512,64,8]{2,4,3,1,0:T(8,128)(2,1)}, u32[]{:S(2)}) copy-start(bf16[4,2,512,64,8]{2,4,3,1,0:T(8,128)(2,1)} %copy.170) | copy-start | bytes 12582916
  207.2 5.4 %copy-start.5 = (bf16[64,4,8,2,128]{4,2,3,1,0:T(8,128)(2,1)S(1)}, bf16[64,4,8,2,128]{4,2,3,1,0:T(8,128)(2,1)}, u32[]{:S(2)}) copy-start(bf16[64,4,8,2,128]{4,2,3,1,0:T(8,128)(2,1)} %get-tuple-element.7) | copy-start | bytes 3145732
  214.5 12.1 %copy-start.9 = (s32[512,2,1]{0,1,2:T(2,128)S(1)}, s32[512,2,1]{0,1,2:T(2,128)}, u32[]{:S(2)}) copy-start(s32[512,2,1]{0,1,2:T(2,128)} %get-tuple-element.5) | copy-start | bytes 12292
  215.8 41.6 %all-to-all-start.1 = ((bf16[64,32,256]{2,1,0:T(8,128)(2,1)}), bf16[64,32,256]{2,1,0:T(8,128)(2,1)}, u32[]{:S(2)}, u32[]{:S(2)}) async-start(bf16[64,32,256]{2,1,0:T(8,128)(2,1)} %bitcast.102), calls=%async_computation.1 | async-start | bytes 2097152 | tf_op jit(solution)/shard_map/all_to_all | solution.py:89
  226.5 94.1 %reduce-scatter.2.cloned.1.call-start = ((), (), s32[]{:S(2)}) async-start(), calls=%async_computation.3 | async-start | bytes 4718592 | tf_op jit(solution)/shard_map/reduce_scatter | solution.py:94
Sparse Core Ops, SparseCore 0:
  267.2 53.4 reduce-scatter.1

commit v3 on v2

--- a/solution.py
+++ b/solution.py
@@ -1,10 +1,64 @@
+import functools
+
 import jax
 import jax.numpy as jnp
 from jax import lax
+from jax.experimental import pallas as pl
 from jax.sharding import PartitionSpec as P
 
 CLUSTERS = 256
 MOST = 8
+
+
+def attention_kernel(q_ref, k_ref, v_ref, ck_ref, cv_ref, valid_ref, out_ref, *, scale):
+    q = q_ref[0, 0, 0]
+    k = k_ref[0, 0, 0]
+    v = v_ref[0, 0, 0]
+    ck = ck_ref[0, 0]
+    cv = cv_ref[0, 0]
+    span = q.shape[0]
+    contract = (((1,), (1,)), ((), ()))
+    local = lax.dot_general(q, k, contract, preferred_element_type=jnp.float32) * scale
+    row = lax.broadcasted_iota(jnp.int32, (span, span), 0)
+    col = lax.broadcasted_iota(jnp.int32, (span, span), 1)
+    allowed = (col <= row) & (valid_ref[0, 0] > 0.5)
+    local = jnp.where(allowed, local, -1e30)
+    memory = lax.dot_general(q, ck, contract, preferred_element_type=jnp.float32) * scale
+    top = jnp.maximum(
+        jnp.max(local, axis=1, keepdims=True), jnp.max(memory, axis=1, keepdims=True)
+    )
+    w_local = jnp.exp(local - top)
+    w_memory = jnp.exp(memory - top)
+    denom = jnp.sum(w_local, axis=1, keepdims=True) + jnp.sum(w_memory, axis=1, keepdims=True)
+    numer = jnp.dot(w_local.astype(v.dtype), v, preferred_element_type=jnp.float32)
+    numer = numer + jnp.dot(w_memory.astype(cv.dtype), cv, preferred_element_type=jnp.float32)
+    out_ref[0, 0] = (numer / denom).astype(out_ref.dtype)
+
+
+def cluster_attention(qkv, cent, valid, scale):
+    _, per_owner, heads_dev, span, head_dim = qkv.shape
+    clusters = cent.shape[2]
+
+    def pick(kind):
+        return pl.BlockSpec((1, 1, 1, span, head_dim), lambda c, h: (kind, c, h, 0, 0))
+
+    def centroid(kind):
+        return pl.BlockSpec((1, 1, clusters, head_dim), lambda c, h: (kind, h, 0, 0))
+
+    return pl.pallas_call(
+        functools.partial(attention_kernel, scale=scale),
+        grid=(per_owner, heads_dev),
+        in_specs=[
+            pick(0),
+            pick(1),
+            pick(2),
+            centroid(0),
+            centroid(1),
+            pl.BlockSpec((1, 1, 1, span), lambda c, h: (c, h, 0, 0)),
+        ],
+        out_specs=pl.BlockSpec((1, 1, span, head_dim), lambda c, h: (c, h, 0, 0)),
+        out_shape=jax.ShapeDtypeStruct((per_owner, heads_dev, span, head_dim), qkv.dtype),
+    )(qkv, qkv, qkv, cent, cent, valid)
 
 
 def on_device(queries, keys, values, clusters, cent_keys, cent_values, out_weight):
@@ -47,43 +101,20 @@
     send = jnp.concatenate([body, cent, counts], axis=1)
     recv = lax.all_to_all(send, "seq", split_axis=0, concat_axis=0, tiled=True)
 
-    five = (owners, per_owner, MOST, heads_dev, head_dim)
-    q_in = recv[:, 0:group].reshape(five)
-    k_in = recv[:, group : 2 * group].reshape(five)
-    v_in = recv[:, 2 * group : 3 * group].reshape(five)
+    span = owners * MOST
+    qkv = recv[:, 0 : 3 * group].reshape(owners, 3, per_owner, MOST, heads_dev, head_dim)
+    qkv = jnp.transpose(qkv, (1, 2, 4, 0, 3, 5)).reshape(3, per_owner, heads_dev, span, head_dim)
     cent_in = recv[:, 3 * group : 3 * group + cent_rows].reshape(
         owners, 2, heads_dev, per_owner, head_dim
     )
     cent_in = jnp.transpose(cent_in, (1, 2, 0, 3, 4)).reshape(2, heads_dev, CLUSTERS, head_dim)
-    cent_k_all, cent_v_all = cent_in[0], cent_in[1]
     cnt = recv[:, 3 * group + cent_rows, : heads_dev * per_owner].astype(jnp.int32)
     cnt = cnt.reshape(owners, heads_dev, per_owner)
-
-    span = owners * MOST
-    local = jnp.einsum("acrhe,bcshe->charbs", q_in, k_in, preferred_element_type=jnp.float32)
-    local = local.reshape(per_owner, heads_dev, span, span) * scale
     depth = jnp.arange(MOST, dtype=jnp.int32)
     valid = depth[None, None, None, :] < jnp.transpose(cnt, (2, 1, 0))[..., None]
-    valid = valid.reshape(per_owner, heads_dev, span)
-    line = jnp.arange(span, dtype=jnp.int32)
-    allowed = valid[:, :, None, :] & (line[None, :] <= line[:, None])[None, None]
-    local = jnp.where(allowed, local, -1e30)
-    memory = jnp.einsum("acrhe,hde->chard", q_in, cent_k_all, preferred_element_type=jnp.float32)
-    memory = memory.reshape(per_owner, heads_dev, span, CLUSTERS) * scale
-    top = jnp.maximum(jnp.max(local, axis=-1), jnp.max(memory, axis=-1))[..., None]
-    w_local = jnp.exp(local - top)
-    w_memory = jnp.exp(memory - top)
-    denom = jnp.sum(w_local, axis=-1) + jnp.sum(w_memory, axis=-1)
-    numer = jnp.einsum(
-        "chrbs,bcshe->chre",
-        w_local.astype(dtype).reshape(per_owner, heads_dev, span, owners, MOST),
-        v_in,
-        preferred_element_type=jnp.float32,
-    )
-    numer = numer + jnp.einsum(
-        "chrd,hde->chre", w_memory.astype(dtype), cent_v_all, preferred_element_type=jnp.float32
-    )
-    result = (numer / denom[..., None]).astype(dtype)
+    valid = valid.astype(jnp.float32).reshape(per_owner, heads_dev, 1, span)
+
+    result = cluster_attention(qkv, cent_in, valid, scale)
     result = result.reshape(per_owner, heads_dev, owners, MOST, head_dim)
     back = jnp.transpose(result, (2, 0, 3, 1, 4)).reshape(owners, group, width)
     back = lax.all_to_all(back, "seq", split_axis=0, concat_axis=0, tiled=True)

time: 331 us -> 272 us (0.82)
  other arithmetic: 32 us -> 6.55 us
  matrix products: 29 us -> 5.91 us
  local copies, waits for them, and re-layouts: 54.5 us -> 33.3 us
  Pallas kernels: 0 us -> 10.9 us
    dot_general x4 -> x0, matrix products: 23.1 us -> none  [the longest x1 12.9 us: on_device(): jnp.einsum('acrhe,bcshe->charbs', q_in, k_in, preferred_element_type=jnp....]
    reduce_sum x2 -> x0, other arithmetic: 12.8 us -> none  [on_device(): denom = jnp.sum(w_local, axis=-1) + jnp.sum(w_memory, axis=-1)]
    convert_element_type x1, other arithmetic: 12.8 us -> 0.61 us  [on_device(): valid = valid.astype(jnp.float32).reshape(per_owner, heads_dev, 1, span)]
    convert_element_type x1 -> x0, local copies, waits for them, and re-layouts: 12 us -> none  [on_device(): w_local.astype(dtype).reshape(per_owner, heads_dev, span, owners, MOST)]
    pallas_call x0 -> x1, Pallas kernels: none -> 10.9 us  [cluster_attention(): pl.pallas_call(functools.partial(attention_kernel, scale=scale), grid=(pe...]
    mul x1 -> x0, local copies, waits for them, and re-layouts: 7.76 us -> none  [on_device(): local = local.reshape(per_owner, heads_dev, span, span) * scale]
    transpose x0 -> x2, local copies, waits for them, and re-layouts: none -> 3.34 us  [the longest x1 2.54 us: on_device(): jnp.transpose(qkv, (1, 2, 4, 0, 3, 5))]
where the time goes in v3:
time: 272 us; the launch traced here: 271 us
  waiting for transfers between devices  171 us (63%)
  local copies, waits for them, and re-layouts  33.3 us (12%)
  starting transfers between devices  30.2 us (11%)
  between operations  13.6 us (5%)
  Pallas kernels  10.9 us (4%)
  other arithmetic  6.55 us (2%)
  matrix products  5.91 us (2%)
    all_to_all x1, waiting for transfers between devices, on_device(): recv = lax.all_to_all(send, 'seq', split_axis=0, concat_axis=0, tiled=True)  86.8 us
    reduce_scatter x1, waiting for transfers between devices, on_device(): lax.psum_scatter(jnp.einsum('kc,tk->ct', out_weight, flat_out, preferred_...  53.6 us
    all_to_all x1, waiting for transfers between devices, on_device(): back = lax.all_to_all(back, 'seq', split_axis=0, concat_axis=0, tiled=True)  30.4 us
    all_to_all x1, starting transfers between devices, on_device(): recv = lax.all_to_all(send, 'seq', split_axis=0, concat_axis=0, tiled=True)  19.2 us
    pallas_call x1, Pallas kernels, cluster_attention(): pl.pallas_call(functools.partial(attention_kernel, scale=scale), grid=(pe...  10.9 us
    all_to_all x1, starting transfers between devices, on_device(): back = lax.all_to_all(back, 'seq', split_axis=0, concat_axis=0, tiled=True)  10.7 us
    reshape x1, local copies, waits for them, and re-layouts, on_device(): body = body.astype(dtype).reshape(owners, 3 * group, width)  5.97 us
  transfers between devices with their start and end apart: 3, of which 3 were waited for; matrix products, arithmetic and copies ran while one was open for 0% of the time, Pallas kernels for 0%

profile of v3, /device:TPU:6, one launch (start us, length us, event | category | flops | bytes accessed | tf_op | source)
XLA Modules:
  0.0 271.2 jit_solution(4517526616839943358)
XLA Ops:
  6.5 0.0 copy-start
  6.5 0.1 iota_compare_fusion.1
  6.6 0.8 pad_maximum_fusion.1
  7.5 0.7 copy.87
  8.2 0.2 convert_reduce_fusion.1
  8.4 0.1 convert_element_type.53
  8.5 0.1 copy.60
  8.6 1.0 copy.86
  9.6 0.7 convert_reduce_fusion
  10.3 0.7 fusion.15
  11.0 0.1 pad.4
  11.1 0.3 copy.73
  11.4 1.1 copy_bitcast_fusion.2
  12.5 2.7 %convert_bitcast_fusion = bf16[64,3,32,2,128]{4,0,2,1,3:T(8,128)(2,1)S(1)} fusion(s32[64,32]{0,1:T(8,128)S(1)} %multiply_add_fusion, s32[2,512]{1,0:T(2,128)S(1)} %get-tuple-element.6, bf16[512,1,2,128]{3,0,1,2:T(8,128)(2,1)S(1)} %get-tuple-element.7, bf16[512,1,2,128]{3,0,1,2:T(8,128)(2,1)S(1)} %get-tuple-element.8, bf16[512,1,2,128]{3,0,1,2:T(8,128)(2,1)S(1)} %bitcast.73), kind=kOutput, calls=%fused_computation.10 | convolution fusion | flops 1616642048 | bytes 3944448 | tf_op jit(solution)/shard_map/hogt,tkhe->okghe/dot_general | solution.py:97
  15.2 4.9 %copy.59 = bf16[64,3,32,2,128]{4,3,2,1,0:T(2,128)(2,1)} copy(bf16[64,3,32,2,128]{4,0,2,1,3:T(8,128)(2,1)S(1)} %convert_bitcast_fusion) | data formatting | bytes 6291456 | tf_op jit(solution)/shard_map/convert_element_type | solution.py:98
  20.1 6.0 %reshape.87 = bf16[64,96,256]{2,1,0:T(8,128)(2,1)} reshape(bf16[64,3,32,2,128]{4,3,2,1,0:T(2,128)(2,1)} %copy.59) | data formatting | bytes 6291456 | tf_op jit(solution)/shard_map/reshape | solution.py:98
  26.1 3.4 %pad_maximum_fusion = bf16[64,112,256]{2,1,0:T(8,128)(2,1)} fusion(bf16[64,8,256]{2,1,0:T(8,128)(2,1)S(1)} %copy.73, bf16[64,8,256]{2,1,0:T(8,128)(2,1)S(1)} %broadcast_in_dim.9, bf16[64,96,256]{2,1,0:T(8,128)(2,1)} %reshape.87), kind=kLoop, calls=%fused_computation.8 | loop fusion | flops 11010048 | bytes 7340032 | tf_op jit(solution)/shard_map/concatenate | solution.py:101
  29.5 19.2 %all-to-all-start = ((bf16[64,112,256]{2,1,0:T(8,128)(2,1)}), bf16[64,112,256]{2,1,0:T(8,128)(2,1)}, u32[]{:S(2)}, u32[]{:S(2)}) async-start(bf16[64,112,256]{2,1,0:T(8,128)(2,1)} %pad_maximum_fusion), calls=%async_computation | async-start | bytes 7340032 | tf_op jit(solution)/shard_map/all_to_all | solution.py:102
  48.7 0.1 lt.55
  48.8 86.8 %all-to-all-done = bf16[64,112,256]{2,1,0:T(8,128)(2,1)} async-done(((bf16[64,112,256]{2,1,0:T(8,128)(2,1)}), bf16[64,112,256]{2,1,0:T(8,128)(2,1)}, u32[]{:S(2)}, u32[]{:S(2)}) %all-to-all-start) | async-done | bytes 3670048 | tf_op jit(solution)/shard_map/all_to_all | solution.py:102
  135.7 0.9 slice.16
  136.6 0.1 copy.75
  136.7 0.1 lt.57
  136.8 0.2 lt.62
  137.0 2.1 slice.14
  139.1 2.5 copy.85
  141.7 1.0 slice.15
  142.6 0.1 reshape.91
  142.7 0.8 copy.63
  143.5 0.6 compare_convert_fusion.valid_ref
  144.1 10.9 %shard_map.73 = bf16[4,2,512,128]{3,2,1,0:T(8,128)(2,1)} custom-call(bf16[3,4,2,512,128]{4,3,2,1,0:T(8,128)(2,1)} %bitcast.65, bf16[3,4,2,512,128]{4,3,2,1,0:T(8,128)(2,1)} %bitcast.66, bf16[3,4,2,512,128]{4,3,2,1,0:T(8,128)(2,1)} %bitcast.67, bf16[2,2,256,128]{3,2,1,0:T(8,128)(2,1)} %bitcast.69, bf16[2,2,256,128]{3,2,1,0:T(8,128)(2,1)} %bitcast.70, ...), custom_call_target="tpu_custom_call" | custom-call | tf_op jit(solution)/shard_map/pallas_call | solution.py:48
  155.0 2.4 copy_bitcast_fusion.1
  157.5 10.7 %all-to-all-start.1 = ((bf16[64,32,256]{2,1,0:T(8,128)(2,1)}), bf16[64,32,256]{2,1,0:T(8,128)(2,1)}, u32[]{:S(2)}, u32[]{:S(2)}) async-start(bf16[64,32,256]{2,1,0:T(8,128)(2,1)} %copy_bitcast_fusion.1), calls=%async_computation.1 | async-start | bytes 2097152 | tf_op jit(solution)/shard_map/all_to_all | solution.py:120
  168.2 0.2 reduce-scatter.2.cloned.1.call-start
  168.4 0.1 copy.69
  168.6 0.2 reshape.98
  168.7 30.4 %all-to-all-done.1 = bf16[64,32,256]{2,1,0:T(8,128)(2,1)} async-done(((bf16[64,32,256]{2,1,0:T(8,128)(2,1)}), bf16[64,32,256]{2,1,0:T(8,128)(2,1)}, u32[]{:S(2)}, u32[]{:S(2)}) %all-to-all-start.1) | async-done | bytes 1048608 | tf_op jit(solution)/shard_map/all_to_all | solution.py:120
  199.1 1.3 reshape.95
  200.4 5.0 %gather_fusion = bf16[1024,128]{1,0:T(8,128)(2,1)S(1)} fusion(bf16[2048,2,128]{2,1,0:T(2,128)(2,1)S(1)} %reshape.95, s32[1024]{0:T(1024)S(1)} %reshape.98), kind=kCustom, calls=%fused_computation | custom fusion | bytes 532480 | tf_op jit(solution)/shard_map/gather | solution.py:122
  205.4 0.1 reshape.96
  205.5 0.0 copy-done
  205.5 3.2 %fusion.3 = bf16[4096,512]{0,1:T(8,128)(2,1)} fusion(bf16[512,256]{1,0:T(8,128)(2,1)S(1)} %reshape.96, bf16[256,4096]{1,0:T(8,128)(2,1)S(1)} %copy-done), kind=kOutput, calls=%fused_computation.5 | convolution fusion | flops 1075838976 | bytes 6553600 | tf_op jit(solution)/shard_map/kc,tk->ct/dot_general | solution.py:126
  208.7 0.0 reduce-scatter.2.cloned.1.call-update
  208.8 53.6 %reduce-scatter.2.cloned.1.call-done = bf16[512,512]{0,1:T(8,128)(2,1)} async-done(((bf16[4096,512]{0,1:T(8,128)(2,1)}), bf16[512,512]{0,1:T(8,128)(2,1)}) %reduce-scatter.2.cloned.1.call-update) | async-done | bytes 524304 | tf_op jit(solution)/shard_map/reduce_scatter | solution.py:125
  262.3 2.0 copy.70
  (7 shorter events, 0.1 us)
Async XLA Ops:
  6.5 199.0 %copy-start = (bf16[256,4096]{1,0:T(8,128)(2,1)S(1)}, bf16[256,4096]{1,0:T(8,128)(2,1)}, u32[]{:S(2)}) copy-start(bf16[256,4096]{1,0:T(8,128)(2,1)} %param.13) | copy-start | bytes 6291460
  29.5 106.2 %all-to-all-start = ((bf16[64,112,256]{2,1,0:T(8,128)(2,1)}), bf16[64,112,256]{2,1,0:T(8,128)(2,1)}, u32[]{:S(2)}, u32[]{:S(2)}) async-start(bf16[64,112,256]{2,1,0:T(8,128)(2,1)} %pad_maximum_fusion), calls=%async_computation | async-start | bytes 7340032 | tf_op jit(solution)/shard_map/all_to_all | solution.py:102
  157.5 41.6 %all-to-all-start.1 = ((bf16[64,32,256]{2,1,0:T(8,128)(2,1)}), bf16[64,32,256]{2,1,0:T(8,128)(2,1)}, u32[]{:S(2)}, u32[]{:S(2)}) async-start(bf16[64,32,256]{2,1,0:T(8,128)(2,1)} %copy_bitcast_fusion.1), calls=%async_computation.1 | async-start | bytes 2097152 | tf_op jit(solution)/shard_map/all_to_all | solution.py:120
  168.2 94.1 %reduce-scatter.2.cloned.1.call-start = ((), (), s32[]{:S(2)}) async-start(), calls=%async_computation.3 | async-start | bytes 4718592 | tf_op jit(solution)/shard_map/reduce_scatter | solution.py:125
Sparse Core Ops, SparseCore 0:
  208.9 53.3 reduce-scatter.1

commit v4 on v3

--- a/solution.py
+++ b/solution.py
@@ -72,6 +72,12 @@
     scale = head_dim ** (-0.5)
     dtype = queries.dtype
 
+    n_head = lax.axis_size("head")
+    rows_dev, features = out_weight.shape
+    feat = features // n_head
+    w_parts = jnp.transpose(out_weight.reshape(rows_dev, n_head, feat), (1, 0, 2))
+    w_mine = lax.all_to_all(w_parts, "head", split_axis=0, concat_axis=0, tiled=True)
+
     assign = clusters[:, :, 0]
     order = jnp.arange(tok_dev, dtype=jnp.int32)
     earlier = (assign[:, :, None] == assign[:, None, :]) & (
@@ -100,6 +106,7 @@
     cent = jnp.broadcast_to(cent, (owners, cent_rows, width))
     send = jnp.concatenate([body, cent, counts], axis=1)
     recv = lax.all_to_all(send, "seq", split_axis=0, concat_axis=0, tiled=True)
+    recv, w_mine = lax.optimization_barrier((recv, w_mine))
 
     span = owners * MOST
     qkv = recv[:, 0 : 3 * group].reshape(owners, 3, per_owner, MOST, heads_dev, head_dim)
@@ -122,14 +129,10 @@
     attended = back[slot_of, head_cols]
 
     flat_out = attended.reshape(tok_dev, heads_dev * head_dim)
-    return lax.psum_scatter(
-        jnp.einsum("kc,tk->ct", out_weight, flat_out, preferred_element_type=jnp.float32).astype(
-            jnp.bfloat16
-        ),
-        "head",
-        scatter_dimension=0,
-        tiled=True,
-    )
+    att_all = lax.all_gather(flat_out, "head", axis=0, tiled=False)
+    partial = jnp.einsum("gkf,gtk->gft", w_mine, att_all, preferred_element_type=jnp.float32)
+    total = jnp.sum(partial.astype(jnp.bfloat16).astype(jnp.float32), axis=0)
+    return total.astype(jnp.bfloat16)
 
 
 def solution(mesh):

time: 272 us -> 297 us (1.092)
  waiting for transfers between devices: 171 us -> 185 us
  local copies, waits for them, and re-layouts: 33.3 us -> 41.9 us
  starting transfers between devices: 30.2 us -> 33.6 us
    reduce_scatter x1 -> x0, waiting for transfers between devices: 53.6 us -> none  [on_device(): lax.psum_scatter(jnp.einsum('kc,tk->ct', out_weight, flat_out, preferred_...]
    all_gather x0 -> x1, waiting for transfers between devices: none -> 38.1 us  [on_device(): att_all = lax.all_gather(flat_out, 'head', axis=0, tiled=False)]
    all_to_all x0 -> x1, waiting for transfers between devices: none -> 31.3 us  [on_device(): lax.all_to_all(w_parts, 'head', split_axis=0, concat_axis=0, tiled=True)]
    optimization_barrier x0 -> x1, local copies, waits for them, and re-layouts: none -> 8.63 us  [on_device(): recv, w_mine = lax.optimization_barrier((recv, w_mine))]
    all_to_all x0 -> x1, starting transfers between devices: none -> 7.41 us  [on_device(): lax.all_to_all(w_parts, 'head', split_axis=0, concat_axis=0, tiled=True)]
    reshape x1, local copies, waits for them, and re-layouts: 0.09 us -> 4.09 us  [on_device(): out_weight.reshape(rows_dev, n_head, feat)]
  transfers between devices with their start and end apart: 3 -> 4, of which waited for: 3 -> 4; matrix products, arithmetic and copies ran while one was open for 0% -> 6% of each run, Pallas kernels for 0% -> 0%
where the time goes in v4:
time: 297 us; the launch traced here: 296 us
  waiting for transfers between devices  185 us (62%)
  local copies, waits for them, and re-layouts  41.9 us (14%)
  starting transfers between devices  33.6 us (11%)
  between operations  13.6 us (5%)
  Pallas kernels  10.9 us (4%)
  matrix products  7.12 us (2%)
  other arithmetic  4.25 us (1%)
    all_to_all x1, waiting for transfers between devices, on_device(): recv = lax.all_to_all(send, 'seq', split_axis=0, concat_axis=0, tiled=True)  86.4 us
    all_gather x1, waiting for transfers between devices, on_device(): att_all = lax.all_gather(flat_out, 'head', axis=0, tiled=False)  38.1 us
    all_to_all x1, waiting for transfers between devices, on_device(): lax.all_to_all(w_parts, 'head', split_axis=0, concat_axis=0, tiled=True)  31.3 us
    all_to_all x1, waiting for transfers between devices, on_device(): back = lax.all_to_all(back, 'seq', split_axis=0, concat_axis=0, tiled=True)  28.7 us
    all_to_all x1, starting transfers between devices, on_device(): recv = lax.all_to_all(send, 'seq', split_axis=0, concat_axis=0, tiled=True)  16.5 us
    pallas_call x1, Pallas kernels, cluster_attention(): pl.pallas_call(functools.partial(attention_kernel, scale=scale), grid=(pe...  10.9 us
    all_to_all x1, starting transfers between devices, on_device(): back = lax.all_to_all(back, 'seq', split_axis=0, concat_axis=0, tiled=True)  9.69 us
    optimization_barrier x1, local copies, waits for them, and re-layouts, on_device(): recv, w_mine = lax.optimization_barrier((recv, w_mine))  8.63 us
  transfers between devices with their start and end apart: 4, of which 4 were waited for; matrix products, arithmetic and copies ran while one was open for 6% of the time, Pallas kernels for 0%

profile of v4, /device:TPU:6, one launch (start us, length us, event | category | flops | bytes accessed | tf_op | source)
XLA Modules:
  0.0 296.0 jit_solution(2524881195569540070)
XLA Ops:
  6.5 4.1 %copy.88 = bf16[256,4096]{0,1:T(8,128)(2,1)} copy(bf16[256,4096]{1,0:T(8,128)(2,1)} %param.13) | data formatting | bytes 4194304 | tf_op jit(solution)/shard_map/reshape | solution.py:78
  10.6 0.0 copy-start.3
  10.6 7.4 %all-to-all-start.1 = ((bf16[8,256,512]{1,2,0:T(8,128)(2,1)}), bf16[8,256,512]{1,2,0:T(8,128)(2,1)}, u32[]{:S(2)}, u32[]{:S(2)}) async-start(bf16[8,256,512]{1,2,0:T(8,128)(2,1)} %bitcast.14), calls=%async_computation.1 | async-start | bytes 4194304 | tf_op jit(solution)/shard_map/all_to_all | solution.py:79
  18.1 0.0 copy-done.3
  18.1 0.0 copy-done
  18.1 0.1 iota_compare_fusion.1
  18.2 0.7 convert_reduce_fusion.1
  18.9 0.0 copy-done.1
  19.0 0.0 copy-done.2
  19.0 0.1 copy_bitcast_fusion.2
  19.0 2.7 convert_bitcast_fusion
  21.8 4.9 %copy.73 = bf16[64,3,32,2,128]{4,3,2,1,0:T(2,128)(2,1)} copy(bf16[64,3,32,2,128]{4,0,2,1,3:T(8,128)(2,1)S(1)} %convert_bitcast_fusion) | data formatting | bytes 6291456 | tf_op jit(solution)/shard_map/convert_element_type | solution.py:104
  26.7 4.6 %reshape.87 = bf16[64,96,256]{2,1,0:T(8,128)(2,1)S(1)} reshape(bf16[64,3,32,2,128]{4,3,2,1,0:T(2,128)(2,1)} %copy.73) | data formatting | bytes 6291456 | tf_op jit(solution)/shard_map/reshape | solution.py:104
  31.3 0.2 convert_reduce_fusion.2
  31.5 0.1 convert_element_type.52
  31.6 0.1 copy.74
  31.7 0.9 pad.4
  32.6 1.3 copy.87
  33.9 0.0 copy-done.4
  33.9 0.0 copy-done.5
  34.0 1.9 pad_maximum_fusion
  35.9 31.3 %all-to-all-done.1 = bf16[8,256,512]{1,2,0:T(8,128)(2,1)} async-done(((bf16[8,256,512]{1,2,0:T(8,128)(2,1)}), bf16[8,256,512]{1,2,0:T(8,128)(2,1)}, u32[]{:S(2)}, u32[]{:S(2)}) %all-to-all-start.1) | async-done | bytes 2097184 | tf_op jit(solution)/shard_map/all_to_all | solution.py:79
  67.2 16.5 %all-to-all-start = ((bf16[64,112,256]{2,1,0:T(8,128)(2,1)}), bf16[64,112,256]{2,1,0:T(8,128)(2,1)}, u32[]{:S(2)}, u32[]{:S(2)}) async-start(bf16[64,112,256]{2,1,0:T(8,128)(2,1)} %pad_maximum_fusion), calls=%async_computation | async-start | bytes 7340032 | tf_op jit(solution)/shard_map/all_to_all | solution.py:108
  83.8 0.1 lt.55
  83.8 86.4 %all-to-all-done = bf16[64,112,256]{2,1,0:T(8,128)(2,1)} async-done(((bf16[64,112,256]{2,1,0:T(8,128)(2,1)}), bf16[64,112,256]{2,1,0:T(8,128)(2,1)}, u32[]{:S(2)}, u32[]{:S(2)}) %all-to-all-start) | async-done | bytes 3670048 | tf_op jit(solution)/shard_map/all_to_all | solution.py:108
  170.3 8.6 %copy.79 = bf16[64,112,256]{0,2,1:T(8,128)(2,1)} copy(bf16[64,112,256]{2,1,0:T(8,128)(2,1)} %all-to-all-done) | data formatting | bytes 7340032 | tf_op jit(solution)/shard_map/optimization_barrier | solution.py:109
  178.9 2.1 slice.9
  181.0 1.0 slice.10
  182.0 0.7 slice_convert_fusion
  182.7 0.8 lt.57
  183.5 1.1 lt.62
  184.6 2.5 copy.99
  187.1 0.1 reshape.92
  187.2 0.8 copy.78
  188.0 0.6 compare_convert_fusion.valid_ref
  188.6 10.9 %shard_map.73 = bf16[4,2,512,128]{3,2,1,0:T(8,128)(2,1)} custom-call(bf16[3,4,2,512,128]{4,3,2,1,0:T(8,128)(2,1)} %bitcast.67, bf16[3,4,2,512,128]{4,3,2,1,0:T(8,128)(2,1)} %bitcast.68, bf16[3,4,2,512,128]{4,3,2,1,0:T(8,128)(2,1)} %bitcast.69, bf16[2,2,256,128]{3,2,1,0:T(8,128)(2,1)} %bitcast.71, bf16[2,2,256,128]{3,2,1,0:T(8,128)(2,1)} %bitcast.72, ...), custom_call_target="tpu_custom_call" | custom-call | tf_op jit(solution)/shard_map/pallas_call | solution.py:48
  199.5 2.3 copy_bitcast_fusion.1
  201.9 9.7 %all-to-all-start.2 = ((bf16[64,32,256]{2,1,0:T(8,128)(2,1)}), bf16[64,32,256]{2,1,0:T(8,128)(2,1)S(1)}, u32[]{:S(2)}, u32[]{:S(2)}) async-start(bf16[64,32,256]{2,1,0:T(8,128)(2,1)} %copy_bitcast_fusion.1), calls=%async_computation.2 | async-start | bytes 2097152 | tf_op jit(solution)/shard_map/all_to_all | solution.py:127
  211.5 0.0 all-gather.2.cloned.1.call-start
  211.6 0.1 copy.84
  211.7 0.2 reshape.98
  211.9 28.7 %all-to-all-done.2 = bf16[64,32,256]{2,1,0:T(8,128)(2,1)S(1)} async-done(((bf16[64,32,256]{2,1,0:T(8,128)(2,1)}), bf16[64,32,256]{2,1,0:T(8,128)(2,1)S(1)}, u32[]{:S(2)}, u32[]{:S(2)}) %all-to-all-start.2) | async-done | bytes 1048608 | tf_op jit(solution)/shard_map/all_to_all | solution.py:127
  240.6 0.3 reshape.96
  240.9 5.0 %gather_fusion = bf16[1024,128]{1,0:T(8,128)(2,1)S(1)} fusion(bf16[2048,2,128]{2,1,0:T(2,128)(2,1)S(1)} %reshape.96, s32[1024]{0:T(1024)S(1)} %reshape.98), kind=kCustom, calls=%fused_computation | custom fusion | bytes 532480 | tf_op jit(solution)/shard_map/gather | solution.py:129
  245.9 0.8 all_gather_reshape.3
  246.7 0.0 all-gather.2.cloned.1.call-update
  246.7 38.1 %all-gather.2.cloned.1.call-done = bf16[8,512,256]{2,1,0:T(8,128)(2,1)} async-done(((bf16[1,512,256]{2,1,0:T(8,128)(2,1)}), bf16[8,512,256]{2,1,0:T(8,128)(2,1)}) %all-gather.2.cloned.1.call-update) | async-done | bytes 2097168 | tf_op jit(solution)/shard_map/all_gather | solution.py:132
  284.8 4.4 %convert_reduce_fusion = bf16[512,512]{1,0:T(8,128)(2,1)} fusion(bf16[8,256,512]{1,2,0:T(8,128)(2,1)} %all-to-all-done.1, bf16[8,512,256]{2,1,0:T(8,128)(2,1)} %all-gather.2.cloned.1.call-done), kind=kOutput, calls=%fused_computation.4 | convolution fusion | flops 1077673984 | bytes 4718592 | tf_op jit(solution)/shard_map/gkf,gtk->gft/dot_general | solution.py:133
  (15 shorter events, 0.1 us)
Async XLA Ops:
  10.6 7.4 %copy-start.3 = (s32[2,512,1]{1,2,0:T(1,128)S(1)}, s32[2,512,1]{1,2,0:T(1,128)}, u32[]{:S(2)}) copy-start(s32[2,512,1]{1,2,0:T(1,128)} %param.10) | copy-start | bytes 12292
  10.6 7.4 %copy-start = (bf16[512,2,128]{2,1,0:T(2,128)(2,1)S(1)}, bf16[512,2,128]{2,1,0:T(2,128)(2,1)}, u32[]{:S(2)}) copy-start(bf16[512,2,128]{2,1,0:T(2,128)(2,1)} %param.7) | copy-start | bytes 786436
  10.6 8.3 %copy-start.1 = (bf16[512,2,128]{2,1,0:T(2,128)(2,1)S(1)}, bf16[512,2,128]{2,1,0:T(2,128)(2,1)}, u32[]{:S(2)}) copy-start(bf16[512,2,128]{2,1,0:T(2,128)(2,1)} %param.9) | copy-start | bytes 786436
  10.6 8.3 %copy-start.2 = (bf16[512,2,128]{2,1,0:T(2,128)(2,1)S(1)}, bf16[512,2,128]{2,1,0:T(2,128)(2,1)}, u32[]{:S(2)}) copy-start(bf16[512,2,128]{2,1,0:T(2,128)(2,1)} %param.8) | copy-start | bytes 786436
  10.6 56.6 %all-to-all-start.1 = ((bf16[8,256,512]{1,2,0:T(8,128)(2,1)}), bf16[8,256,512]{1,2,0:T(8,128)(2,1)}, u32[]{:S(2)}, u32[]{:S(2)}) async-start(bf16[8,256,512]{1,2,0:T(8,128)(2,1)} %bitcast.14), calls=%async_computation.1 | async-start | bytes 4194304 | tf_op jit(solution)/shard_map/all_to_all | solution.py:79
  26.6 7.2 %copy-start.4 = (bf16[2,4,128]{2,1,0:T(4,128)(2,1)S(1)}, bf16[2,4,128]{2,1,0:T(4,128)(2,1)}, u32[]{:S(2)}) copy-start(bf16[2,4,128]{2,1,0:T(4,128)(2,1)} %param.12) | copy-start | bytes 6148
  26.6 7.2 %copy-start.5 = (bf16[2,4,128]{2,1,0:T(4,128)(2,1)S(1)}, bf16[2,4,128]{2,1,0:T(4,128)(2,1)}, u32[]{:S(2)}) copy-start(bf16[2,4,128]{2,1,0:T(4,128)(2,1)} %param.11) | copy-start | bytes 6148
  67.2 103.0 %all-to-all-start = ((bf16[64,112,256]{2,1,0:T(8,128)(2,1)}), bf16[64,112,256]{2,1,0:T(8,128)(2,1)}, u32[]{:S(2)}, u32[]{:S(2)}) async-start(bf16[64,112,256]{2,1,0:T(8,128)(2,1)} %pad_maximum_fusion), calls=%async_computation | async-start | bytes 7340032 | tf_op jit(solution)/shard_map/all_to_all | solution.py:108
  201.9 38.8 %all-to-all-start.2 = ((bf16[64,32,256]{2,1,0:T(8,128)(2,1)}), bf16[64,32,256]{2,1,0:T(8,128)(2,1)S(1)}, u32[]{:S(2)}, u32[]{:S(2)}) async-start(bf16[64,32,256]{2,1,0:T(8,128)(2,1)} %copy_bitcast_fusion.1), calls=%async_computation.2 | async-start | bytes 2097152 | tf_op jit(solution)/shard_map/all_to_all | solution.py:127
  211.5 73.2 %all-gather.2.cloned.1.call-start = ((), (), s32[]{:S(2)}) async-start(), calls=%async_computation.3 | async-start | bytes 2359296 | tf_op jit(solution)/shard_map/all_gather | solution.py:132
Sparse Core Ops, SparseCore 0:
  246.8 37.9 all-gather.1

commit v5 on v3

--- a/solution.py
+++ b/solution.py
@@ -11,12 +11,17 @@
 
 
 def attention_kernel(q_ref, k_ref, v_ref, ck_ref, cv_ref, valid_ref, out_ref, *, scale):
-    q = q_ref[0, 0, 0]
-    k = k_ref[0, 0, 0]
-    v = v_ref[0, 0, 0]
+    sources, depth, head_dim = q_ref.shape
+    span = sources * depth
+
+    def flat(ref):
+        return ref[...].astype(jnp.float32).reshape(span, head_dim).astype(ref.dtype)
+
+    q = flat(q_ref)
+    k = flat(k_ref)
+    v = flat(v_ref)
     ck = ck_ref[0, 0]
     cv = cv_ref[0, 0]
-    span = q.shape[0]
     contract = (((1,), (1,)), ((), ()))
     local = lax.dot_general(q, k, contract, preferred_element_type=jnp.float32) * scale
     row = lax.broadcasted_iota(jnp.int32, (span, span), 0)
@@ -32,15 +37,19 @@
     denom = jnp.sum(w_local, axis=1, keepdims=True) + jnp.sum(w_memory, axis=1, keepdims=True)
     numer = jnp.dot(w_local.astype(v.dtype), v, preferred_element_type=jnp.float32)
     numer = numer + jnp.dot(w_memory.astype(cv.dtype), cv, preferred_element_type=jnp.float32)
-    out_ref[0, 0] = (numer / denom).astype(out_ref.dtype)
+    result = (numer / denom).astype(out_ref.dtype).astype(jnp.float32)
+    out_ref[...] = result.reshape(sources, depth, head_dim).astype(out_ref.dtype)
 
 
-def cluster_attention(qkv, cent, valid, scale):
-    _, per_owner, heads_dev, span, head_dim = qkv.shape
+def cluster_attention(recv, cent, valid, scale, per_owner, heads_dev):
+    sources, _, width = recv.shape
+    head_dim = width // heads_dev
     clusters = cent.shape[2]
 
     def pick(kind):
-        return pl.BlockSpec((1, 1, 1, span, head_dim), lambda c, h: (kind, c, h, 0, 0))
+        return pl.BlockSpec(
+            (sources, MOST, head_dim), lambda c, h: (0, kind * per_owner + c, h)
+        )
 
     def centroid(kind):
         return pl.BlockSpec((1, 1, clusters, head_dim), lambda c, h: (kind, h, 0, 0))
@@ -54,11 +63,11 @@
             pick(2),
             centroid(0),
             centroid(1),
-            pl.BlockSpec((1, 1, 1, span), lambda c, h: (c, h, 0, 0)),
+            pl.BlockSpec((1, 1, 1, sources * MOST), lambda c, h: (c, h, 0, 0)),
         ],
-        out_specs=pl.BlockSpec((1, 1, span, head_dim), lambda c, h: (c, h, 0, 0)),
-        out_shape=jax.ShapeDtypeStruct((per_owner, heads_dev, span, head_dim), qkv.dtype),
-    )(qkv, qkv, qkv, cent, cent, valid)
+        out_specs=pl.BlockSpec((sources, MOST, head_dim), lambda c, h: (0, c, h)),
+        out_shape=jax.ShapeDtypeStruct((sources, per_owner * MOST, width), recv.dtype),
+    )(recv, recv, recv, cent, cent, valid)
 
 
 def on_device(queries, keys, values, clusters, cent_keys, cent_values, out_weight):
@@ -102,8 +111,6 @@
     recv = lax.all_to_all(send, "seq", split_axis=0, concat_axis=0, tiled=True)
 
     span = owners * MOST
-    qkv = recv[:, 0 : 3 * group].reshape(owners, 3, per_owner, MOST, heads_dev, head_dim)
-    qkv = jnp.transpose(qkv, (1, 2, 4, 0, 3, 5)).reshape(3, per_owner, heads_dev, span, head_dim)
     cent_in = recv[:, 3 * group : 3 * group + cent_rows].reshape(
         owners, 2, heads_dev, per_owner, head_dim
     )
@@ -114,9 +121,7 @@
     valid = depth[None, None, None, :] < jnp.transpose(cnt, (2, 1, 0))[..., None]
     valid = valid.astype(jnp.float32).reshape(per_owner, heads_dev, 1, span)
 
-    result = cluster_attention(qkv, cent_in, valid, scale)
-    result = result.reshape(per_owner, heads_dev, owners, MOST, head_dim)
-    back = jnp.transpose(result, (2, 0, 3, 1, 4)).reshape(owners, group, width)
+    back = cluster_attention(recv, cent_in, valid, scale, per_owner, heads_dev)
     back = lax.all_to_all(back, "seq", split_axis=0, concat_axis=0, tiled=True)
     back = back.reshape(owners * group, heads_dev, head_dim)
     attended = back[slot_of, head_cols]

time: 272 us -> 264 us (0.971)
  local copies, waits for them, and re-layouts: 33.3 us -> 25.5 us
    transpose x2 -> x0, local copies, waits for them, and re-layouts: 3.34 us -> none  [the longest x1 2.54 us: on_device(): jnp.transpose(qkv, (1, 2, 4, 0, 3, 5))]
    slice x2 -> x0, local copies, waits for them, and re-layouts: 3.03 us -> none  [the longest x1 2.11 us: on_device(): recv[:, 0:3 * group]]
where the time goes in v5:
time: 264 us
  waiting for transfers between devices  171 us (65%)
  starting transfers between devices  30.1 us (11%)
  local copies, waits for them, and re-layouts  25.5 us (10%)
  between operations  13.6 us (5%)
  Pallas kernels  11.1 us (4%)
  other arithmetic  6.63 us (3%)
  matrix products  5.91 us (2%)
    all_to_all x1, waiting for transfers between devices, on_device(): recv = lax.all_to_all(send, 'seq', split_axis=0, concat_axis=0, tiled=True)  86.9 us
    reduce_scatter x1, waiting for transfers between devices, on_device(): lax.psum_scatter(jnp.einsum('kc,tk->ct', out_weight, flat_out, preferred_...  53.6 us
    all_to_all x1, waiting for transfers between devices, on_device(): back = lax.all_to_all(back, 'seq', split_axis=0, concat_axis=0, tiled=True)  30.4 us
    all_to_all x1, starting transfers between devices, on_device(): recv = lax.all_to_all(send, 'seq', split_axis=0, concat_axis=0, tiled=True)  19.2 us
    pallas_call x1, Pallas kernels, cluster_attention(): pl.pallas_call(functools.partial(attention_kernel, scale=scale), grid=(pe...  11.1 us
    all_to_all x1, starting transfers between devices, on_device(): back = lax.all_to_all(back, 'seq', split_axis=0, concat_axis=0, tiled=True)  10.7 us
    reshape x1, local copies, waits for them, and re-layouts, on_device(): body = body.astype(dtype).reshape(owners, 3 * group, width)  6.01 us
  transfers between devices with their start and end apart: 3, of which 3 were waited for; matrix products, arithmetic and copies ran while one was open for 0% of the time, Pallas kernels for 0%

profile of v5, /device:TPU:6, one launch (start us, length us, event | category | flops | bytes accessed | tf_op | source)
XLA Modules:
  0.0 263.7 jit_solution(15787185368511529359)
XLA Ops:
  6.5 0.0 copy-start
  6.5 0.1 iota_compare_fusion.1
  6.6 0.8 copy.64
  7.5 0.2 convert_reduce_fusion.1
  7.7 0.7 convert_reduce_fusion
  8.4 0.7 fusion.15
  9.1 1.0 copy.63
  10.1 1.1 copy_bitcast_fusion
  11.2 2.7 %convert_bitcast_fusion = bf16[64,3,32,2,128]{4,0,2,1,3:T(8,128)(2,1)S(1)} fusion(s32[64,32]{0,1:T(8,128)S(1)} %multiply_add_fusion, s32[2,512]{1,0:T(2,128)S(1)} %get-tuple-element.6, bf16[512,1,2,128]{3,0,1,2:T(8,128)(2,1)S(1)} %get-tuple-element.7, bf16[512,1,2,128]{3,0,1,2:T(8,128)(2,1)S(1)} %get-tuple-element.8, bf16[512,1,2,128]{3,0,1,2:T(8,128)(2,1)S(1)} %bitcast.55), kind=kOutput, calls=%fused_computation.9 | convolution fusion | flops 1616642048 | bytes 3944448 | tf_op jit(solution)/shard_map/hogt,tkhe->okghe/dot_general | solution.py:106
  13.9 4.9 %copy.42 = bf16[64,3,32,2,128]{4,3,2,1,0:T(2,128)(2,1)} copy(bf16[64,3,32,2,128]{4,0,2,1,3:T(8,128)(2,1)S(1)} %convert_bitcast_fusion) | data formatting | bytes 6291456 | tf_op jit(solution)/shard_map/convert_element_type | solution.py:107
  18.8 0.0 copy-start.1
  18.8 0.0 copy-start.2
  18.8 6.0 %reshape.75 = bf16[64,96,256]{2,1,0:T(8,128)(2,1)} reshape(bf16[64,3,32,2,128]{4,3,2,1,0:T(2,128)(2,1)} %copy.42) | data formatting | bytes 6291456 | tf_op jit(solution)/shard_map/reshape | solution.py:107
  24.8 0.1 convert_element_type.53
  24.9 0.1 copy.43
  25.0 0.1 pad.4
  25.1 0.3 copy.54
  25.4 0.0 copy-done.1
  25.4 0.0 copy-done.2
  25.5 3.4 %pad_maximum_fusion = bf16[64,112,256]{2,1,0:T(8,128)(2,1)} fusion(bf16[64,8,256]{2,1,0:T(8,128)(2,1)S(1)} %copy.54, bf16[64,8,256]{2,1,0:T(8,128)(2,1)S(1)} %broadcast_in_dim.9, bf16[64,96,256]{2,1,0:T(8,128)(2,1)} %reshape.75), kind=kLoop, calls=%fused_computation.8 | loop fusion | flops 11010048 | bytes 7340032 | tf_op jit(solution)/shard_map/concatenate | solution.py:110
  28.9 19.2 %all-to-all-start = ((bf16[64,112,256]{2,1,0:T(8,128)(2,1)}), bf16[64,112,256]{2,1,0:T(8,128)(2,1)}, u32[]{:S(2)}, u32[]{:S(2)}) async-start(bf16[64,112,256]{2,1,0:T(8,128)(2,1)} %pad_maximum_fusion), calls=%async_computation | async-start | bytes 7340032 | tf_op jit(solution)/shard_map/all_to_all | solution.py:111
  48.1 0.1 lt.55
  48.2 86.9 %all-to-all-done.q_ref.k_ref.v_ref = bf16[64,112,256]{2,1,0:T(8,128)(2,1)} async-done(((bf16[64,112,256]{2,1,0:T(8,128)(2,1)}), bf16[64,112,256]{2,1,0:T(8,128)(2,1)}, u32[]{:S(2)}, u32[]{:S(2)}) %all-to-all-start) | async-done | bytes 3670048 | tf_op jit(solution)/shard_map/all_to_all | solution.py:111
  135.0 1.0 slice.10
  136.0 0.1 reshape.77
  136.1 0.8 copy.45
  136.9 0.9 slice_convert_fusion
  137.8 0.1 copy.46
  137.9 0.1 lt.57
  138.0 0.2 lt.62
  138.2 0.6 compare_convert_fusion.valid_ref
  138.8 11.1 %shard_map.73 = bf16[64,32,256]{2,1,0:T(8,128)(2,1)} custom-call(bf16[64,112,256]{2,1,0:T(8,128)(2,1)} %all-to-all-done.q_ref.k_ref.v_ref, bf16[64,112,256]{2,1,0:T(8,128)(2,1)} %all-to-all-done.q_ref.k_ref.v_ref, bf16[64,112,256]{2,1,0:T(8,128)(2,1)} %all-to-all-done.q_ref.k_ref.v_ref, bf16[2,2,256,128]{3,2,1,0:T(8,128)(2,1)} %bitcast.52, ...), custom_call_target="tpu_custom_call" | custom-call | tf_op jit(solution)/shard_map/pallas_call | solution.py:57
  149.9 10.7 %all-to-all-start.1 = ((bf16[64,32,256]{2,1,0:T(8,128)(2,1)}), bf16[64,32,256]{2,1,0:T(8,128)(2,1)}, u32[]{:S(2)}, u32[]{:S(2)}) async-start(bf16[64,32,256]{2,1,0:T(8,128)(2,1)} %shard_map.73), calls=%async_computation.1 | async-start | bytes 2097152 | tf_op jit(solution)/shard_map/all_to_all | solution.py:125
  160.7 0.2 reduce-scatter.2.cloned.1.call-start
  160.9 0.1 copy.50
  161.1 0.2 reshape.82
  161.2 30.4 %all-to-all-done.1 = bf16[64,32,256]{2,1,0:T(8,128)(2,1)} async-done(((bf16[64,32,256]{2,1,0:T(8,128)(2,1)}), bf16[64,32,256]{2,1,0:T(8,128)(2,1)}, u32[]{:S(2)}, u32[]{:S(2)}) %all-to-all-start.1) | async-done | bytes 1048608 | tf_op jit(solution)/shard_map/all_to_all | solution.py:125
  191.6 1.3 reshape.79
  192.9 5.0 %gather_fusion = bf16[1024,128]{1,0:T(8,128)(2,1)S(1)} fusion(bf16[2048,2,128]{2,1,0:T(2,128)(2,1)S(1)} %reshape.79, s32[1024]{0:T(1024)S(1)} %reshape.82), kind=kCustom, calls=%fused_computation | custom fusion | bytes 532480 | tf_op jit(solution)/shard_map/gather | solution.py:127
  197.9 0.1 reshape.80
  198.0 0.0 copy-done
  198.0 3.2 %fusion.3 = bf16[4096,512]{0,1:T(8,128)(2,1)} fusion(bf16[512,256]{1,0:T(8,128)(2,1)S(1)} %reshape.80, bf16[256,4096]{1,0:T(8,128)(2,1)S(1)} %copy-done), kind=kOutput, calls=%fused_computation.5 | convolution fusion | flops 1075838976 | bytes 6553600 | tf_op jit(solution)/shard_map/kc,tk->ct/dot_general | solution.py:131
  201.2 0.0 reduce-scatter.2.cloned.1.call-update
  201.2 53.6 %reduce-scatter.2.cloned.1.call-done = bf16[512,512]{0,1:T(8,128)(2,1)} async-done(((bf16[4096,512]{0,1:T(8,128)(2,1)}), bf16[512,512]{0,1:T(8,128)(2,1)}) %reduce-scatter.2.cloned.1.call-update) | async-done | bytes 524304 | tf_op jit(solution)/shard_map/reduce_scatter | solution.py:130
  254.8 2.0 copy.51
  (7 shorter events, 0.1 us)
Async XLA Ops:
  6.5 191.5 %copy-start = (bf16[256,4096]{1,0:T(8,128)(2,1)S(1)}, bf16[256,4096]{1,0:T(8,128)(2,1)}, u32[]{:S(2)}) copy-start(bf16[256,4096]{1,0:T(8,128)(2,1)} %param.13) | copy-start | bytes 6291460
  18.8 6.6 %copy-start.1 = (bf16[2,4,128]{2,1,0:T(4,128)(2,1)S(1)}, bf16[2,4,128]{2,1,0:T(4,128)(2,1)}, u32[]{:S(2)}) copy-start(bf16[2,4,128]{2,1,0:T(4,128)(2,1)} %param.12) | copy-start | bytes 6148
  18.8 6.6 %copy-start.2 = (bf16[2,4,128]{2,1,0:T(4,128)(2,1)S(1)}, bf16[2,4,128]{2,1,0:T(4,128)(2,1)}, u32[]{:S(2)}) copy-start(bf16[2,4,128]{2,1,0:T(4,128)(2,1)} %param.11) | copy-start | bytes 6148
  28.9 106.2 %all-to-all-start = ((bf16[64,112,256]{2,1,0:T(8,128)(2,1)}), bf16[64,112,256]{2,1,0:T(8,128)(2,1)}, u32[]{:S(2)}, u32[]{:S(2)}) async-start(bf16[64,112,256]{2,1,0:T(8,128)(2,1)} %pad_maximum_fusion), calls=%async_computation | async-start | bytes 7340032 | tf_op jit(solution)/shard_map/all_to_all | solution.py:111
  149.9 41.6 %all-to-all-start.1 = ((bf16[64,32,256]{2,1,0:T(8,128)(2,1)}), bf16[64,32,256]{2,1,0:T(8,128)(2,1)}, u32[]{:S(2)}, u32[]{:S(2)}) async-start(bf16[64,32,256]{2,1,0:T(8,128)(2,1)} %shard_map.73), calls=%async_computation.1 | async-start | bytes 2097152 | tf_op jit(solution)/shard_map/all_to_all | solution.py:125
  160.7 94.1 %reduce-scatter.2.cloned.1.call-start = ((), (), s32[]{:S(2)}) async-start(), calls=%async_computation.3 | async-start | bytes 4718592 | tf_op jit(solution)/shard_map/reduce_scatter | solution.py:130
Sparse Core Ops, SparseCore 0:
  201.4 53.3 reduce-scatter.1

commit v6 on v5

--- a/solution.py
+++ b/solution.py
@@ -8,6 +8,54 @@
 
 CLUSTERS = 256
 MOST = 8
+
+
+def place_kernel(slot_ref, q_ref, k_ref, v_ref, cent_ref, count_ref, out_ref, *, group):
+    block, _, width = out_ref.shape
+    heads_dev = slot_ref.shape[0]
+    tok_dev, _ = q_ref.shape
+    head_dim = width // heads_dev
+    slots = block * group
+    base = pl.program_id(0) * slots
+    slot_ids = lax.broadcasted_iota(jnp.int32, (slots, tok_dev), 0) + base
+    for h in range(heads_dev):
+        onehot = (slot_ref[h] == slot_ids).astype(q_ref.dtype)
+        cols = slice(h * head_dim, (h + 1) * head_dim)
+        for kind, ref in enumerate((q_ref, k_ref, v_ref)):
+            picked = jnp.dot(onehot, ref[:, cols], preferred_element_type=jnp.float32)
+            out_ref[:, kind * group : (kind + 1) * group, cols] = picked.reshape(
+                block, group, head_dim
+            ).astype(out_ref.dtype)
+    cent_rows = cent_ref.shape[0]
+    out_ref[:, 3 * group : 3 * group + cent_rows, :] = jnp.broadcast_to(
+        cent_ref[...][None], (block, cent_rows, width)
+    )
+    out_ref[:, 3 * group + cent_rows :, :] = count_ref[...]
+
+
+def place(slot_rows, queries, keys, values, cent, counts, group, block):
+    owners, count_rows, width = counts.shape
+    tok_dev = queries.shape[0]
+    cent_rows = cent.shape[0]
+    rows = 3 * group + cent_rows + count_rows
+
+    def whole(shape):
+        return pl.BlockSpec(shape, lambda i: (0,) * len(shape))
+
+    return pl.pallas_call(
+        functools.partial(place_kernel, group=group),
+        grid=(owners // block,),
+        in_specs=[
+            whole(slot_rows.shape),
+            whole((tok_dev, width)),
+            whole((tok_dev, width)),
+            whole((tok_dev, width)),
+            whole((cent_rows, width)),
+            pl.BlockSpec((block, count_rows, width), lambda i: (i, 0, 0)),
+        ],
+        out_specs=pl.BlockSpec((block, rows, width), lambda i: (i, 0, 0)),
+        out_shape=jax.ShapeDtypeStruct((owners, rows, width), queries.dtype),
+    )(slot_rows, queries, keys, values, cent, counts)
 
 
 def attention_kernel(q_ref, k_ref, v_ref, ck_ref, cv_ref, valid_ref, out_ref, *, scale):
@@ -99,15 +147,17 @@
     counts = jnp.pad(counts, ((0, 0), (0, count_rows * width - heads_dev * per_owner)))
     counts = counts.reshape(owners, count_rows, width)
 
-    slot_ids = jnp.arange(owners * group, dtype=jnp.int32)
-    onehot = (slot_of.T[:, None, :] == slot_ids[None, :, None]).astype(dtype)
-    onehot = onehot.reshape(heads_dev, owners, group, tok_dev)
-    rows = jnp.stack([queries, keys, values], axis=1)
-    body = jnp.einsum("hogt,tkhe->okghe", onehot, rows, preferred_element_type=jnp.float32)
-    body = body.astype(dtype).reshape(owners, 3 * group, width)
-    cent = jnp.stack([cent_keys, cent_values], axis=0).reshape(1, cent_rows, width)
-    cent = jnp.broadcast_to(cent, (owners, cent_rows, width))
-    send = jnp.concatenate([body, cent, counts], axis=1)
+    cent = jnp.stack([cent_keys, cent_values], axis=0).reshape(cent_rows, width)
+    send = place(
+        slot_of.T.reshape(heads_dev, 1, tok_dev),
+        queries.reshape(tok_dev, width),
+        keys.reshape(tok_dev, width),
+        values.reshape(tok_dev, width),
+        cent,
+        counts,
+        group,
+        min(8, owners),
+    )
     recv = lax.all_to_all(send, "seq", split_axis=0, concat_axis=0, tiled=True)
 
     span = owners * MOST

time: 264 us -> 257 us (0.973)
  local copies, waits for them, and re-layouts: 25.5 us -> 15.4 us
  Pallas kernels: 11.1 us -> 18.5 us
  other arithmetic: 6.63 us -> 3.86 us
  matrix products: 5.91 us -> 3.21 us
    pallas_call x0 -> x1, Pallas kernels: none -> 7.35 us  [place(): pl.pallas_call(functools.partial(place_kernel, group=group), grid=(owners...]
    convert_element_type x1 -> x0, local copies, waits for them, and re-layouts: 4.9 us -> none  [on_device(): body = body.astype(dtype).reshape(owners, 3 * group, width)]
    reshape x1 -> x2, local copies, waits for them, and re-layouts: 6.01 us -> 1.47 us  [the longest x1 0.87 us: on_device(): values.reshape(tok_dev, width)]
    concatenate x1 -> x0, other arithmetic: 3.37 us -> none  [on_device(): send = jnp.concatenate([body, cent, counts], axis=1)]
    dot_general x1 -> x0, matrix products: 2.71 us -> none  [on_device(): jnp.einsum('hogt,tkhe->okghe', onehot, rows, preferred_element_type=jnp.f...]
where the time goes in v6:
time: 257 us; the launch traced here: 256 us
  waiting for transfers between devices  171 us (67%)
  starting transfers between devices  30.1 us (12%)
  Pallas kernels  18.5 us (7%)
  local copies, waits for them, and re-layouts  15.4 us (6%)
  between operations  13.6 us (5%)
  other arithmetic  3.86 us (2%)
  matrix products  3.21 us (1%)
    all_to_all x1, waiting for transfers between devices, on_device(): recv = lax.all_to_all(send, 'seq', split_axis=0, concat_axis=0, tiled=True)  86.9 us
    reduce_scatter x1, waiting for transfers between devices, on_device(): lax.psum_scatter(jnp.einsum('kc,tk->ct', out_weight, flat_out, preferred_...  53.6 us
    all_to_all x1, waiting for transfers between devices, on_device(): back = lax.all_to_all(back, 'seq', split_axis=0, concat_axis=0, tiled=True)  30.5 us
    all_to_all x1, starting transfers between devices, on_device(): recv = lax.all_to_all(send, 'seq', split_axis=0, concat_axis=0, tiled=True)  19.2 us
    pallas_call x1, Pallas kernels, cluster_attention(): pl.pallas_call(functools.partial(attention_kernel, scale=scale), grid=(pe...  11.1 us
    all_to_all x1, starting transfers between devices, on_device(): back = lax.all_to_all(back, 'seq', split_axis=0, concat_axis=0, tiled=True)  10.9 us
    pallas_call x1, Pallas kernels, place(): pl.pallas_call(functools.partial(place_kernel, group=group), grid=(owners...  7.35 us
  transfers between devices with their start and end apart: 3, of which 3 were waited for; matrix products, arithmetic and copies ran while one was open for 0% of the time, Pallas kernels for 0%

profile of v6, /device:TPU:6, one launch (start us, length us, event | category | flops | bytes accessed | tf_op | source)
XLA Modules:
  0.0 255.5 jit_solution(197791293078511557)
XLA Ops:
  6.5 0.0 copy-start
  6.5 0.0 copy-start.1
  6.5 0.0 copy-start.6
  6.5 0.0 copy-start.2
  6.6 0.1 iota_compare_fusion.1
  6.6 0.8 copy.48
  7.5 0.2 convert_reduce_fusion.1
  7.7 0.7 convert_reduce_fusion
  8.4 1.3 bitcast_add_fusion.slot_ref
  9.7 0.1 convert_element_type.44
  9.8 0.1 copy.27
  9.9 0.1 pad.4
  10.0 1.0 copy.36.count_ref
  11.0 0.0 copy-done.1
  11.0 0.7 copy.47
  11.7 0.0 copy-done.6
  11.7 0.0 copy-done.5
  11.7 0.6 reshape.95.cent_ref
  12.4 0.0 copy-done.3
  12.4 0.0 copy-done.2
  12.4 0.9 copy_bitcast_fusion
  13.2 7.4 %shard_map.73 = bf16[64,112,256]{2,1,0:T(8,128)(2,1)} custom-call(s32[2,1,512]{2,1,0:T(1,128)} %bitcast_add_fusion.slot_ref, bf16[512,256]{1,0:T(8,128)(2,1)} %bitcast.45, bf16[512,256]{1,0:T(8,128)(2,1)} %get-tuple-element.6.k_ref, bf16[512,256]{1,0:T(8,128)(2,1)} %get-tuple-element.5.v_ref, bf16[8,256]{1,0:T(8,128)(2,1)} %reshape.95.cent_ref, ...), custom_call_target="tpu_custom_call" | custom-call | tf_op jit(solution)/shard_map/pallas_call | solution.py:45
  20.6 19.2 %all-to-all-start = ((bf16[64,112,256]{2,1,0:T(8,128)(2,1)}), bf16[64,112,256]{2,1,0:T(8,128)(2,1)}, u32[]{:S(2)}, u32[]{:S(2)}) async-start(bf16[64,112,256]{2,1,0:T(8,128)(2,1)} %shard_map.73), calls=%async_computation | async-start | bytes 7340032 | tf_op jit(solution)/shard_map/all_to_all | solution.py:161
  39.8 0.1 lt.55
  39.9 86.9 %all-to-all-done.q_ref.k_ref.v_ref = bf16[64,112,256]{2,1,0:T(8,128)(2,1)} async-done(((bf16[64,112,256]{2,1,0:T(8,128)(2,1)}), bf16[64,112,256]{2,1,0:T(8,128)(2,1)}, u32[]{:S(2)}, u32[]{:S(2)}) %all-to-all-start) | async-done | bytes 3670048 | tf_op jit(solution)/shard_map/all_to_all | solution.py:161
  126.7 1.0 slice.10
  127.7 0.1 reshape.97
  127.8 0.8 copy.29
  128.6 0.9 slice_convert_fusion
  129.5 0.1 copy.30
  129.6 0.1 lt.57
  129.7 0.2 lt.62
  129.9 0.6 compare_convert_fusion.valid_ref
  130.5 11.1 %shard_map.74 = bf16[64,32,256]{2,1,0:T(8,128)(2,1)} custom-call(bf16[64,112,256]{2,1,0:T(8,128)(2,1)} %all-to-all-done.q_ref.k_ref.v_ref, bf16[64,112,256]{2,1,0:T(8,128)(2,1)} %all-to-all-done.q_ref.k_ref.v_ref, bf16[64,112,256]{2,1,0:T(8,128)(2,1)} %all-to-all-done.q_ref.k_ref.v_ref, bf16[2,2,256,128]{3,2,1,0:T(8,128)(2,1)} %bitcast.42, ...), custom_call_target="tpu_custom_call" | custom-call | tf_op jit(solution)/shard_map/pallas_call | solution.py:105
  141.7 10.9 %all-to-all-start.1 = ((bf16[64,32,256]{2,1,0:T(8,128)(2,1)}), bf16[64,32,256]{2,1,0:T(8,128)(2,1)}, u32[]{:S(2)}, u32[]{:S(2)}) async-start(bf16[64,32,256]{2,1,0:T(8,128)(2,1)} %shard_map.74), calls=%async_computation.1 | async-start | bytes 2097152 | tf_op jit(solution)/shard_map/all_to_all | solution.py:175
  152.5 0.0 reduce-scatter.2.cloned.1.call-start
  152.6 0.0 copy-done.4
  152.6 0.1 copy.34
  152.8 0.2 reshape.102
  152.9 30.5 %all-to-all-done.1 = bf16[64,32,256]{2,1,0:T(8,128)(2,1)} async-done(((bf16[64,32,256]{2,1,0:T(8,128)(2,1)}), bf16[64,32,256]{2,1,0:T(8,128)(2,1)}, u32[]{:S(2)}, u32[]{:S(2)}) %all-to-all-start.1) | async-done | bytes 1048608 | tf_op jit(solution)/shard_map/all_to_all | solution.py:175
  183.4 1.3 reshape.99
  184.8 5.0 %gather_fusion = bf16[1024,128]{1,0:T(8,128)(2,1)S(1)} fusion(bf16[2048,2,128]{2,1,0:T(2,128)(2,1)S(1)} %reshape.99, s32[1024]{0:T(1024)S(1)} %reshape.102), kind=kCustom, calls=%fused_computation | custom fusion | bytes 532480 | tf_op jit(solution)/shard_map/gather | solution.py:177
  189.8 0.1 reshape.100
  189.9 0.0 copy-done
  189.9 3.2 %fusion = bf16[4096,512]{0,1:T(8,128)(2,1)} fusion(bf16[512,256]{1,0:T(8,128)(2,1)S(1)} %reshape.100, bf16[256,4096]{1,0:T(8,128)(2,1)S(1)} %copy-done), kind=kOutput, calls=%fused_computation.2 | convolution fusion | flops 1075838976 | bytes 6553600 | tf_op jit(solution)/shard_map/kc,tk->ct/dot_general | solution.py:181
  193.1 0.0 reduce-scatter.2.cloned.1.call-update
  193.1 53.6 %reduce-scatter.2.cloned.1.call-done = bf16[512,512]{0,1:T(8,128)(2,1)} async-done(((bf16[4096,512]{0,1:T(8,128)(2,1)}), bf16[512,512]{0,1:T(8,128)(2,1)}) %reduce-scatter.2.cloned.1.call-update) | async-done | bytes 524304 | tf_op jit(solution)/shard_map/reduce_scatter | solution.py:180
  246.7 2.0 copy.35
  (8 shorter events, 0.0 us)
Async XLA Ops:
  6.5 183.3 %copy-start = (bf16[256,4096]{1,0:T(8,128)(2,1)S(1)}, bf16[256,4096]{1,0:T(8,128)(2,1)}, u32[]{:S(2)}) copy-start(bf16[256,4096]{1,0:T(8,128)(2,1)} %param.13) | copy-start | bytes 6291460
  6.5 4.5 %copy-start.1 = (bf16[512,2,128]{2,1,0:T(2,128)(2,1)S(1)}, bf16[512,2,128]{2,1,0:T(2,128)(2,1)}, u32[]{:S(2)}) copy-start(bf16[512,2,128]{2,1,0:T(2,128)(2,1)} %param.7) | copy-start | bytes 786436
  6.5 5.2 %copy-start.6 = (bf16[2,4,128]{2,1,0:T(4,128)(2,1)S(1)}, bf16[2,4,128]{2,1,0:T(4,128)(2,1)}, u32[]{:S(2)}) copy-start(bf16[2,4,128]{2,1,0:T(4,128)(2,1)} %param.11) | copy-start | bytes 6148
  6.5 5.2 %copy-start.5 = (bf16[2,4,128]{2,1,0:T(4,128)(2,1)S(1)}, bf16[2,4,128]{2,1,0:T(4,128)(2,1)}, u32[]{:S(2)}) copy-start(bf16[2,4,128]{2,1,0:T(4,128)(2,1)} %param.12) | copy-start | bytes 6148
  6.5 5.8 %copy-start.3 = (bf16[512,2,128]{2,1,0:T(2,128)(2,1)S(1)}, bf16[512,2,128]{2,1,0:T(2,128)(2,1)}, u32[]{:S(2)}) copy-start(bf16[512,2,128]{2,1,0:T(2,128)(2,1)} %param.8) | copy-start | bytes 786436
  6.5 5.8 %copy-start.2 = (bf16[512,2,128]{2,1,0:T(2,128)(2,1)S(1)}, bf16[512,2,128]{2,1,0:T(2,128)(2,1)}, u32[]{:S(2)}) copy-start(bf16[512,2,128]{2,1,0:T(2,128)(2,1)} %param.9) | copy-start | bytes 786436
  20.6 106.2 %all-to-all-start = ((bf16[64,112,256]{2,1,0:T(8,128)(2,1)}), bf16[64,112,256]{2,1,0:T(8,128)(2,1)}, u32[]{:S(2)}, u32[]{:S(2)}) async-start(bf16[64,112,256]{2,1,0:T(8,128)(2,1)} %shard_map.73), calls=%async_computation | async-start | bytes 7340032 | tf_op jit(solution)/shard_map/all_to_all | solution.py:161
  141.7 10.9 %copy-start.4 = (s32[2,512,1]{1,2,0:T(1,128)S(1)}, s32[2,512,1]{1,2,0:T(1,128)}, u32[]{:S(2)}) copy-start(s32[2,512,1]{1,2,0:T(1,128)} %param.10) | copy-start | bytes 12292
  141.7 41.8 %all-to-all-start.1 = ((bf16[64,32,256]{2,1,0:T(8,128)(2,1)}), bf16[64,32,256]{2,1,0:T(8,128)(2,1)}, u32[]{:S(2)}, u32[]{:S(2)}) async-start(bf16[64,32,256]{2,1,0:T(8,128)(2,1)} %shard_map.74), calls=%async_computation.1 | async-start | bytes 2097152 | tf_op jit(solution)/shard_map/all_to_all | solution.py:175
  152.5 94.1 %reduce-scatter.2.cloned.1.call-start = ((), (), s32[]{:S(2)}) async-start(), calls=%async_computation.3 | async-start | bytes 4718592 | tf_op jit(solution)/shard_map/reduce_scatter | solution.py:180
Sparse Core Ops, SparseCore 0:
  193.2 53.3 reduce-scatter.1

commit v7 on v6

--- a/solution.py
+++ b/solution.py
@@ -4,10 +4,52 @@
 import jax.numpy as jnp
 from jax import lax
 from jax.experimental import pallas as pl
+from jax.experimental.pallas import tpu as pltpu
 from jax.sharding import PartitionSpec as P
 
 CLUSTERS = 256
 MOST = 8
+
+
+def project_kernel(slot_ref, back_ref, wt_ref, out_ref, att_ref):
+    tok_dev, heads_dev = slot_ref.shape
+    slots, width = back_ref.shape
+    head_dim = width // heads_dev
+
+    @pl.when(pl.program_id(0) == 0)
+    def _():
+        ids = lax.broadcasted_iota(jnp.int32, (tok_dev, slots), 1)
+        for h in range(heads_dev):
+            cols = slice(h * head_dim, (h + 1) * head_dim)
+            onehot = (slot_ref[:, h : h + 1] == ids).astype(back_ref.dtype)
+            att_ref[:, cols] = jnp.dot(
+                onehot, back_ref[:, cols], preferred_element_type=jnp.float32
+            ).astype(att_ref.dtype)
+
+    contract = (((1,), (1,)), ((), ()))
+    out_ref[...] = lax.dot_general(
+        wt_ref[...], att_ref[...], contract, preferred_element_type=jnp.float32
+    ).astype(out_ref.dtype)
+
+
+def project(slot_of, back, weight_t, steps):
+    tok_dev, heads_dev = slot_of.shape
+    slots, width = back.shape
+    features = weight_t.shape[0]
+    chunk = features // steps
+    return pl.pallas_call(
+        project_kernel,
+        grid=(steps,),
+        in_specs=[
+            pl.BlockSpec((tok_dev, heads_dev), lambda i: (0, 0)),
+            pl.BlockSpec((slots, width), lambda i: (0, 0)),
+            pl.BlockSpec((chunk, width), lambda i: (i, 0)),
+        ],
+        out_specs=pl.BlockSpec((chunk, tok_dev), lambda i: (i, 0)),
+        out_shape=jax.ShapeDtypeStruct((features, tok_dev), back.dtype),
+        scratch_shapes=[pltpu.VMEM((tok_dev, width), back.dtype)],
+        compiler_params=pltpu.CompilerParams(dimension_semantics=("arbitrary",)),
+    )(slot_of, back, weight_t)
 
 
 def place_kernel(slot_ref, q_ref, k_ref, v_ref, cent_ref, count_ref, out_ref, *, group):
@@ -173,18 +215,9 @@
 
     back = cluster_attention(recv, cent_in, valid, scale, per_owner, heads_dev)
     back = lax.all_to_all(back, "seq", split_axis=0, concat_axis=0, tiled=True)
-    back = back.reshape(owners * group, heads_dev, head_dim)
-    attended = back[slot_of, head_cols]
-
-    flat_out = attended.reshape(tok_dev, heads_dev * head_dim)
-    return lax.psum_scatter(
-        jnp.einsum("kc,tk->ct", out_weight, flat_out, preferred_element_type=jnp.float32).astype(
-            jnp.bfloat16
-        ),
-        "head",
-        scatter_dimension=0,
-        tiled=True,
-    )
+    back = back.reshape(owners * group, width)
+    mixed = project(slot_of, back, out_weight.T, 4)
+    return lax.psum_scatter(mixed, "head", scatter_dimension=0, tiled=True)
 
 
 def solution(mesh):

time: 257 us -> 254 us (0.988)
  Pallas kernels: 18.5 us -> 25.2 us
  waiting for transfers between devices: 171 us -> 166 us
  local copies, waits for them, and re-layouts: 15.4 us -> 12 us
  matrix products: 3.21 us -> 0 us
    pallas_call x0 -> x1, Pallas kernels: none -> 6.78 us  [project(): pl.pallas_call(project_kernel, grid=(steps,), in_specs=[pl.BlockSpec((tok...]
    gather x1 -> x0, local copies, waits for them, and re-layouts: 4.98 us -> none  [on_device(): attended = back[slot_of, head_cols]]
    all_to_all x1, waiting for transfers between devices: 30.5 us -> 26 us  [on_device(): back = lax.all_to_all(back, 'seq', split_axis=0, concat_axis=0, tiled=True)]
    unnamed x16 -> x11, local copies, waits for them, and re-layouts: 1.61 us -> 6.02 us
    dot_general x1 -> x0, matrix products: 3.21 us -> none  [on_device(): jnp.einsum('kc,tk->ct', out_weight, flat_out, preferred_element_type=jnp....]
  transfers between devices with their start and end apart: 3 -> 3, of which waited for: 3 -> 3; matrix products, arithmetic and copies ran while one was open for 0% -> 2% of each run, Pallas kernels for 0% -> 0%
where the time goes in v7:
time: 254 us; the launch traced here: 253 us
  waiting for transfers between devices  166 us (65%)
  starting transfers between devices  29.9 us (12%)
  Pallas kernels  25.2 us (10%)
  between operations  13.5 us (5%)
  local copies, waits for them, and re-layouts  12 us (5%)
  other arithmetic  6.24 us (2%)
    all_to_all x1, waiting for transfers between devices, on_device(): recv = lax.all_to_all(send, 'seq', split_axis=0, concat_axis=0, tiled=True)  86.8 us
    reduce_scatter x1, waiting for transfers between devices, on_device(): return lax.psum_scatter(mixed, 'head', scatter_dimension=0, tiled=True)  53.6 us
    all_to_all x1, waiting for transfers between devices, on_device(): back = lax.all_to_all(back, 'seq', split_axis=0, concat_axis=0, tiled=True)  26 us
    all_to_all x1, starting transfers between devices, on_device(): recv = lax.all_to_all(send, 'seq', split_axis=0, concat_axis=0, tiled=True)  19.2 us
    pallas_call x1, Pallas kernels, cluster_attention(): pl.pallas_call(functools.partial(attention_kernel, scale=scale), grid=(pe...  11.1 us
    all_to_all x1, starting transfers between devices, on_device(): back = lax.all_to_all(back, 'seq', split_axis=0, concat_axis=0, tiled=True)  10.7 us
    pallas_call x1, Pallas kernels, place(): pl.pallas_call(functools.partial(place_kernel, group=group), grid=(owners...  7.35 us
    pallas_call x1, Pallas kernels, project(): pl.pallas_call(project_kernel, grid=(steps,), in_specs=[pl.BlockSpec((tok...  6.78 us
  transfers between devices with their start and end apart: 3, of which 3 were waited for; matrix products, arithmetic and copies ran while one was open for 2% of the time, Pallas kernels for 0%

profile of v7, /device:TPU:6, one launch (start us, length us, event | category | flops | bytes accessed | tf_op | source)
XLA Modules:
  0.0 253.3 jit_solution(12021960233880780822)
XLA Ops:
  6.5 0.0 copy-start.2
  6.5 0.0 copy-start.3
  6.5 0.1 iota_compare_fusion.1
  6.6 0.9 copy.42
  7.5 0.1 copy.43
  7.6 0.2 convert_reduce_fusion.1
  7.9 0.7 convert_reduce_fusion
  8.6 1.3 bitcast_add_fusion.slot_ref
  9.8 1.7 copy.62
  11.5 0.7 pad_maximum_fusion
  12.2 0.6 reshape.89.cent_ref
  12.8 0.1 convert_element_type.38
  13.0 0.1 copy.47
  13.1 0.1 pad.4
  13.2 1.0 copy.55.count_ref
  14.1 0.0 copy-done.2
  14.1 0.0 copy-done.3
  14.1 0.9 copy_bitcast_fusion
  15.0 7.4 %shard_map.73 = bf16[64,112,256]{2,1,0:T(8,128)(2,1)} custom-call(s32[2,1,512]{2,1,0:T(1,128)} %bitcast_add_fusion.slot_ref, bf16[512,256]{1,0:T(8,128)(2,1)} %bitcast.37, bf16[512,256]{1,0:T(8,128)(2,1)} %get-tuple-element.6.k_ref, bf16[512,256]{1,0:T(8,128)(2,1)} %get-tuple-element.5.v_ref, bf16[8,256]{1,0:T(8,128)(2,1)} %reshape.89.cent_ref, ...), custom_call_target="tpu_custom_call" | custom-call | tf_op jit(solution)/shard_map/pallas_call | solution.py:87
  22.3 19.2 %all-to-all-start = ((bf16[64,112,256]{2,1,0:T(8,128)(2,1)}), bf16[64,112,256]{2,1,0:T(8,128)(2,1)}, u32[]{:S(2)}, u32[]{:S(2)}) async-start(bf16[64,112,256]{2,1,0:T(8,128)(2,1)} %shard_map.73), calls=%async_computation | async-start | bytes 7340032 | tf_op jit(solution)/shard_map/all_to_all | solution.py:203
  41.6 0.1 lt.48
  41.7 86.8 %all-to-all-done.q_ref.k_ref.v_ref = bf16[64,112,256]{2,1,0:T(8,128)(2,1)} async-done(((bf16[64,112,256]{2,1,0:T(8,128)(2,1)}), bf16[64,112,256]{2,1,0:T(8,128)(2,1)}, u32[]{:S(2)}, u32[]{:S(2)}) %all-to-all-start) | async-done | bytes 3670048 | tf_op jit(solution)/shard_map/all_to_all | solution.py:203
  128.5 1.0 slice.8
  129.5 0.1 reshape.91
  129.5 0.8 copy.49
  130.3 0.9 slice_convert_fusion
  131.3 0.1 copy.50
  131.3 0.1 lt.50
  131.5 0.2 lt.53
  131.7 0.6 compare_convert_fusion.valid_ref
  132.3 11.1 %shard_map.74 = bf16[64,32,256]{2,1,0:T(8,128)(2,1)} custom-call(bf16[64,112,256]{2,1,0:T(8,128)(2,1)} %all-to-all-done.q_ref.k_ref.v_ref, bf16[64,112,256]{2,1,0:T(8,128)(2,1)} %all-to-all-done.q_ref.k_ref.v_ref, bf16[64,112,256]{2,1,0:T(8,128)(2,1)} %all-to-all-done.q_ref.k_ref.v_ref, bf16[2,2,256,128]{3,2,1,0:T(8,128)(2,1)} %bitcast.33, ...), custom_call_target="tpu_custom_call" | custom-call | tf_op jit(solution)/shard_map/pallas_call | solution.py:147
  143.4 0.0 copy-start.1
  143.4 10.7 %all-to-all-start.1 = ((bf16[64,32,256]{2,1,0:T(8,128)(2,1)}), bf16[64,32,256]{2,1,0:T(8,128)(2,1)S(1)}, u32[]{:S(2)}, u32[]{:S(2)}) async-start(bf16[64,32,256]{2,1,0:T(8,128)(2,1)} %shard_map.74), calls=%async_computation.1 | async-start | bytes 2097152 | tf_op jit(solution)/shard_map/all_to_all | solution.py:217
  154.1 0.0 reduce-scatter.2.cloned.1.call-start
  154.1 0.9 copy.45
  155.0 0.0 copy-done.1
  155.0 2.4 copy.54
  157.4 1.7 add_bitcast_fusion.slot_ref
  159.1 26.0 %all-to-all-done.1 = bf16[64,32,256]{2,1,0:T(8,128)(2,1)S(1)} async-done(((bf16[64,32,256]{2,1,0:T(8,128)(2,1)}), bf16[64,32,256]{2,1,0:T(8,128)(2,1)S(1)}, u32[]{:S(2)}, u32[]{:S(2)}) %all-to-all-start.1) | async-done | bytes 1048608 | tf_op jit(solution)/shard_map/all_to_all | solution.py:217
  185.1 0.0 copy-start
  185.1 1.0 copy-done
  186.1 6.8 %shard_map.75 = bf16[4096,512]{1,0:T(8,128)(2,1)} custom-call(s32[512,2]{1,0:T(8,128)} %add_bitcast_fusion.slot_ref, bf16[2048,256]{1,0:T(8,128)(2,1)} %bitcast.32, bf16[4096,256]{1,0:T(8,128)(2,1)} %bitcast.31), custom_call_target="tpu_custom_call" | custom-call | tf_op jit(solution)/shard_map/pallas_call | solution.py:40
  192.9 0.0 reduce-scatter.2.cloned.1.call-update
  192.9 53.6 %reduce-scatter.2.cloned.1.call-done = bf16[512,512]{1,0:T(8,128)(2,1)} async-done(((bf16[4096,512]{1,0:T(8,128)(2,1)}), bf16[512,512]{1,0:T(8,128)(2,1)}) %reduce-scatter.2.cloned.1.call-update) | async-done | bytes 524304 | tf_op jit(solution)/shard_map/reduce_scatter | solution.py:220
  (3 shorter events, 0.0 us)
Async XLA Ops:
  6.5 7.6 %copy-start.2 = (bf16[512,2,128]{2,1,0:T(2,128)(2,1)S(1)}, bf16[512,2,128]{2,1,0:T(2,128)(2,1)}, u32[]{:S(2)}) copy-start(bf16[512,2,128]{2,1,0:T(2,128)(2,1)} %param.9) | copy-start | bytes 786436
  6.5 7.6 %copy-start.3 = (bf16[512,2,128]{2,1,0:T(2,128)(2,1)S(1)}, bf16[512,2,128]{2,1,0:T(2,128)(2,1)}, u32[]{:S(2)}) copy-start(bf16[512,2,128]{2,1,0:T(2,128)(2,1)} %param.8) | copy-start | bytes 786436
  22.3 106.2 %all-to-all-start = ((bf16[64,112,256]{2,1,0:T(8,128)(2,1)}), bf16[64,112,256]{2,1,0:T(8,128)(2,1)}, u32[]{:S(2)}, u32[]{:S(2)}) async-start(bf16[64,112,256]{2,1,0:T(8,128)(2,1)} %shard_map.73), calls=%async_computation | async-start | bytes 7340032 | tf_op jit(solution)/shard_map/all_to_all | solution.py:203
  143.4 11.6 %copy-start.1 = (bf16[256,4096]{1,0:T(8,128)(2,1)S(1)}, bf16[256,4096]{1,0:T(8,128)(2,1)}, u32[]{:S(2)}) copy-start(bf16[256,4096]{1,0:T(8,128)(2,1)} %param.13) | copy-start | bytes 6291460
  143.4 41.7 %all-to-all-start.1 = ((bf16[64,32,256]{2,1,0:T(8,128)(2,1)}), bf16[64,32,256]{2,1,0:T(8,128)(2,1)S(1)}, u32[]{:S(2)}, u32[]{:S(2)}) async-start(bf16[64,32,256]{2,1,0:T(8,128)(2,1)} %shard_map.74), calls=%async_computation.1 | async-start | bytes 2097152 | tf_op jit(solution)/shard_map/all_to_all | solution.py:217
  154.1 92.3 %reduce-scatter.2.cloned.1.call-start = ((), (), s32[]{:S(2)}) async-start(), calls=%async_computation.3 | async-start | bytes 4718592 | tf_op jit(solution)/shard_map/reduce_scatter | solution.py:220
  185.1 1.0 copy-start
Sparse Core Ops, SparseCore 0:
  193.0 53.3 reduce-scatter.1

commit v8 on v7

--- a/solution.py
+++ b/solution.py
@@ -113,22 +113,37 @@
     ck = ck_ref[0, 0]
     cv = cv_ref[0, 0]
     contract = (((1,), (1,)), ((), ()))
-    local = lax.dot_general(q, k, contract, preferred_element_type=jnp.float32) * scale
-    row = lax.broadcasted_iota(jnp.int32, (span, span), 0)
-    col = lax.broadcasted_iota(jnp.int32, (span, span), 1)
-    allowed = (col <= row) & (valid_ref[0, 0] > 0.5)
-    local = jnp.where(allowed, local, -1e30)
-    memory = lax.dot_general(q, ck, contract, preferred_element_type=jnp.float32) * scale
-    top = jnp.maximum(
-        jnp.max(local, axis=1, keepdims=True), jnp.max(memory, axis=1, keepdims=True)
-    )
-    w_local = jnp.exp(local - top)
-    w_memory = jnp.exp(memory - top)
-    denom = jnp.sum(w_local, axis=1, keepdims=True) + jnp.sum(w_memory, axis=1, keepdims=True)
-    numer = jnp.dot(w_local.astype(v.dtype), v, preferred_element_type=jnp.float32)
-    numer = numer + jnp.dot(w_memory.astype(cv.dtype), cv, preferred_element_type=jnp.float32)
-    result = (numer / denom).astype(out_ref.dtype).astype(jnp.float32)
-    out_ref[...] = result.reshape(sources, depth, head_dim).astype(out_ref.dtype)
+    memory_all = lax.dot_general(q, ck, contract, preferred_element_type=jnp.float32) * scale
+    valid = valid_ref[0, 0] > 0.5
+    rows = min(128, span)
+    for b in range(span // rows):
+        first = b * rows
+        seen = first + rows
+        local = (
+            lax.dot_general(q[first:seen], k[:seen], contract, preferred_element_type=jnp.float32)
+            * scale
+        )
+        row = lax.broadcasted_iota(jnp.int32, (rows, seen), 0) + first
+        col = lax.broadcasted_iota(jnp.int32, (rows, seen), 1)
+        allowed = (col <= row) & valid[:, :seen]
+        local = jnp.where(allowed, local, -1e30)
+        memory = memory_all[first:seen]
+        top = jnp.maximum(
+            jnp.max(local, axis=1, keepdims=True), jnp.max(memory, axis=1, keepdims=True)
+        )
+        w_local = jnp.exp(local - top)
+        w_memory = jnp.exp(memory - top)
+        denom = jnp.sum(w_local, axis=1, keepdims=True) + jnp.sum(
+            w_memory, axis=1, keepdims=True
+        )
+        numer = jnp.dot(w_local.astype(v.dtype), v[:seen], preferred_element_type=jnp.float32)
+        numer = numer + jnp.dot(
+            w_memory.astype(cv.dtype), cv, preferred_element_type=jnp.float32
+        )
+        result = (numer / denom).astype(out_ref.dtype).astype(jnp.float32)
+        out_ref[first // depth : seen // depth] = result.reshape(
+            rows // depth, depth, head_dim
+        ).astype(out_ref.dtype)
 
 
 def cluster_attention(recv, cent, valid, scale, per_owner, heads_dev):

time: 254 us -> 256 us (level)
  no operation moved by 1% of the time
where the time goes in v8:
time: 256 us; the launch traced here: 255 us
  waiting for transfers between devices  166 us (65%)
  starting transfers between devices  29.9 us (12%)
  Pallas kernels  26.9 us (11%)
  between operations  13.5 us (5%)
  local copies, waits for them, and re-layouts  12 us (5%)
  other arithmetic  6.24 us (2%)
    all_to_all x1, waiting for transfers between devices, on_device(): recv = lax.all_to_all(send, 'seq', split_axis=0, concat_axis=0, tiled=True)  86.8 us
    reduce_scatter x1, waiting for transfers between devices, on_device(): return lax.psum_scatter(mixed, 'head', scatter_dimension=0, tiled=True)  53.6 us
    all_to_all x1, waiting for transfers between devices, on_device(): back = lax.all_to_all(back, 'seq', split_axis=0, concat_axis=0, tiled=True)  26 us
    all_to_all x1, starting transfers between devices, on_device(): recv = lax.all_to_all(send, 'seq', split_axis=0, concat_axis=0, tiled=True)  19.2 us
    pallas_call x1, Pallas kernels, cluster_attention(): pl.pallas_call(functools.partial(attention_kernel, scale=scale), grid=(pe...  12.8 us
    all_to_all x1, starting transfers between devices, on_device(): back = lax.all_to_all(back, 'seq', split_axis=0, concat_axis=0, tiled=True)  10.7 us
    pallas_call x1, Pallas kernels, place(): pl.pallas_call(functools.partial(place_kernel, group=group), grid=(owners...  7.35 us
    pallas_call x1, Pallas kernels, project(): pl.pallas_call(project_kernel, grid=(steps,), in_specs=[pl.BlockSpec((tok...  6.78 us
  transfers between devices with their start and end apart: 3, of which 3 were waited for; matrix products, arithmetic and copies ran while one was open for 2% of the time, Pallas kernels for 0%

profile of v8, /device:TPU:6, one launch (start us, length us, event | category | flops | bytes accessed | tf_op | source)
XLA Modules:
  0.0 254.9 jit_solution(6083021093798142881)
XLA Ops:
  6.5 0.0 copy-start.2
  6.5 0.0 copy-start.3
  6.5 0.1 iota_compare_fusion.1
  6.6 0.9 copy.42
  7.5 0.1 copy.43
  7.6 0.2 convert_reduce_fusion.1
  7.9 0.7 convert_reduce_fusion
  8.6 1.3 bitcast_add_fusion.slot_ref
  9.8 1.7 copy.62
  11.5 0.7 pad_maximum_fusion
  12.2 0.6 reshape.89.cent_ref
  12.8 0.1 convert_element_type.38
  13.0 0.1 copy.47
  13.1 0.1 pad.4
  13.2 1.0 copy.55.count_ref
  14.1 0.0 copy-done.2
  14.1 0.0 copy-done.3
  14.1 0.9 copy_bitcast_fusion
  15.0 7.4 %shard_map.73 = bf16[64,112,256]{2,1,0:T(8,128)(2,1)} custom-call(s32[2,1,512]{2,1,0:T(1,128)} %bitcast_add_fusion.slot_ref, bf16[512,256]{1,0:T(8,128)(2,1)} %bitcast.37, bf16[512,256]{1,0:T(8,128)(2,1)} %get-tuple-element.6.k_ref, bf16[512,256]{1,0:T(8,128)(2,1)} %get-tuple-element.5.v_ref, bf16[8,256]{1,0:T(8,128)(2,1)} %reshape.89.cent_ref, ...), custom_call_target="tpu_custom_call" | custom-call | tf_op jit(solution)/shard_map/pallas_call | solution.py:87
  22.3 19.2 %all-to-all-start = ((bf16[64,112,256]{2,1,0:T(8,128)(2,1)}), bf16[64,112,256]{2,1,0:T(8,128)(2,1)}, u32[]{:S(2)}, u32[]{:S(2)}) async-start(bf16[64,112,256]{2,1,0:T(8,128)(2,1)} %shard_map.73), calls=%async_computation | async-start | bytes 7340032 | tf_op jit(solution)/shard_map/all_to_all | solution.py:218
  41.6 0.1 lt.48
  41.7 86.8 %all-to-all-done.q_ref.k_ref.v_ref = bf16[64,112,256]{2,1,0:T(8,128)(2,1)} async-done(((bf16[64,112,256]{2,1,0:T(8,128)(2,1)}), bf16[64,112,256]{2,1,0:T(8,128)(2,1)}, u32[]{:S(2)}, u32[]{:S(2)}) %all-to-all-start) | async-done | bytes 3670048 | tf_op jit(solution)/shard_map/all_to_all | solution.py:218
  128.5 1.0 slice.8
  129.5 0.1 reshape.91
  129.5 0.8 copy.49
  130.3 0.9 slice_convert_fusion
  131.3 0.1 copy.50
  131.3 0.1 lt.50
  131.5 0.2 lt.53
  131.7 0.6 compare_convert_fusion.valid_ref
  132.3 12.8 %shard_map.74 = bf16[64,32,256]{2,1,0:T(8,128)(2,1)} custom-call(bf16[64,112,256]{2,1,0:T(8,128)(2,1)} %all-to-all-done.q_ref.k_ref.v_ref, bf16[64,112,256]{2,1,0:T(8,128)(2,1)} %all-to-all-done.q_ref.k_ref.v_ref, bf16[64,112,256]{2,1,0:T(8,128)(2,1)} %all-to-all-done.q_ref.k_ref.v_ref, bf16[2,2,256,128]{3,2,1,0:T(8,128)(2,1)} %bitcast.33, ...), custom_call_target="tpu_custom_call" | custom-call | tf_op jit(solution)/shard_map/pallas_call | solution.py:162
  145.0 0.0 copy-start.1
  145.0 10.7 %all-to-all-start.1 = ((bf16[64,32,256]{2,1,0:T(8,128)(2,1)}), bf16[64,32,256]{2,1,0:T(8,128)(2,1)S(1)}, u32[]{:S(2)}, u32[]{:S(2)}) async-start(bf16[64,32,256]{2,1,0:T(8,128)(2,1)} %shard_map.74), calls=%async_computation.1 | async-start | bytes 2097152 | tf_op jit(solution)/shard_map/all_to_all | solution.py:232
  155.7 0.0 reduce-scatter.2.cloned.1.call-start
  155.8 0.9 copy.45
  156.6 0.0 copy-done.1
  156.7 2.4 copy.54
  159.1 1.7 add_bitcast_fusion.slot_ref
  160.8 26.0 %all-to-all-done.1 = bf16[64,32,256]{2,1,0:T(8,128)(2,1)S(1)} async-done(((bf16[64,32,256]{2,1,0:T(8,128)(2,1)}), bf16[64,32,256]{2,1,0:T(8,128)(2,1)S(1)}, u32[]{:S(2)}, u32[]{:S(2)}) %all-to-all-start.1) | async-done | bytes 1048608 | tf_op jit(solution)/shard_map/all_to_all | solution.py:232
  186.7 0.0 copy-start
  186.7 1.0 copy-done
  187.7 6.8 %shard_map.75 = bf16[4096,512]{1,0:T(8,128)(2,1)} custom-call(s32[512,2]{1,0:T(8,128)} %add_bitcast_fusion.slot_ref, bf16[2048,256]{1,0:T(8,128)(2,1)} %bitcast.32, bf16[4096,256]{1,0:T(8,128)(2,1)} %bitcast.31), custom_call_target="tpu_custom_call" | custom-call | tf_op jit(solution)/shard_map/pallas_call | solution.py:40
  194.5 0.0 reduce-scatter.2.cloned.1.call-update
  194.5 53.6 %reduce-scatter.2.cloned.1.call-done = bf16[512,512]{1,0:T(8,128)(2,1)} async-done(((bf16[4096,512]{1,0:T(8,128)(2,1)}), bf16[512,512]{1,0:T(8,128)(2,1)}) %reduce-scatter.2.cloned.1.call-update) | async-done | bytes 524304 | tf_op jit(solution)/shard_map/reduce_scatter | solution.py:235
  (3 shorter events, 0.0 us)
Async XLA Ops:
  6.5 7.6 %copy-start.2 = (bf16[512,2,128]{2,1,0:T(2,128)(2,1)S(1)}, bf16[512,2,128]{2,1,0:T(2,128)(2,1)}, u32[]{:S(2)}) copy-start(bf16[512,2,128]{2,1,0:T(2,128)(2,1)} %param.9) | copy-start | bytes 786436
  6.5 7.6 %copy-start.3 = (bf16[512,2,128]{2,1,0:T(2,128)(2,1)S(1)}, bf16[512,2,128]{2,1,0:T(2,128)(2,1)}, u32[]{:S(2)}) copy-start(bf16[512,2,128]{2,1,0:T(2,128)(2,1)} %param.8) | copy-start | bytes 786436
  22.3 106.2 %all-to-all-start = ((bf16[64,112,256]{2,1,0:T(8,128)(2,1)}), bf16[64,112,256]{2,1,0:T(8,128)(2,1)}, u32[]{:S(2)}, u32[]{:S(2)}) async-start(bf16[64,112,256]{2,1,0:T(8,128)(2,1)} %shard_map.73), calls=%async_computation | async-start | bytes 7340032 | tf_op jit(solution)/shard_map/all_to_all | solution.py:218
  145.0 11.6 %copy-start.1 = (bf16[256,4096]{1,0:T(8,128)(2,1)S(1)}, bf16[256,4096]{1,0:T(8,128)(2,1)}, u32[]{:S(2)}) copy-start(bf16[256,4096]{1,0:T(8,128)(2,1)} %param.13) | copy-start | bytes 6291460
  145.0 41.7 %all-to-all-start.1 = ((bf16[64,32,256]{2,1,0:T(8,128)(2,1)}), bf16[64,32,256]{2,1,0:T(8,128)(2,1)S(1)}, u32[]{:S(2)}, u32[]{:S(2)}) async-start(bf16[64,32,256]{2,1,0:T(8,128)(2,1)} %shard_map.74), calls=%async_computation.1 | async-start | bytes 2097152 | tf_op jit(solution)/shard_map/all_to_all | solution.py:232
  155.7 92.4 %reduce-scatter.2.cloned.1.call-start = ((), (), s32[]{:S(2)}) async-start(), calls=%async_computation.3 | async-start | bytes 4718592 | tf_op jit(solution)/shard_map/reduce_scatter | solution.py:235
  186.7 1.0 copy-start
Sparse Core Ops, SparseCore 0:
  194.7 53.3 reduce-scatter.1

commit v9 on v8

--- a/solution.py
+++ b/solution.py
@@ -101,33 +101,31 @@
 
 
 def attention_kernel(q_ref, k_ref, v_ref, ck_ref, cv_ref, valid_ref, out_ref, *, scale):
-    sources, depth, head_dim = q_ref.shape
+    sources, depth, width = q_ref.shape
+    heads_dev = ck_ref.shape[1]
+    head_dim = width // heads_dev
     span = sources * depth
 
     def flat(ref):
-        return ref[...].astype(jnp.float32).reshape(span, head_dim).astype(ref.dtype)
-
-    q = flat(q_ref)
-    k = flat(k_ref)
-    v = flat(v_ref)
-    ck = ck_ref[0, 0]
-    cv = cv_ref[0, 0]
+        return ref[...].astype(jnp.float32).reshape(span, width).astype(ref.dtype)
+
+    q_all = flat(q_ref)
+    k_all = flat(k_ref)
+    v_all = flat(v_ref)
     contract = (((1,), (1,)), ((), ()))
-    memory_all = lax.dot_general(q, ck, contract, preferred_element_type=jnp.float32) * scale
-    valid = valid_ref[0, 0] > 0.5
-    rows = min(128, span)
-    for b in range(span // rows):
-        first = b * rows
-        seen = first + rows
-        local = (
-            lax.dot_general(q[first:seen], k[:seen], contract, preferred_element_type=jnp.float32)
-            * scale
-        )
-        row = lax.broadcasted_iota(jnp.int32, (rows, seen), 0) + first
-        col = lax.broadcasted_iota(jnp.int32, (rows, seen), 1)
-        allowed = (col <= row) & valid[:, :seen]
+    row = lax.broadcasted_iota(jnp.int32, (span, span), 0)
+    col = lax.broadcasted_iota(jnp.int32, (span, span), 1)
+    for h in range(heads_dev):
+        cols = slice(h * head_dim, (h + 1) * head_dim)
+        q = q_all[:, cols]
+        k = k_all[:, cols]
+        v = v_all[:, cols]
+        ck = ck_ref[0, h]
+        cv = cv_ref[0, h]
+        local = lax.dot_general(q, k, contract, preferred_element_type=jnp.float32) * scale
+        allowed = (col <= row) & (valid_ref[0, h] > 0.5)
         local = jnp.where(allowed, local, -1e30)
-        memory = memory_all[first:seen]
+        memory = lax.dot_general(q, ck, contract, preferred_element_type=jnp.float32) * scale
         top = jnp.maximum(
             jnp.max(local, axis=1, keepdims=True), jnp.max(memory, axis=1, keepdims=True)
         )
@@ -136,14 +134,12 @@
         denom = jnp.sum(w_local, axis=1, keepdims=True) + jnp.sum(
             w_memory, axis=1, keepdims=True
         )
-        numer = jnp.dot(w_local.astype(v.dtype), v[:seen], preferred_element_type=jnp.float32)
+        numer = jnp.dot(w_local.astype(v.dtype), v, preferred_element_type=jnp.float32)
         numer = numer + jnp.dot(
             w_memory.astype(cv.dtype), cv, preferred_element_type=jnp.float32
         )
         result = (numer / denom).astype(out_ref.dtype).astype(jnp.float32)
-        out_ref[first // depth : seen // depth] = result.reshape(
-            rows // depth, depth, head_dim
-        ).astype(out_ref.dtype)
+        out_ref[:, :, cols] = result.reshape(sources, depth, head_dim).astype(out_ref.dtype)
 
 
 def cluster_attention(recv, cent, valid, scale, per_owner, heads_dev):
@@ -152,25 +148,23 @@
     clusters = cent.shape[2]
 
     def pick(kind):
-        return pl.BlockSpec(
-            (sources, MOST, head_dim), lambda c, h: (0, kind * per_owner + c, h)
-        )
+        return pl.BlockSpec((sources, MOST, width), lambda c: (0, kind * per_owner + c, 0))
 
     def centroid(kind):
-        return pl.BlockSpec((1, 1, clusters, head_dim), lambda c, h: (kind, h, 0, 0))
+        return pl.BlockSpec((1, heads_dev, clusters, head_dim), lambda c: (kind, 0, 0, 0))
 
     return pl.pallas_call(
         functools.partial(attention_kernel, scale=scale),
-        grid=(per_owner, heads_dev),
+        grid=(per_owner,),
         in_specs=[
             pick(0),
             pick(1),
             pick(2),
             centroid(0),
             centroid(1),
-            pl.BlockSpec((1, 1, 1, sources * MOST), lambda c, h: (c, h, 0, 0)),
+            pl.BlockSpec((1, heads_dev, 1, sources * MOST), lambda c: (c, 0, 0, 0)),
         ],
-        out_specs=pl.BlockSpec((sources, MOST, head_dim), lambda c, h: (0, c, h)),
+        out_specs=pl.BlockSpec((sources, MOST, width), lambda c: (0, c, 0)),
         out_shape=jax.ShapeDtypeStruct((sources, per_owner * MOST, width), recv.dtype),
     )(recv, recv, recv, cent, cent, valid)
 

time: 256 us -> 252 us (0.984)
  Pallas kernels: 26.9 us -> 22.7 us
    pallas_call x1, Pallas kernels: 12.8 us -> 8.53 us  [cluster_attention(): pl.pallas_call(functools.partial(attention_kernel, scale=scale), grid=(pe...]
where the time goes in v9:
time: 252 us; the launch traced here: 251 us
  waiting for transfers between devices  166 us (66%)
  starting transfers between devices  29.9 us (12%)
  Pallas kernels  22.7 us (9%)
  between operations  13.5 us (5%)
  local copies, waits for them, and re-layouts  12 us (5%)
  other arithmetic  6.24 us (2%)
    all_to_all x1, waiting for transfers between devices, on_device(): recv = lax.all_to_all(send, 'seq', split_axis=0, concat_axis=0, tiled=True)  86.8 us
    reduce_scatter x1, waiting for transfers between devices, on_device(): return lax.psum_scatter(mixed, 'head', scatter_dimension=0, tiled=True)  53.6 us
    all_to_all x1, waiting for transfers between devices, on_device(): back = lax.all_to_all(back, 'seq', split_axis=0, concat_axis=0, tiled=True)  25.9 us
    all_to_all x1, starting transfers between devices, on_device(): recv = lax.all_to_all(send, 'seq', split_axis=0, concat_axis=0, tiled=True)  19.2 us
    all_to_all x1, starting transfers between devices, on_device(): back = lax.all_to_all(back, 'seq', split_axis=0, concat_axis=0, tiled=True)  10.7 us
    pallas_call x1, Pallas kernels, cluster_attention(): pl.pallas_call(functools.partial(attention_kernel, scale=scale), grid=(pe...  8.53 us
    pallas_call x1, Pallas kernels, place(): pl.pallas_call(functools.partial(place_kernel, group=group), grid=(owners...  7.35 us
    pallas_call x1, Pallas kernels, project(): pl.pallas_call(project_kernel, grid=(steps,), in_specs=[pl.BlockSpec((tok...  6.78 us
  transfers between devices with their start and end apart: 3, of which 3 were waited for; matrix products, arithmetic and copies ran while one was open for 2% of the time, Pallas kernels for 0%

profile of v9, /device:TPU:6, one launch (start us, length us, event | category | flops | bytes accessed | tf_op | source)
XLA Modules:
  0.0 250.7 jit_solution(15001660121906088698)
XLA Ops:
  6.5 0.0 copy-start.2
  6.5 0.0 copy-start.3
  6.5 0.1 iota_compare_fusion.1
  6.6 0.9 copy.42
  7.5 0.1 copy.43
  7.6 0.2 convert_reduce_fusion.1
  7.9 0.7 convert_reduce_fusion
  8.6 1.3 bitcast_add_fusion.slot_ref
  9.8 1.7 copy.62
  11.5 0.7 pad_maximum_fusion
  12.2 0.6 reshape.89.cent_ref
  12.8 0.1 convert_element_type.38
  13.0 0.1 copy.47
  13.1 0.1 pad.4
  13.2 1.0 copy.55.count_ref
  14.1 0.0 copy-done.2
  14.1 0.0 copy-done.3
  14.1 0.9 copy_bitcast_fusion
  15.0 7.4 %shard_map.73 = bf16[64,112,256]{2,1,0:T(8,128)(2,1)} custom-call(s32[2,1,512]{2,1,0:T(1,128)} %bitcast_add_fusion.slot_ref, bf16[512,256]{1,0:T(8,128)(2,1)} %bitcast.37, bf16[512,256]{1,0:T(8,128)(2,1)} %get-tuple-element.6.k_ref, bf16[512,256]{1,0:T(8,128)(2,1)} %get-tuple-element.5.v_ref, bf16[8,256]{1,0:T(8,128)(2,1)} %reshape.89.cent_ref, ...), custom_call_target="tpu_custom_call" | custom-call | tf_op jit(solution)/shard_map/pallas_call | solution.py:87
  22.3 19.2 %all-to-all-start = ((bf16[64,112,256]{2,1,0:T(8,128)(2,1)}), bf16[64,112,256]{2,1,0:T(8,128)(2,1)}, u32[]{:S(2)}, u32[]{:S(2)}) async-start(bf16[64,112,256]{2,1,0:T(8,128)(2,1)} %shard_map.73), calls=%async_computation | async-start | bytes 7340032 | tf_op jit(solution)/shard_map/all_to_all | solution.py:212
  41.6 0.1 lt.48
  41.7 86.8 %all-to-all-done.q_ref.k_ref.v_ref = bf16[64,112,256]{2,1,0:T(8,128)(2,1)} async-done(((bf16[64,112,256]{2,1,0:T(8,128)(2,1)}), bf16[64,112,256]{2,1,0:T(8,128)(2,1)}, u32[]{:S(2)}, u32[]{:S(2)}) %all-to-all-start) | async-done | bytes 3670048 | tf_op jit(solution)/shard_map/all_to_all | solution.py:212
  128.5 1.0 slice.8
  129.5 0.1 reshape.91
  129.5 0.8 copy.49
  130.3 0.9 slice_convert_fusion
  131.3 0.1 copy.50
  131.3 0.1 lt.50
  131.5 0.2 lt.53
  131.7 0.6 compare_convert_fusion.valid_ref
  132.3 8.5 %shard_map.74 = bf16[64,32,256]{2,1,0:T(8,128)(2,1)} custom-call(bf16[64,112,256]{2,1,0:T(8,128)(2,1)} %all-to-all-done.q_ref.k_ref.v_ref, bf16[64,112,256]{2,1,0:T(8,128)(2,1)} %all-to-all-done.q_ref.k_ref.v_ref, bf16[64,112,256]{2,1,0:T(8,128)(2,1)} %all-to-all-done.q_ref.k_ref.v_ref, bf16[2,2,256,128]{3,2,1,0:T(8,128)(2,1)} %bitcast.33, ...), custom_call_target="tpu_custom_call" | custom-call | tf_op jit(solution)/shard_map/pallas_call | solution.py:156
  140.8 0.0 copy-start.1
  140.8 10.7 %all-to-all-start.1 = ((bf16[64,32,256]{2,1,0:T(8,128)(2,1)}), bf16[64,32,256]{2,1,0:T(8,128)(2,1)S(1)}, u32[]{:S(2)}, u32[]{:S(2)}) async-start(bf16[64,32,256]{2,1,0:T(8,128)(2,1)} %shard_map.74), calls=%async_computation.1 | async-start | bytes 2097152 | tf_op jit(solution)/shard_map/all_to_all | solution.py:226
  151.5 0.0 reduce-scatter.2.cloned.1.call-start
  151.6 0.9 copy.45
  152.4 0.0 copy-done.1
  152.4 2.4 copy.54
  154.9 1.7 add_bitcast_fusion.slot_ref
  156.5 25.9 %all-to-all-done.1 = bf16[64,32,256]{2,1,0:T(8,128)(2,1)S(1)} async-done(((bf16[64,32,256]{2,1,0:T(8,128)(2,1)}), bf16[64,32,256]{2,1,0:T(8,128)(2,1)S(1)}, u32[]{:S(2)}, u32[]{:S(2)}) %all-to-all-start.1) | async-done | bytes 1048608 | tf_op jit(solution)/shard_map/all_to_all | solution.py:226
  182.5 0.0 copy-start
  182.5 1.0 copy-done
  183.5 6.8 %shard_map.75 = bf16[4096,512]{1,0:T(8,128)(2,1)} custom-call(s32[512,2]{1,0:T(8,128)} %add_bitcast_fusion.slot_ref, bf16[2048,256]{1,0:T(8,128)(2,1)} %bitcast.32, bf16[4096,256]{1,0:T(8,128)(2,1)} %bitcast.31), custom_call_target="tpu_custom_call" | custom-call | tf_op jit(solution)/shard_map/pallas_call | solution.py:40
  190.3 0.0 reduce-scatter.2.cloned.1.call-update
  190.3 53.6 %reduce-scatter.2.cloned.1.call-done = bf16[512,512]{1,0:T(8,128)(2,1)} async-done(((bf16[4096,512]{1,0:T(8,128)(2,1)}), bf16[512,512]{1,0:T(8,128)(2,1)}) %reduce-scatter.2.cloned.1.call-update) | async-done | bytes 524304 | tf_op jit(solution)/shard_map/reduce_scatter | solution.py:229
  (3 shorter events, 0.0 us)
Async XLA Ops:
  6.5 7.6 %copy-start.2 = (bf16[512,2,128]{2,1,0:T(2,128)(2,1)S(1)}, bf16[512,2,128]{2,1,0:T(2,128)(2,1)}, u32[]{:S(2)}) copy-start(bf16[512,2,128]{2,1,0:T(2,128)(2,1)} %param.9) | copy-start | bytes 786436
  6.5 7.6 %copy-start.3 = (bf16[512,2,128]{2,1,0:T(2,128)(2,1)S(1)}, bf16[512,2,128]{2,1,0:T(2,128)(2,1)}, u32[]{:S(2)}) copy-start(bf16[512,2,128]{2,1,0:T(2,128)(2,1)} %param.8) | copy-start | bytes 786436
  22.3 106.2 %all-to-all-start = ((bf16[64,112,256]{2,1,0:T(8,128)(2,1)}), bf16[64,112,256]{2,1,0:T(8,128)(2,1)}, u32[]{:S(2)}, u32[]{:S(2)}) async-start(bf16[64,112,256]{2,1,0:T(8,128)(2,1)} %shard_map.73), calls=%async_computation | async-start | bytes 7340032 | tf_op jit(solution)/shard_map/all_to_all | solution.py:212
  140.8 11.6 %copy-start.1 = (bf16[256,4096]{1,0:T(8,128)(2,1)S(1)}, bf16[256,4096]{1,0:T(8,128)(2,1)}, u32[]{:S(2)}) copy-start(bf16[256,4096]{1,0:T(8,128)(2,1)} %param.13) | copy-start | bytes 6291460
  140.8 41.7 %all-to-all-start.1 = ((bf16[64,32,256]{2,1,0:T(8,128)(2,1)}), bf16[64,32,256]{2,1,0:T(8,128)(2,1)S(1)}, u32[]{:S(2)}, u32[]{:S(2)}) async-start(bf16[64,32,256]{2,1,0:T(8,128)(2,1)} %shard_map.74), calls=%async_computation.1 | async-start | bytes 2097152 | tf_op jit(solution)/shard_map/all_to_all | solution.py:226
  151.5 92.3 %reduce-scatter.2.cloned.1.call-start = ((), (), s32[]{:S(2)}) async-start(), calls=%async_computation.3 | async-start | bytes 4718592 | tf_op jit(solution)/shard_map/reduce_scatter | solution.py:229
  182.5 1.0 copy-start
Sparse Core Ops, SparseCore 0:
  190.4 53.3 reduce-scatter.1

commit v10 on v9

--- a/solution.py
+++ b/solution.py
@@ -207,7 +207,7 @@
         cent,
         counts,
         group,
-        min(8, owners),
+        min(16, owners),
     )
     recv = lax.all_to_all(send, "seq", split_axis=0, concat_axis=0, tiled=True)
 

time: 252 us -> 250 us (level)
  no operation moved by 1% of the time
where the time goes in v10:
time: 250 us; the launch traced here: 249 us
  waiting for transfers between devices  166 us (66%)
  starting transfers between devices  29.9 us (12%)
  Pallas kernels  21.4 us (9%)
  between operations  13.5 us (5%)
  local copies, waits for them, and re-layouts  12 us (5%)
  other arithmetic  6.24 us (2%)
    all_to_all x1, waiting for transfers between devices, on_device(): recv = lax.all_to_all(send, 'seq', split_axis=0, concat_axis=0, tiled=True)  86.8 us
    reduce_scatter x1, waiting for transfers between devices, on_device(): return lax.psum_scatter(mixed, 'head', scatter_dimension=0, tiled=True)  53.6 us
    all_to_all x1, waiting for transfers between devices, on_device(): back = lax.all_to_all(back, 'seq', split_axis=0, concat_axis=0, tiled=True)  25.9 us
    all_to_all x1, starting transfers between devices, on_device(): recv = lax.all_to_all(send, 'seq', split_axis=0, concat_axis=0, tiled=True)  19.2 us
    all_to_all x1, starting transfers between devices, on_device(): back = lax.all_to_all(back, 'seq', split_axis=0, concat_axis=0, tiled=True)  10.7 us
    pallas_call x1, Pallas kernels, cluster_attention(): pl.pallas_call(functools.partial(attention_kernel, scale=scale), grid=(pe...  8.53 us
    pallas_call x1, Pallas kernels, project(): pl.pallas_call(project_kernel, grid=(steps,), in_specs=[pl.BlockSpec((tok...  6.78 us
    pallas_call x1, Pallas kernels, place(): pl.pallas_call(functools.partial(place_kernel, group=group), grid=(owners...  6.13 us
  transfers between devices with their start and end apart: 3, of which 3 were waited for; matrix products, arithmetic and copies ran while one was open for 2% of the time, Pallas kernels for 0%

profile of v10, /device:TPU:6, one launch (start us, length us, event | category | flops | bytes accessed | tf_op | source)
XLA Modules:
  0.0 249.5 jit_solution(15803728274264808669)
XLA Ops:
  6.5 0.0 copy-start.2
  6.5 0.0 copy-start.3
  6.5 0.1 iota_compare_fusion.1
  6.6 0.9 copy.42
  7.5 0.1 copy.43
  7.6 0.2 convert_reduce_fusion.1
  7.9 0.7 convert_reduce_fusion
  8.6 1.3 bitcast_add_fusion.slot_ref
  9.8 1.7 copy.62
  11.5 0.7 pad_maximum_fusion
  12.2 0.6 reshape.89.cent_ref
  12.8 0.1 convert_element_type.38
  13.0 0.1 copy.47
  13.1 0.1 pad.4
  13.2 1.0 copy.55.count_ref
  14.1 0.0 copy-done.2
  14.1 0.0 copy-done.3
  14.1 0.9 copy_bitcast_fusion
  15.0 6.1 %shard_map.73 = bf16[64,112,256]{2,1,0:T(8,128)(2,1)} custom-call(s32[2,1,512]{2,1,0:T(1,128)} %bitcast_add_fusion.slot_ref, bf16[512,256]{1,0:T(8,128)(2,1)} %bitcast.37, bf16[512,256]{1,0:T(8,128)(2,1)} %get-tuple-element.6.k_ref, bf16[512,256]{1,0:T(8,128)(2,1)} %get-tuple-element.5.v_ref, bf16[8,256]{1,0:T(8,128)(2,1)} %reshape.89.cent_ref, ...), custom_call_target="tpu_custom_call" | custom-call | tf_op jit(solution)/shard_map/pallas_call | solution.py:87
  21.1 19.2 %all-to-all-start = ((bf16[64,112,256]{2,1,0:T(8,128)(2,1)}), bf16[64,112,256]{2,1,0:T(8,128)(2,1)}, u32[]{:S(2)}, u32[]{:S(2)}) async-start(bf16[64,112,256]{2,1,0:T(8,128)(2,1)} %shard_map.73), calls=%async_computation | async-start | bytes 7340032 | tf_op jit(solution)/shard_map/all_to_all | solution.py:212
  40.3 0.1 lt.48
  40.4 86.8 %all-to-all-done.q_ref.k_ref.v_ref = bf16[64,112,256]{2,1,0:T(8,128)(2,1)} async-done(((bf16[64,112,256]{2,1,0:T(8,128)(2,1)}), bf16[64,112,256]{2,1,0:T(8,128)(2,1)}, u32[]{:S(2)}, u32[]{:S(2)}) %all-to-all-start) | async-done | bytes 3670048 | tf_op jit(solution)/shard_map/all_to_all | solution.py:212
  127.3 1.0 slice.8
  128.3 0.1 reshape.91
  128.3 0.8 copy.49
  129.1 0.9 slice_convert_fusion
  130.1 0.1 copy.50
  130.1 0.1 lt.50
  130.3 0.2 lt.53
  130.4 0.6 compare_convert_fusion.valid_ref
  131.1 8.5 %shard_map.74 = bf16[64,32,256]{2,1,0:T(8,128)(2,1)} custom-call(bf16[64,112,256]{2,1,0:T(8,128)(2,1)} %all-to-all-done.q_ref.k_ref.v_ref, bf16[64,112,256]{2,1,0:T(8,128)(2,1)} %all-to-all-done.q_ref.k_ref.v_ref, bf16[64,112,256]{2,1,0:T(8,128)(2,1)} %all-to-all-done.q_ref.k_ref.v_ref, bf16[2,2,256,128]{3,2,1,0:T(8,128)(2,1)} %bitcast.33, ...), custom_call_target="tpu_custom_call" | custom-call | tf_op jit(solution)/shard_map/pallas_call | solution.py:156
  139.6 0.0 copy-start.1
  139.6 10.7 %all-to-all-start.1 = ((bf16[64,32,256]{2,1,0:T(8,128)(2,1)}), bf16[64,32,256]{2,1,0:T(8,128)(2,1)S(1)}, u32[]{:S(2)}, u32[]{:S(2)}) async-start(bf16[64,32,256]{2,1,0:T(8,128)(2,1)} %shard_map.74), calls=%async_computation.1 | async-start | bytes 2097152 | tf_op jit(solution)/shard_map/all_to_all | solution.py:226
  150.3 0.0 reduce-scatter.2.cloned.1.call-start
  150.3 0.9 copy.45
  151.2 0.0 copy-done.1
  151.2 2.4 copy.54
  153.6 1.7 add_bitcast_fusion.slot_ref
  155.3 25.9 %all-to-all-done.1 = bf16[64,32,256]{2,1,0:T(8,128)(2,1)S(1)} async-done(((bf16[64,32,256]{2,1,0:T(8,128)(2,1)}), bf16[64,32,256]{2,1,0:T(8,128)(2,1)S(1)}, u32[]{:S(2)}, u32[]{:S(2)}) %all-to-all-start.1) | async-done | bytes 1048608 | tf_op jit(solution)/shard_map/all_to_all | solution.py:226
  181.2 0.0 copy-start
  181.2 1.0 copy-done
  182.2 6.8 %shard_map.75 = bf16[4096,512]{1,0:T(8,128)(2,1)} custom-call(s32[512,2]{1,0:T(8,128)} %add_bitcast_fusion.slot_ref, bf16[2048,256]{1,0:T(8,128)(2,1)} %bitcast.32, bf16[4096,256]{1,0:T(8,128)(2,1)} %bitcast.31), custom_call_target="tpu_custom_call" | custom-call | tf_op jit(solution)/shard_map/pallas_call | solution.py:40
  189.0 0.0 reduce-scatter.2.cloned.1.call-update
  189.0 53.6 %reduce-scatter.2.cloned.1.call-done = bf16[512,512]{1,0:T(8,128)(2,1)} async-done(((bf16[4096,512]{1,0:T(8,128)(2,1)}), bf16[512,512]{1,0:T(8,128)(2,1)}) %reduce-scatter.2.cloned.1.call-update) | async-done | bytes 524304 | tf_op jit(solution)/shard_map/reduce_scatter | solution.py:229
  (3 shorter events, 0.0 us)
Async XLA Ops:
  6.5 7.6 %copy-start.2 = (bf16[512,2,128]{2,1,0:T(2,128)(2,1)S(1)}, bf16[512,2,128]{2,1,0:T(2,128)(2,1)}, u32[]{:S(2)}) copy-start(bf16[512,2,128]{2,1,0:T(2,128)(2,1)} %param.9) | copy-start | bytes 786436
  6.5 7.6 %copy-start.3 = (bf16[512,2,128]{2,1,0:T(2,128)(2,1)S(1)}, bf16[512,2,128]{2,1,0:T(2,128)(2,1)}, u32[]{:S(2)}) copy-start(bf16[512,2,128]{2,1,0:T(2,128)(2,1)} %param.8) | copy-start | bytes 786436
  21.1 106.2 %all-to-all-start = ((bf16[64,112,256]{2,1,0:T(8,128)(2,1)}), bf16[64,112,256]{2,1,0:T(8,128)(2,1)}, u32[]{:S(2)}, u32[]{:S(2)}) async-start(bf16[64,112,256]{2,1,0:T(8,128)(2,1)} %shard_map.73), calls=%async_computation | async-start | bytes 7340032 | tf_op jit(solution)/shard_map/all_to_all | solution.py:212
  139.6 11.6 %copy-start.1 = (bf16[256,4096]{1,0:T(8,128)(2,1)S(1)}, bf16[256,4096]{1,0:T(8,128)(2,1)}, u32[]{:S(2)}) copy-start(bf16[256,4096]{1,0:T(8,128)(2,1)} %param.13) | copy-start | bytes 6291460
  139.6 41.6 %all-to-all-start.1 = ((bf16[64,32,256]{2,1,0:T(8,128)(2,1)}), bf16[64,32,256]{2,1,0:T(8,128)(2,1)S(1)}, u32[]{:S(2)}, u32[]{:S(2)}) async-start(bf16[64,32,256]{2,1,0:T(8,128)(2,1)} %shard_map.74), calls=%async_computation.1 | async-start | bytes 2097152 | tf_op jit(solution)/shard_map/all_to_all | solution.py:226
  150.3 92.4 %reduce-scatter.2.cloned.1.call-start = ((), (), s32[]{:S(2)}) async-start(), calls=%async_computation.3 | async-start | bytes 4718592 | tf_op jit(solution)/shard_map/reduce_scatter | solution.py:229
  181.2 1.0 copy-start
Sparse Core Ops, SparseCore 0:
  189.2 53.4 reduce-scatter.1

commit v11 on v10

--- a/solution.py
+++ b/solution.py
@@ -207,7 +207,7 @@
         cent,
         counts,
         group,
-        min(16, owners),
+        min(32, owners),
     )
     recv = lax.all_to_all(send, "seq", split_axis=0, concat_axis=0, tiled=True)
 

time: 250 us -> 250 us (level)
  no operation moved by 1% of the time
where the time goes in v11:
time: 250 us; the launch traced here: 249 us
  waiting for transfers between devices  166 us (66%)
  starting transfers between devices  29.9 us (12%)
  Pallas kernels  21.3 us (9%)
  between operations  13.5 us (5%)
  local copies, waits for them, and re-layouts  12 us (5%)
  other arithmetic  6.24 us (2%)
    all_to_all x1, waiting for transfers between devices, on_device(): recv = lax.all_to_all(send, 'seq', split_axis=0, concat_axis=0, tiled=True)  86.9 us
    reduce_scatter x1, waiting for transfers between devices, on_device(): return lax.psum_scatter(mixed, 'head', scatter_dimension=0, tiled=True)  53.6 us
    all_to_all x1, waiting for transfers between devices, on_device(): back = lax.all_to_all(back, 'seq', split_axis=0, concat_axis=0, tiled=True)  26 us
    all_to_all x1, starting transfers between devices, on_device(): recv = lax.all_to_all(send, 'seq', split_axis=0, concat_axis=0, tiled=True)  19.2 us
    all_to_all x1, starting transfers between devices, on_device(): back = lax.all_to_all(back, 'seq', split_axis=0, concat_axis=0, tiled=True)  10.7 us
    pallas_call x1, Pallas kernels, cluster_attention(): pl.pallas_call(functools.partial(attention_kernel, scale=scale), grid=(pe...  8.53 us
    pallas_call x1, Pallas kernels, project(): pl.pallas_call(project_kernel, grid=(steps,), in_specs=[pl.BlockSpec((tok...  6.78 us
    pallas_call x1, Pallas kernels, place(): pl.pallas_call(functools.partial(place_kernel, group=group), grid=(owners...  6.04 us
  transfers between devices with their start and end apart: 3, of which 3 were waited for; matrix products, arithmetic and copies ran while one was open for 2% of the time, Pallas kernels for 0%

profile of v11, /device:TPU:6, one launch (start us, length us, event | category | flops | bytes accessed | tf_op | source)
XLA Modules:
  0.0 249.4 jit_solution(1962189769969815599)
XLA Ops:
  6.5 0.0 copy-start.2
  6.5 0.0 copy-start.3
  6.5 0.1 iota_compare_fusion.1
  6.6 0.9 copy.42
  7.5 0.1 copy.43
  7.6 0.2 convert_reduce_fusion.1
  7.9 0.7 convert_reduce_fusion
  8.6 1.3 bitcast_add_fusion.slot_ref
  9.8 1.7 copy.62
  11.5 0.7 pad_maximum_fusion
  12.2 0.6 reshape.89.cent_ref
  12.8 0.1 convert_element_type.38
  13.0 0.1 copy.47
  13.1 0.1 pad.4
  13.2 1.0 copy.55.count_ref
  14.1 0.0 copy-done.2
  14.1 0.0 copy-done.3
  14.1 0.9 copy_bitcast_fusion
  15.0 6.0 %shard_map.73 = bf16[64,112,256]{2,1,0:T(8,128)(2,1)} custom-call(s32[2,1,512]{2,1,0:T(1,128)} %bitcast_add_fusion.slot_ref, bf16[512,256]{1,0:T(8,128)(2,1)} %bitcast.37, bf16[512,256]{1,0:T(8,128)(2,1)} %get-tuple-element.6.k_ref, bf16[512,256]{1,0:T(8,128)(2,1)} %get-tuple-element.5.v_ref, bf16[8,256]{1,0:T(8,128)(2,1)} %reshape.89.cent_ref, ...), custom_call_target="tpu_custom_call" | custom-call | tf_op jit(solution)/shard_map/pallas_call | solution.py:87
  21.0 19.2 %all-to-all-start = ((bf16[64,112,256]{2,1,0:T(8,128)(2,1)}), bf16[64,112,256]{2,1,0:T(8,128)(2,1)}, u32[]{:S(2)}, u32[]{:S(2)}) async-start(bf16[64,112,256]{2,1,0:T(8,128)(2,1)} %shard_map.73), calls=%async_computation | async-start | bytes 7340032 | tf_op jit(solution)/shard_map/all_to_all | solution.py:212
  40.2 0.1 lt.48
  40.3 86.9 %all-to-all-done.q_ref.k_ref.v_ref = bf16[64,112,256]{2,1,0:T(8,128)(2,1)} async-done(((bf16[64,112,256]{2,1,0:T(8,128)(2,1)}), bf16[64,112,256]{2,1,0:T(8,128)(2,1)}, u32[]{:S(2)}, u32[]{:S(2)}) %all-to-all-start) | async-done | bytes 3670048 | tf_op jit(solution)/shard_map/all_to_all | solution.py:212
  127.2 1.0 slice.8
  128.2 0.1 reshape.91
  128.2 0.8 copy.49
  129.0 0.9 slice_convert_fusion
  130.0 0.1 copy.50
  130.0 0.1 lt.50
  130.2 0.2 lt.53
  130.4 0.6 compare_convert_fusion.valid_ref
  131.0 8.5 %shard_map.74 = bf16[64,32,256]{2,1,0:T(8,128)(2,1)} custom-call(bf16[64,112,256]{2,1,0:T(8,128)(2,1)} %all-to-all-done.q_ref.k_ref.v_ref, bf16[64,112,256]{2,1,0:T(8,128)(2,1)} %all-to-all-done.q_ref.k_ref.v_ref, bf16[64,112,256]{2,1,0:T(8,128)(2,1)} %all-to-all-done.q_ref.k_ref.v_ref, bf16[2,2,256,128]{3,2,1,0:T(8,128)(2,1)} %bitcast.33, ...), custom_call_target="tpu_custom_call" | custom-call | tf_op jit(solution)/shard_map/pallas_call | solution.py:156
  139.5 0.0 copy-start.1
  139.5 10.7 %all-to-all-start.1 = ((bf16[64,32,256]{2,1,0:T(8,128)(2,1)}), bf16[64,32,256]{2,1,0:T(8,128)(2,1)S(1)}, u32[]{:S(2)}, u32[]{:S(2)}) async-start(bf16[64,32,256]{2,1,0:T(8,128)(2,1)} %shard_map.74), calls=%async_computation.1 | async-start | bytes 2097152 | tf_op jit(solution)/shard_map/all_to_all | solution.py:226
  150.2 0.0 reduce-scatter.2.cloned.1.call-start
  150.2 0.9 copy.45
  151.1 0.0 copy-done.1
  151.1 2.4 copy.54
  153.5 1.7 add_bitcast_fusion.slot_ref
  155.2 26.0 %all-to-all-done.1 = bf16[64,32,256]{2,1,0:T(8,128)(2,1)S(1)} async-done(((bf16[64,32,256]{2,1,0:T(8,128)(2,1)}), bf16[64,32,256]{2,1,0:T(8,128)(2,1)S(1)}, u32[]{:S(2)}, u32[]{:S(2)}) %all-to-all-start.1) | async-done | bytes 1048608 | tf_op jit(solution)/shard_map/all_to_all | solution.py:226
  181.2 0.0 copy-start
  181.2 1.0 copy-done
  182.2 6.8 %shard_map.75 = bf16[4096,512]{1,0:T(8,128)(2,1)} custom-call(s32[512,2]{1,0:T(8,128)} %add_bitcast_fusion.slot_ref, bf16[2048,256]{1,0:T(8,128)(2,1)} %bitcast.32, bf16[4096,256]{1,0:T(8,128)(2,1)} %bitcast.31), custom_call_target="tpu_custom_call" | custom-call | tf_op jit(solution)/shard_map/pallas_call | solution.py:40
  189.0 0.0 reduce-scatter.2.cloned.1.call-update
  189.0 53.6 %reduce-scatter.2.cloned.1.call-done = bf16[512,512]{1,0:T(8,128)(2,1)} async-done(((bf16[4096,512]{1,0:T(8,128)(2,1)}), bf16[512,512]{1,0:T(8,128)(2,1)}) %reduce-scatter.2.cloned.1.call-update) | async-done | bytes 524304 | tf_op jit(solution)/shard_map/reduce_scatter | solution.py:229
  (3 shorter events, 0.0 us)
Async XLA Ops:
  6.5 7.6 %copy-start.2 = (bf16[512,2,128]{2,1,0:T(2,128)(2,1)S(1)}, bf16[512,2,128]{2,1,0:T(2,128)(2,1)}, u32[]{:S(2)}) copy-start(bf16[512,2,128]{2,1,0:T(2,128)(2,1)} %param.9) | copy-start | bytes 786436
  6.5 7.6 %copy-start.3 = (bf16[512,2,128]{2,1,0:T(2,128)(2,1)S(1)}, bf16[512,2,128]{2,1,0:T(2,128)(2,1)}, u32[]{:S(2)}) copy-start(bf16[512,2,128]{2,1,0:T(2,128)(2,1)} %param.8) | copy-start | bytes 786436
  21.0 106.2 %all-to-all-start = ((bf16[64,112,256]{2,1,0:T(8,128)(2,1)}), bf16[64,112,256]{2,1,0:T(8,128)(2,1)}, u32[]{:S(2)}, u32[]{:S(2)}) async-start(bf16[64,112,256]{2,1,0:T(8,128)(2,1)} %shard_map.73), calls=%async_computation | async-start | bytes 7340032 | tf_op jit(solution)/shard_map/all_to_all | solution.py:212
  139.5 11.6 %copy-start.1 = (bf16[256,4096]{1,0:T(8,128)(2,1)S(1)}, bf16[256,4096]{1,0:T(8,128)(2,1)}, u32[]{:S(2)}) copy-start(bf16[256,4096]{1,0:T(8,128)(2,1)} %param.13) | copy-start | bytes 6291460
  139.5 41.7 %all-to-all-start.1 = ((bf16[64,32,256]{2,1,0:T(8,128)(2,1)}), bf16[64,32,256]{2,1,0:T(8,128)(2,1)S(1)}, u32[]{:S(2)}, u32[]{:S(2)}) async-start(bf16[64,32,256]{2,1,0:T(8,128)(2,1)} %shard_map.74), calls=%async_computation.1 | async-start | bytes 2097152 | tf_op jit(solution)/shard_map/all_to_all | solution.py:226
  150.2 92.4 %reduce-scatter.2.cloned.1.call-start = ((), (), s32[]{:S(2)}) async-start(), calls=%async_computation.3 | async-start | bytes 4718592 | tf_op jit(solution)/shard_map/reduce_scatter | solution.py:229
  181.2 1.0 copy-start
Sparse Core Ops, SparseCore 0:
  189.1 53.3 reduce-scatter.1
